TPU v7x, 512 devices: a whole 4x8x8 slice. The times are simulated.
512 devices in a mesh: panel: 2 (over y_hi), gx: 16 (over x, y_lo), gy: 16 (over z, core).
Axes of the slice: x: 4, y: 8 (y_hi: 2, y_lo: 4; y = y_hi * 4 + y_lo), z: 8, core: 2. Of those that a mesh axis runs over, the one named last changes fastest.
Arguments:
- state: float32 [2, 3, 1, 2048, 2048], P('panel', None, None, 'gx', 'gy'), may hold values from -6 to 6
- coriolis: float32 [2, 2048, 2048], P('panel', 'gx', 'gy'), may hold values from -1.5 to 1.5
- edge_rotation: int32 [2, 4], P('panel'), may hold values from 0 to 3
- nest_block_state: float32 [2, 16, 256, 3, 1, 576], P('panel', 'gx', 'gy'), may hold values from -6 to 6
- parent_tile_index: int32 [2, 16, 256, 1], P('panel', 'gx', 'gy'), may hold values from 0 to 15; in each aligned block of 16 rows (0 to 15, 16 to 31, ..., all dimensions but the last counted through in order) at most 2 rows name the same one
- parent_spot_index: int32 [2, 16, 256], P('panel', 'gx', 'gy'), may hold values from 0 to 255
Outputs:
- parent_out: float32 [2, 3, 1, 2048, 2048], P('panel', None, None, 'gx', 'gy')
- nest_out: float32 [2, 16, 256, 3, 1, 576], P('panel', 'gx', 'gy')
Inputs may be any that keep to these rules, and one draw needn't show every extreme that they name: `parent_tile_index`: among the 16 nest blocks that one device owns (aligned blocks of 16 along the line), no tile of the line is named more than 2 times, and in every draw some device names one tile exactly 2 times.
All inputs are finite; a program needn't handle non-finite values.
Results may differ from a plain program's by a relative error of at most 0.0003.
Values sent between devices are 32-bit elements; how exact they have to be, the bound alone decides.
No kernel may reach another device: no remote copies, remote signals or barrier semaphores. Data moves between devices by JAX's collectives and lax.ppermute only.
A program may use at most 64 MiB of HBM per device.

v0:
```python
import jax
import jax.numpy as jnp
from jax import lax
from jax.sharding import PartitionSpec as P

NSUB = 2
PATCH = 8
RATIO = 3
FINE = 24


DT_STEP = 0.25
GRAVITY = 1.0
DAMPING = 0.5
DEPTH = 1.0
KAPPA = 0.2
ALPHA = 0.5
BETA = 0.5


def from_partner(block, axis, stride):
    count = lax.axis_size(axis)
    route = []
    for low in range(count):
        high = low | 1 << stride
        if high != low and high < count:
            route += [(low, high), (high, low)]
    return lax.ppermute(block, axis, route)


def extended(block, sides, width):
    for axis, dim in sides:
        count = lax.axis_size(axis)
        forward = [(i, i + 1) for i in range(count - 1)]
        backward = [(target, source) for source, target in forward]
        low = lax.ppermute(
            lax.slice_in_dim(block, block.shape[dim] - width, None, axis=dim), axis, forward
        )
        high = lax.ppermute(lax.slice_in_dim(block, 0, width, axis=dim), axis, backward)
        block = jnp.concatenate([low, block, high], axis=dim)
    return block


def rotated(code, east_part, north_part):
    along = (code == 0).astype(east_part.dtype) - (code == 2).astype(east_part.dtype)
    across = (code == 3).astype(east_part.dtype) - (code == 1).astype(east_part.dtype)
    return (along * east_part + across * north_part, along * north_part - across * east_part)


def centre(field):
    return field[..., 1:-1, 1:-1]


def along_x(field):
    return 0.5 * (field[..., 2:, 1:-1] - field[..., :-2, 1:-1])


def along_y(field):
    return 0.5 * (field[..., 1:-1, 2:] - field[..., 1:-1, :-2])


def laplacian(field):
    return (
        field[..., 2:, 1:-1]
        + field[..., :-2, 1:-1]
        + field[..., 1:-1, 2:]
        + field[..., 1:-1, :-2]
        - 4.0 * centre(field)
    )


def advance(height, east, north, coriolis):
    absolute = coriolis + along_x(north) - along_y(east)
    depth = DEPTH + height
    divergence = along_x(depth * east) + along_y(depth * north)
    new_height = centre(height) - DT_STEP * divergence
    new_east = centre(east) + DT_STEP * (
        absolute * centre(north) - GRAVITY * along_x(height) + DAMPING * laplacian(east)
    )
    new_north = centre(north) + DT_STEP * (
        -absolute * centre(east) - GRAVITY * along_y(height) + DAMPING * laplacian(north)
    )
    return (new_height, new_east, new_north)


def smooth_blocks(blocks):
    count = blocks.shape[0]
    square = blocks.reshape(count, 3, blocks.shape[2], FINE, FINE)
    padded = jnp.pad(square, ((0, 0), (0, 0), (0, 0), (1, 1), (1, 1)), mode="edge")
    return (square + KAPPA * laplacian(padded)).reshape(blocks.shape)


def blend_nest(blocks, parent):
    count = blocks.shape[0]
    coarse = parent.reshape(count, 3, blocks.shape[2], PATCH, PATCH)
    upsampled = jnp.repeat(jnp.repeat(coarse, RATIO, axis=3), RATIO, axis=4).reshape(blocks.shape)
    smoothed = smooth_blocks(blocks)
    return smoothed + ALPHA * (upsampled - smoothed)


def block_means(blocks):
    count = blocks.shape[0]
    grouped = blocks.reshape(count, 3, blocks.shape[2], PATCH, RATIO, PATCH, RATIO)
    return jnp.mean(grouped, axis=(4, 6)).reshape(count, -1)


def tile_table(tile):
    level_stack = tile.shape[1]
    quarter = tile.shape[-1] // PATCH
    shaped = tile.reshape(3, level_stack, quarter, PATCH, quarter, PATCH)
    return jnp.transpose(shaped, (2, 4, 0, 1, 3, 5)).reshape(
        quarter * quarter, 3 * level_stack * PATCH * PATCH
    )


def table_tile(table, level_stack, quarter):
    shaped = table.reshape(quarter, quarter, 3, level_stack, PATCH, PATCH)
    return jnp.transpose(shaped, (2, 3, 0, 4, 1, 5)).reshape(
        3, level_stack, quarter * PATCH, quarter * PATCH
    )


def pick_blocks(tile, spots):
    return jnp.take(tile_table(tile), spots, axis=0)


def place_side(padded, side, strip, flag, depth):
    zero = 0
    if side == 0:
        old = padded[:, :, depth, 1:-1]
        new = jnp.where(flag, strip, old)[:, :, None, :]
        return lax.dynamic_update_slice(padded, new, (zero, zero, depth, 1))
    if side == 1:
        row = padded.shape[2] - 1 - depth
        old = padded[:, :, row, 1:-1]
        new = jnp.where(flag, strip, old)[:, :, None, :]
        return lax.dynamic_update_slice(padded, new, (zero, zero, row, 1))
    if side == 2:
        old = padded[:, :, 1:-1, depth]
        new = jnp.where(flag, strip, old)[:, :, :, None]
        return lax.dynamic_update_slice(padded, new, (zero, zero, 1, depth))
    column = padded.shape[3] - 1 - depth
    old = padded[:, :, 1:-1, column]
    new = jnp.where(flag, strip, old)[:, :, :, None]
    return lax.dynamic_update_slice(padded, new, (zero, zero, 1, column))


def partner_edges(strips):
    return from_partner(strips, "panel", 0)


def fill_edges(padded, partner, codes, flags, depth):
    for side in range(4):
        strip = partner[side]
        east_rot, north_rot = rotated(codes[side], strip[1], strip[2])
        strip = jnp.stack([strip[0], east_rot, north_rot], axis=0)
        padded = place_side(padded, side, strip, flags[side], depth)
    return padded


def body(state, coriolis, edge_rotation, nest_block_state, parent_tile_index, parent_spot_index):
    devices_y = lax.axis_size("gy")
    slots = nest_block_state.shape[2]
    capacity = max(2, 2 * slots // devices_y)
    width = devices_y * capacity
    my_row = lax.axis_index("gy")
    my_column = lax.axis_index("gx")
    last_x = lax.axis_size("gx") - 1
    last_y = devices_y - 1
    source_tiles, block_spots = (
        lax.all_gather(parent_tile_index, "gy", axis=2, tiled=True),
        lax.all_gather(parent_spot_index, "gy", axis=2, tiled=True),
    )
    source_tiles = source_tiles.reshape(-1)
    block_spots = block_spots.reshape(-1)
    order = jnp.arange(source_tiles.shape[0], dtype=jnp.int32)
    owner = order // slots
    earlier = (
        (source_tiles[:, None] == source_tiles[None, :])
        & (owner[:, None] == owner[None, :])
        & (order[None, :] < order[:, None])
    )
    rank = jnp.sum(earlier.astype(jnp.int32), axis=1)
    target = owner * capacity + rank
    hits = (jnp.arange(width, dtype=jnp.int32)[:, None] == target[None, :]) & (
        source_tiles[None, :] == my_row
    )
    valid = jnp.any(hits, axis=1)
    place_row = jnp.sum(jnp.where(hits, block_spots[None, :], 0), axis=1)
    tile = state[0]
    level_stack = tile.shape[1]
    side_cells = tile.shape[-1]
    quarter = side_cells // PATCH
    outgoing = jnp.where(valid[:, None], pick_blocks(tile, place_row), 0.0)
    incoming = lax.all_to_all(
        outgoing.reshape(devices_y, capacity, -1), "gy", split_axis=0, concat_axis=0, tiled=True
    )
    mine = parent_tile_index.reshape(-1)
    local = jnp.arange(slots, dtype=jnp.int32)
    own_rank = jnp.sum(
        ((mine[:, None] == mine[None, :]) & (local[None, :] < local[:, None])).astype(jnp.int32),
        axis=1,
    )
    own_index = mine * capacity + own_rank
    slot_table = (jnp.arange(width, dtype=jnp.int32)[:, None] == own_index[None, :]).astype(
        jnp.float32
    )
    codes = edge_rotation[0]
    flags = [my_column == 0, my_column == last_x, my_row == 0, my_row == last_y]
    field = tile
    cell_coriolis = coriolis[0][None]
    for sub in range(NSUB):
        padded = extended(field, (("gx", 2), ("gy", 3)), 1)
        strips = jnp.stack(
            [field[:, :, 0, :], field[:, :, -1, :], field[:, :, :, 0], field[:, :, :, -1]], axis=0
        )
        partner = partner_edges(strips)
        padded = fill_edges(padded, partner, codes, flags, 0)
        height, east, north = advance(padded[0], padded[1], padded[2], cell_coriolis)
        field = jnp.stack([height, east, north], axis=0)
    parent = incoming.reshape(width, -1)[own_index]
    blocks_out = blend_nest(nest_block_state[0, 0], parent)
    payload = blocks_out.reshape(slots, -1)
    backward = jnp.dot(
        slot_table, payload, precision=lax.Precision.HIGHEST, preferred_element_type=jnp.float32
    )
    returned = lax.all_to_all(
        backward.reshape(devices_y, capacity, -1), "gy", split_axis=0, concat_axis=0, tiled=True
    )
    means = block_means(returned.reshape(width, 3, level_stack, -1))
    after_table = tile_table(field)
    after_blocks = jnp.take(after_table, place_row, axis=0)
    change = jnp.where(valid[:, None], BETA * (means - after_blocks), 0.0)
    spot_select = (
        (jnp.arange(quarter * quarter, dtype=jnp.int32)[:, None] == place_row[None, :])
        & valid[None, :]
    ).astype(jnp.float32)
    added = jnp.dot(
        spot_select, change, precision=lax.Precision.HIGHEST, preferred_element_type=jnp.float32
    )
    final_result = table_tile(after_table + added, level_stack, quarter)
    return (final_result[None], blocks_out[None, None])


def solution(mesh):
    in_specs = (
        P("panel", None, None, "gx", "gy"),
        P("panel", "gx", "gy"),
        P("panel", None),
        P("panel", "gx", "gy", None, None, None),
        P("panel", "gx", "gy", None),
        P("panel", "gx", "gy"),
    )
    out_specs = (P("panel", None, None, "gx", "gy"), P("panel", "gx", "gy", None, None, None))
    return jax.shard_map(body, mesh=mesh, in_specs=in_specs, out_specs=out_specs, check_vma=False)
```

profile of v0, /device:TPU:7, one launch (start us, length us, event | category | flops | bytes accessed | tf_op | source)
XLA Modules:
  0.0 190.4 jit_solution(7452512858063121386)
XLA Ops:
  0.6 1.1 copy.809
  1.7 0.8 slice_reduce_fusion.2
  2.5 0.6 pad_maximum_fusion.12
  3.1 7.4 %collective-permute-start.4 = (f32[4,3,1,128]{3,0,2,1:T(4,128)}, f32[4,3,1,128]{3,0,2,1:T(4,128)S(1)}, u32[]{:S(2)}, u32[]{:S(2)}) collective-permute-start(f32[4,3,1,128]{3,0,2,1:T(4,128)} %pad_maximum_fusion.12), channel_id=1, source_target_pairs={{0,256},{256,0},{1,257},{257,1},{2,258},{258,2},{3,259},{259,3},{4... | collective-permute-start | bytes 18440 | tf_op jit(solution)/shard_map/ppermute | solution.py:28
  10.6 2.8 %collective-permute-start.1 = (f32[3,1,1,128]{2,3,1,0:T(8,128)}, f32[3,1,1,128]{2,3,1,0:T(8,128)}, u32[]{:S(2)}, u32[]{:S(2)}) collective-permute-start(f32[3,1,1,128]{2,3,1,0:T(8,128)} %get-tuple-element.55), channel_id=1, source_target_pairs={{16,0},{32,16},{48,32},{64,48},{80,64},{96,80},{112,96},{128,112},... | collective-permute-start | bytes 4616 | tf_op jit(solution)/shard_map/ppermute | solution.py:39
  13.4 2.5 %collective-permute-start = (f32[3,1,1,128]{2,3,1,0:T(8,128)}, f32[3,1,1,128]{2,3,1,0:T(8,128)S(1)}, u32[]{:S(2)}, u32[]{:S(2)}) collective-permute-start(f32[3,1,1,128]{2,3,1,0:T(8,128)} %get-tuple-element.56), channel_id=1, source_target_pairs={{0,16},{16,32},{32,48},{48,64},{64,80},{80,96},{96,112},{112,128},... | collective-permute-start | bytes 4616 | tf_op jit(solution)/shard_map/ppermute | solution.py:36
  15.9 0.9 convert_reduce_fusion.1
  16.8 1.3 dynamic-slice
  18.8 0.8 bitcast_dynamic-update-slice_fusion
  19.5 1.2 multiply_add_fusion.7
  20.7 17.9 %all-reduce.2 = (s32[256]{0:T(256)S(1)}, s32[256]{0:T(256)S(1)}) all-reduce(s32[256]{0:T(256)S(1)} %bitcast_dynamic-update-slice_fusion, s32[256]{0:T(256)S(1)} %get-tuple-element.88), channel_id=1, replica_groups=mesh['panel'=2,'gx'=16,'gy'=16] {'gy'}, use_global_device_ids=true, to_apply=%add.1 | all-reduce | flops 512 | bytes 4096
  39.6 2.6 %reshape_squeeze.7 = f32[3,1,16,8,16,8]{5,4,3,2,0,1:T(8,128)S(1)} reshape(f32[1,3,1,128,128]{4,3,2,1,0:T(8,128)} %param.8) | data formatting | bytes 393216 | tf_op jit(solution)/shard_map/reshape;squeeze | solution.py:110
  42.3 0.6 pad_clamp_fusion.1
  42.9 2.1 %copy.875 = f32[16,16,3,1,8,8]{1,0,5,4,2,3:T(8,128)} copy(f32[16,16,3,1,8,8]{5,1,4,0,2,3:T(8,128)S(1)} %bitcast.174) | data formatting | bytes 393216 | tf_op jit(solution)/shard_map/transpose | solution.py:111
  45.0 2.0 %reshape.994 = f32[256,192]{0,1:T(8,128)S(1)} reshape(f32[16,16,3,1,8,8]{1,0,5,4,2,3:T(8,128)} %copy.875) | data formatting | bytes 393216 | tf_op jit(solution)/shard_map/reshape | solution.py:111
  47.1 0.9 gather_fusion.1
  47.9 0.7 select_select_fusion
  48.7 0.6 reshape.995
  49.3 7.0 %all-to-all-start = ((f32[16,2,192]{2,1,0:T(2,128)}), f32[16,2,192]{2,1,0:T(2,128)}, u32[]{:S(2)}, u32[]{:S(2)}) async-start(f32[16,2,192]{2,1,0:T(2,128)} %reshape.995), calls=%async_computation | async-start | bytes 65536 | tf_op jit(solution)/shard_map/all_to_all | solution.py:195
  56.3 0.7 fusion.53
  57.5 0.6 fusion.61
  58.1 0.9 copy.874
  69.6 0.7 copy.868
  70.4 0.8 pad_maximum_fusion.21
  71.3 3.5 %collective-permute-start.2 = (f32[3,1,130,1]{2,3,1,0:T(1,128)S(1)}, f32[3,1,130,1]{2,3,1,0:T(1,128)S(1)}, u32[]{:S(2)}, u32[]{:S(2)}) collective-permute-start(f32[3,1,130,1]{2,3,1,0:T(1,128)S(1)} %get-tuple-element.41), channel_id=1, source_target_pairs={{0,1},{1,2},{2,3},{3,4},{4,5},{5,6},{6,7},{7,8},{8,9},{9,10},{10,1... | collective-permute-start | bytes 4688 | tf_op jit(solution)/shard_map/ppermute | solution.py:36
  74.8 1.9 %collective-permute-start.3 = (f32[3,1,130,1]{2,3,1,0:T(1,128)S(1)}, f32[3,1,130,1]{2,3,1,0:T(1,128)S(1)}, u32[]{:S(2)}, u32[]{:S(2)}) collective-permute-start(f32[3,1,130,1]{2,3,1,0:T(1,128)S(1)} %get-tuple-element.42), channel_id=1, source_target_pairs={{1,0},{2,1},{3,2},{4,3},{5,4},{6,5},{7,6},{8,7},{9,8},{10,9},{11,1... | collective-permute-start | bytes 4688 | tf_op jit(solution)/shard_map/ppermute | solution.py:39
  76.8 2.9 %collective-permute-done.3 = f32[3,1,130,1]{2,3,1,0:T(1,128)S(1)} collective-permute-done((f32[3,1,130,1]{2,3,1,0:T(1,128)S(1)}, f32[3,1,130,1]{2,3,1,0:T(1,128)S(1)}, u32[]{:S(2)}, u32[]{:S(2)}) %collective-permute-start.3) | collective-permute-done | bytes 1592 | tf_op jit(solution)/shard_map/ppermute | solution.py:39
  79.7 1.2 pad_maximum_fusion.9
  81.3 0.7 dynamic_update_slice.24
  82.4 1.3 dynamic_update_slice.25
  84.5 0.6 dynamic_update_slice.27
  86.7 5.5 %collective-permute-start.6 = (f32[3,1,1,128]{2,3,1,0:T(8,128)S(1)}, f32[3,1,1,128]{2,3,1,0:T(8,128)S(1)}, u32[]{:S(2)}, u32[]{:S(2)}) collective-permute-start(f32[3,1,1,128]{2,3,1,0:T(8,128)S(1)} %get-tuple-element.51), channel_id=1, source_target_pairs={{16,0},{32,16},{48,32},{64,48},{80,64},{96,80},{112,96},{128,112},... | collective-permute-start | bytes 4616 | tf_op jit(solution)/shard_map/ppermute | solution.py:39
  92.2 1.9 %collective-permute-start.5 = (f32[3,1,1,128]{2,3,1,0:T(8,128)S(1)}, f32[3,1,1,128]{2,3,1,0:T(8,128)S(1)}, u32[]{:S(2)}, u32[]{:S(2)}) collective-permute-start(f32[3,1,1,128]{2,3,1,0:T(8,128)S(1)} %get-tuple-element.52), channel_id=1, source_target_pairs={{0,16},{16,32},{32,48},{48,64},{64,80},{80,96},{96,112},{112,128},... | collective-permute-start | bytes 4616 | tf_op jit(solution)/shard_map/ppermute | solution.py:36
  94.1 2.8 %collective-permute-done.6 = f32[3,1,1,128]{2,3,1,0:T(8,128)S(1)} collective-permute-done((f32[3,1,1,128]{2,3,1,0:T(8,128)S(1)}, f32[3,1,1,128]{2,3,1,0:T(8,128)S(1)}, u32[]{:S(2)}, u32[]{:S(2)}) %collective-permute-start.6) | collective-permute-done | bytes 1568 | tf_op jit(solution)/shard_map/ppermute | solution.py:39
  96.9 5.4 %collective-permute-done.5 = f32[3,1,1,128]{2,3,1,0:T(8,128)S(1)} collective-permute-done((f32[3,1,1,128]{2,3,1,0:T(8,128)S(1)}, f32[3,1,1,128]{2,3,1,0:T(8,128)S(1)}, u32[]{:S(2)}, u32[]{:S(2)}) %collective-permute-start.5) | collective-permute-done | bytes 1568 | tf_op jit(solution)/shard_map/ppermute | solution.py:36
  102.4 4.3 %collective-permute-start.7 = (f32[3,1,130,1]{2,3,1,0:T(1,128)S(1)}, f32[3,1,130,1]{2,3,1,0:T(1,128)S(1)}, u32[]{:S(2)}, u32[]{:S(2)}) collective-permute-start(f32[3,1,130,1]{2,3,1,0:T(1,128)S(1)} %get-tuple-element.39), channel_id=1, source_target_pairs={{0,1},{1,2},{2,3},{3,4},{4,5},{5,6},{6,7},{7,8},{8,9},{9,10},{10,1... | collective-permute-start | bytes 4688 | tf_op jit(solution)/shard_map/ppermute | solution.py:36
  106.7 1.9 %collective-permute-start.8 = (f32[3,1,130,1]{2,3,1,0:T(1,128)S(1)}, f32[3,1,130,1]{2,3,1,0:T(1,128)S(1)}, u32[]{:S(2)}, u32[]{:S(2)}) collective-permute-start(f32[3,1,130,1]{2,3,1,0:T(1,128)S(1)} %get-tuple-element.40), channel_id=1, source_target_pairs={{1,0},{2,1},{3,2},{4,3},{5,4},{6,5},{7,6},{8,7},{9,8},{10,9},{11,1... | collective-permute-start | bytes 4688 | tf_op jit(solution)/shard_map/ppermute | solution.py:39
  108.7 4.6 %collective-permute-start.9 = (f32[4,3,1,128]{3,0,2,1:T(4,128)S(1)}, f32[4,3,1,128]{3,0,2,1:T(4,128)S(1)}, u32[]{:S(2)}, u32[]{:S(2)}) collective-permute-start(f32[4,3,1,128]{3,0,2,1:T(4,128)S(1)} %pad_maximum_fusion.13), channel_id=1, source_target_pairs={{0,256},{256,0},{1,257},{257,1},{2,258},{258,2},{3,259},{259,3},{4... | collective-permute-start | bytes 18440 | tf_op jit(solution)/shard_map/ppermute | solution.py:28
  113.6 3.4 %collective-permute-done.9 = f32[4,3,1,128]{3,0,2,1:T(4,128)S(1)} collective-permute-done((f32[4,3,1,128]{3,0,2,1:T(4,128)S(1)}, f32[4,3,1,128]{3,0,2,1:T(4,128)S(1)}, u32[]{:S(2)}, u32[]{:S(2)}) %collective-permute-start.9) | collective-permute-done | bytes 6176 | tf_op jit(solution)/shard_map/ppermute | solution.py:28
  117.3 0.7 dynamic_update_slice.28
  118.7 10.8 %dynamic_update_slice.29 = f32[3,1,130,130]{2,0,3,1:T(4,128)S(1)} dynamic-update-slice(f32[3,1,130,130]{2,0,3,1:T(4,128)S(1)} %copy.859, f32[3,1,1,128]{2,0,3,1:T(4,128)S(1)} %copy.860, s32[]{:T(128)} %constant.75.clone.1, s32[]{:T(128)} %constant.75.clone.1, s32[]{:T(128)} %constant.82.clone.1, s32[]{:T(128)} %constant.80.clone.1) | dynamic-update-slice | bytes 3076 | tf_op jit(solution)/shard_map/dynamic_update_slice | solution.py:137
  130.6 1.8 slice_subtract_fusion.4
  132.4 1.0 multiply_add_fusion.3
  133.8 1.6 stack.98
  135.3 1.6 stack.96
  136.9 1.6 stack.97
  138.5 0.8 reshape.996
  140.1 0.9 broadcast_in_dim.83
  141.0 2.2 %copy.879 = f32[16,3,1,24,24]{4,3,0,1,2:T(8,128)} copy(f32[16,3,1,24,24]{3,0,4,1,2:T(8,128)} %bitcast.182) | data formatting | bytes 221184 | tf_op jit(solution)/shard_map/broadcast_in_dim | solution.py:96
  143.1 2.7 %multiply_add_fusion = (f32[16,3,1,24,24]{4,3,0,1,2:T(8,128)S(1)}, f32[16,3,1,24,24]{4,3,0,1,2:T(8,128)}) fusion(f32[16,3,1,24,24]{4,3,0,1,2:T(8,128)} %copy.879, f32[16,3,1,24,24]{4,3,0,1,2:T(8,128)S(1)} %reshape_squeeze.6, f32[16,3,1,1,24]{4,3,0,1,2:T(1,128)S(1)} %copy-done.5, f32[16,3,1,1,24]{4,3,0,1,2:T(1,128)S(1)} %copy-done.3, ...), kind=kLoop, calls=%fused_computation.20 | loop fusion | flops 497664 | bytes 461568 | tf_op jit(solution)/shard_map/add | solution.py:98
  146.4 0.9 copy.881
  147.3 9.4 %all-to-all-start.1 = ((f32[16,2,1728]{2,1,0:T(2,128)}), f32[16,2,1728]{2,1,0:T(2,128)}, u32[]{:S(2)}, u32[]{:S(2)}) async-start(f32[16,2,1728]{2,1,0:T(2,128)} %copy.881), calls=%async_computation.1 | async-start | bytes 458752 | tf_op jit(solution)/shard_map/all_to_all | solution.py:227
  156.7 2.1 %maximum_bitcast_fusion = f32[16,16,3,1,8,8]{5,1,4,0,3,2:T(8,128)S(1)} fusion(f32[1,1,16,8,16,8]{5,4,3,2,1,0:T(8,128)} %stack.98, f32[1,1,16,8,16,8]{5,4,3,2,1,0:T(8,128)} %stack.97, f32[1,1,16,8,16,8]{5,4,3,2,1,0:T(8,128)} %stack.96), kind=kLoop, calls=%fused_computation.3 | loop fusion | flops 98304 | bytes 393216 | tf_op jit(solution)/shard_map/transpose | solution.py:111
  158.8 2.1 %copy.873 = f32[16,16,3,1,8,8]{1,0,5,4,2,3:T(8,128)} copy(f32[16,16,3,1,8,8]{5,1,4,0,3,2:T(8,128)S(1)} %maximum_bitcast_fusion) | data formatting | bytes 393216 | tf_op jit(solution)/shard_map/transpose | solution.py:111
  160.9 2.0 %reshape.992 = f32[256,192]{0,1:T(8,128)S(1)} reshape(f32[16,16,3,1,8,8]{1,0,5,4,2,3:T(8,128)} %copy.873) | data formatting | bytes 393216 | tf_op jit(solution)/shard_map/reshape | solution.py:111
  163.0 0.7 gather_fusion.2
  163.7 1.3 reshape.999
  166.1 0.8 copy.889
  166.9 0.9 all-to-all-done.1
  167.7 11.4 %reshape_reshape.4 = f32[32,3,8,3,8,3]{5,4,3,2,1,0:T(8,128)} reshape(f32[16,2,1728]{2,1,0:T(2,128)} %all-to-all-done.1) | data formatting | bytes 442368 | tf_op jit(solution)/shard_map/reshape;reshape | solution.py:103
  179.1 4.6 %reduce_sum.42 = f32[32,3,8,8]{3,2,1,0:T(8,128)S(1)} reduce(f32[32,3,8,3,8,3]{5,4,3,2,1,0:T(8,128)} %reshape_reshape.4, f32[]{:T(128)} %constant.93.clone.1), dimensions={3,5}, to_apply=%region_4.6 | reduce | flops 49152 | bytes 245764 | tf_op jit(solution)/shard_map/reduce_sum | solution.py:104
  184.4 1.7 reshape.998
  186.0 2.2 %copy.885 = f32[16,16,3,1,8,8]{5,1,4,0,2,3:T(8,128)S(1)} copy(f32[16,16,3,1,8,8]{1,0,5,4,2,3:T(8,128)} %reshape.998) | data formatting | bytes 393216 | tf_op jit(solution)/shard_map/reshape | solution.py:117
  188.2 2.1 %broadcast_in_dim_reshape.2 = f32[1,3,1,128,128]{4,3,1,2,0:T(8,128)} reshape(f32[3,1,16,8,16,8]{5,4,3,2,0,1:T(8,128)S(1)} %bitcast.175) | data formatting | bytes 393216 | tf_op jit(solution)/shard_map/broadcast_in_dim;reshape | solution.py:242
  (120 shorter events, 11.6 us)
Async XLA Ops:
  3.1 77.8 %collective-permute-start.4 = (f32[4,3,1,128]{3,0,2,1:T(4,128)}, f32[4,3,1,128]{3,0,2,1:T(4,128)S(1)}, u32[]{:S(2)}, u32[]{:S(2)}) collective-permute-start(f32[4,3,1,128]{3,0,2,1:T(4,128)} %pad_maximum_fusion.12), channel_id=1, source_target_pairs={{0,256},{256,0},{1,257},{257,1},{2,258},{258,2},{3,259},{259,3},{4... | collective-permute-start | bytes 18440 | tf_op jit(solution)/shard_map/ppermute | solution.py:28
  10.6 59.8 %collective-permute-start.1 = (f32[3,1,1,128]{2,3,1,0:T(8,128)}, f32[3,1,1,128]{2,3,1,0:T(8,128)}, u32[]{:S(2)}, u32[]{:S(2)}) collective-permute-start(f32[3,1,1,128]{2,3,1,0:T(8,128)} %get-tuple-element.55), channel_id=1, source_target_pairs={{16,0},{32,16},{48,32},{64,48},{80,64},{96,80},{112,96},{128,112},... | collective-permute-start | bytes 4616 | tf_op jit(solution)/shard_map/ppermute | solution.py:39
  13.4 57.0 %collective-permute-start = (f32[3,1,1,128]{2,3,1,0:T(8,128)}, f32[3,1,1,128]{2,3,1,0:T(8,128)S(1)}, u32[]{:S(2)}, u32[]{:S(2)}) collective-permute-start(f32[3,1,1,128]{2,3,1,0:T(8,128)} %get-tuple-element.56), channel_id=1, source_target_pairs={{0,16},{16,32},{32,48},{48,64},{64,80},{80,96},{96,112},{112,128},... | collective-permute-start | bytes 4616 | tf_op jit(solution)/shard_map/ppermute | solution.py:36
  16.8 3.9 %copy-start.12 = (s32[16]{0:T(128)}, s32[16]{0:T(128)S(1)}, u32[]{:S(2)}) copy-start(s32[16]{0:T(128)S(1)} %convert_reduce_fusion.1) | copy-start | bytes 196
  39.1 0.6 copy-start.9
  42.9 14.6 %copy-start.6 = (s32[1,4]{1,0:T(1,128)S(1)}, s32[1,4]{1,0:T(1,128)}, u32[]{:S(2)}) copy-start(s32[1,4]{1,0:T(1,128)} %param.10) | copy-start | bytes 52
  47.1 22.5 %copy-start.1 = (f32[1,128,128]{2,1,0:T(8,128)S(1)}, f32[1,128,128]{2,1,0:T(8,128)}, u32[]{:S(2)}) copy-start(f32[1,128,128]{2,1,0:T(8,128)} %param.9) | copy-start | bytes 196612
  49.3 89.2 %all-to-all-start = ((f32[16,2,192]{2,1,0:T(2,128)}), f32[16,2,192]{2,1,0:T(2,128)}, u32[]{:S(2)}, u32[]{:S(2)}) async-start(f32[16,2,192]{2,1,0:T(2,128)} %reshape.995), calls=%async_computation | async-start | bytes 65536 | tf_op jit(solution)/shard_map/all_to_all | solution.py:195
  59.3 21.6 %copy-start.2 = (f32[16,3,1,1,24]{4,3,0,1,2:T(1,128)}, f32[16,3,1,1,24]{4,3,0,1,2:T(1,128)S(1)}, u32[]{:S(2)}) copy-start(f32[16,3,1,1,24]{4,3,0,1,2:T(1,128)S(1)} %get-tuple-element.37) | copy-start | bytes 13828
  59.3 21.6 %copy-start.4 = (f32[16,3,1,1,24]{4,3,0,1,2:T(1,128)}, f32[16,3,1,1,24]{4,3,0,1,2:T(1,128)S(1)}, u32[]{:S(2)}) copy-start(f32[16,3,1,1,24]{4,3,0,1,2:T(1,128)S(1)} %get-tuple-element.38) | copy-start | bytes 13828
  71.3 5.6 %collective-permute-start.2 = (f32[3,1,130,1]{2,3,1,0:T(1,128)S(1)}, f32[3,1,130,1]{2,3,1,0:T(1,128)S(1)}, u32[]{:S(2)}, u32[]{:S(2)}) collective-permute-start(f32[3,1,130,1]{2,3,1,0:T(1,128)S(1)} %get-tuple-element.41), channel_id=1, source_target_pairs={{0,1},{1,2},{2,3},{3,4},{4,5},{5,6},{6,7},{7,8},{8,9},{9,10},{10,1... | collective-permute-start | bytes 4688 | tf_op jit(solution)/shard_map/ppermute | solution.py:36
  74.8 4.9 %collective-permute-start.3 = (f32[3,1,130,1]{2,3,1,0:T(1,128)S(1)}, f32[3,1,130,1]{2,3,1,0:T(1,128)S(1)}, u32[]{:S(2)}, u32[]{:S(2)}) collective-permute-start(f32[3,1,130,1]{2,3,1,0:T(1,128)S(1)} %get-tuple-element.42), channel_id=1, source_target_pairs={{1,0},{2,1},{3,2},{4,3},{5,4},{6,5},{7,6},{8,7},{9,8},{10,9},{11,1... | collective-permute-start | bytes 4688 | tf_op jit(solution)/shard_map/ppermute | solution.py:39
  86.7 10.2 %collective-permute-start.6 = (f32[3,1,1,128]{2,3,1,0:T(8,128)S(1)}, f32[3,1,1,128]{2,3,1,0:T(8,128)S(1)}, u32[]{:S(2)}, u32[]{:S(2)}) collective-permute-start(f32[3,1,1,128]{2,3,1,0:T(8,128)S(1)} %get-tuple-element.51), channel_id=1, source_target_pairs={{16,0},{32,16},{48,32},{64,48},{80,64},{96,80},{112,96},{128,112},... | collective-permute-start | bytes 4616 | tf_op jit(solution)/shard_map/ppermute | solution.py:39
  92.2 10.1 %collective-permute-start.5 = (f32[3,1,1,128]{2,3,1,0:T(8,128)S(1)}, f32[3,1,1,128]{2,3,1,0:T(8,128)S(1)}, u32[]{:S(2)}, u32[]{:S(2)}) collective-permute-start(f32[3,1,1,128]{2,3,1,0:T(8,128)S(1)} %get-tuple-element.52), channel_id=1, source_target_pairs={{0,16},{16,32},{32,48},{48,64},{64,80},{80,96},{96,112},{112,128},... | collective-permute-start | bytes 4616 | tf_op jit(solution)/shard_map/ppermute | solution.py:36
  102.4 28.2 %copy-start = (f32[1,128,128]{1,0,2:T(1,128)S(1)}, f32[1,128,128]{1,0,2:T(1,128)}, u32[]{:S(2)}) copy-start(f32[1,128,128]{1,0,2:T(1,128)} %copy.868) | copy-start | bytes 196612
  102.4 10.9 %collective-permute-start.7 = (f32[3,1,130,1]{2,3,1,0:T(1,128)S(1)}, f32[3,1,130,1]{2,3,1,0:T(1,128)S(1)}, u32[]{:S(2)}, u32[]{:S(2)}) collective-permute-start(f32[3,1,130,1]{2,3,1,0:T(1,128)S(1)} %get-tuple-element.39), channel_id=1, source_target_pairs={{0,1},{1,2},{2,3},{3,4},{4,5},{5,6},{6,7},{7,8},{8,9},{9,10},{10,1... | collective-permute-start | bytes 4688 | tf_op jit(solution)/shard_map/ppermute | solution.py:36
  106.7 6.6 %collective-permute-start.8 = (f32[3,1,130,1]{2,3,1,0:T(1,128)S(1)}, f32[3,1,130,1]{2,3,1,0:T(1,128)S(1)}, u32[]{:S(2)}, u32[]{:S(2)}) collective-permute-start(f32[3,1,130,1]{2,3,1,0:T(1,128)S(1)} %get-tuple-element.40), channel_id=1, source_target_pairs={{1,0},{2,1},{3,2},{4,3},{5,4},{6,5},{7,6},{8,7},{9,8},{10,9},{11,1... | collective-permute-start | bytes 4688 | tf_op jit(solution)/shard_map/ppermute | solution.py:39
  108.7 8.3 %collective-permute-start.9 = (f32[4,3,1,128]{3,0,2,1:T(4,128)S(1)}, f32[4,3,1,128]{3,0,2,1:T(4,128)S(1)}, u32[]{:S(2)}, u32[]{:S(2)}) collective-permute-start(f32[4,3,1,128]{3,0,2,1:T(4,128)S(1)} %pad_maximum_fusion.13), channel_id=1, source_target_pairs={{0,256},{256,0},{1,257},{257,1},{2,258},{258,2},{3,259},{259,3},{4... | collective-permute-start | bytes 18440 | tf_op jit(solution)/shard_map/ppermute | solution.py:28
  133.8 9.4 %copy-start.3 = (f32[16,3,1,1,24]{4,3,0,1,2:T(1,128)S(1)}, f32[16,3,1,1,24]{4,3,0,1,2:T(1,128)}, u32[]{:S(2)}) copy-start(f32[16,3,1,1,24]{4,3,0,1,2:T(1,128)} %copy-done.2) | copy-start | bytes 13828
  133.8 9.4 %copy-start.5 = (f32[16,3,1,1,24]{4,3,0,1,2:T(1,128)S(1)}, f32[16,3,1,1,24]{4,3,0,1,2:T(1,128)}, u32[]{:S(2)}) copy-start(f32[16,3,1,1,24]{4,3,0,1,2:T(1,128)} %copy-done.4) | copy-start | bytes 13828
  143.1 3.0 %copy-start.8 = (s32[16]{0:T(128)S(1)}, s32[16]{0:T(128)}, u32[]{:S(2)}) copy-start(s32[16]{0:T(128)} %get-tuple-element.87) | copy-start | bytes 196
  143.1 3.0 %copy-start.11 = (s32[16,2]{0,1:T(2,128)S(1)}, s32[16,2]{0,1:T(2,128)}, u32[]{:S(2)}) copy-start(s32[16,2]{0,1:T(2,128)} %multiply_add_fusion.5) | copy-start | bytes 388
  147.3 20.5 %all-to-all-start.1 = ((f32[16,2,1728]{2,1,0:T(2,128)}), f32[16,2,1728]{2,1,0:T(2,128)}, u32[]{:S(2)}, u32[]{:S(2)}) async-start(f32[16,2,1728]{2,1,0:T(2,128)} %copy.881), calls=%async_computation.1 | async-start | bytes 458752 | tf_op jit(solution)/shard_map/all_to_all | solution.py:227
  179.1 4.9 %copy-start.7 = (pred[32]{0:T(512)(128)(4,1)S(1)}, pred[32]{0:T(512)(128)(4,1)}, u32[]{:S(2)}) copy-start(pred[32]{0:T(512)(128)(4,1)} %compare_and_fusion) | copy-start | bytes 100
  179.1 4.9 %copy-start.10 = (s32[32]{0:T(128)S(1)}, s32[32]{0:T(128)}, u32[]{:S(2)}) copy-start(s32[32]{0:T(128)} %copy-done.9) | copy-start | bytes 388
where the time goes:
time: 192 us; the launch traced here: 190 us
  local copies, waits for them, and re-layouts  68.7 us (36%)
  starting transfers between devices  52.8 us (28%)
  other arithmetic  22.9 us (12%)
  blocking collectives  17.9 us (9%)
  waiting for transfers between devices  15.3 us (8%)
  between operations  12 us (6%)
    unnamed x1, blocking collectives  17.9 us
    ppermute x4, starting transfers between devices, extended(): lax.ppermute(lax.slice_in_dim(block, block.shape[dim] - width, None, axis...  12.3 us
    ppermute x4, starting transfers between devices, extended(): lax.ppermute(lax.slice_in_dim(block, 0, width, axis=dim), axis, backward)  12.1 us
    ppermute x2, starting transfers between devices, from_partner(): return lax.ppermute(block, axis, route)  12.1 us
    dynamic_update_slice x2, local copies, waits for them, and re-layouts, place_side(): return lax.dynamic_update_slice(padded, new, (zero, zero, row, 1))  12 us
    another operation x1, local copies, waits for them, and re-layouts, block_means(): blocks.reshape(count, 3, blocks.shape[2], PATCH, RATIO, PATCH, RATIO)  11.4 us
    all_to_all x1, starting transfers between devices, body(): lax.all_to_all(backward.reshape(devices_y, capacity, -1), 'gy', split_axi...  9.43 us
    all_to_all x1, starting transfers between devices, body(): lax.all_to_all(outgoing.reshape(devices_y, capacity, -1), 'gy', split_axi...  6.96 us
  transfers between devices with their start and end apart: 12, of which 5 were waited for; matrix products, arithmetic and copies ran while one was open for 31% of the time, Pallas kernels for 0%

commit v1 on v0

v1 whole, which is shorter than its diff:
```python
import jax
import jax.numpy as jnp
from jax import lax
from jax.sharding import PartitionSpec as P

NSUB = 2
PATCH = 8
RATIO = 3
FINE = 24


DT_STEP = 0.25
GRAVITY = 1.0
DAMPING = 0.5
DEPTH = 1.0
KAPPA = 0.2
ALPHA = 0.5
BETA = 0.5

HI = lax.Precision.HIGHEST


def shift_pairs(count, step):
    return [(i, i + step) for i in range(count) if 0 <= i + step < count]


def rotated(code, east_part, north_part):
    along = (code == 0).astype(east_part.dtype) - (code == 2).astype(east_part.dtype)
    across = (code == 3).astype(east_part.dtype) - (code == 1).astype(east_part.dtype)
    return (along * east_part + across * north_part, along * north_part - across * east_part)


def centre(field):
    return field[..., 1:-1, 1:-1]


def along_x(field):
    return 0.5 * (field[..., 2:, 1:-1] - field[..., :-2, 1:-1])


def along_y(field):
    return 0.5 * (field[..., 1:-1, 2:] - field[..., 1:-1, :-2])


def laplacian(field):
    return (
        field[..., 2:, 1:-1]
        + field[..., :-2, 1:-1]
        + field[..., 1:-1, 2:]
        + field[..., 1:-1, :-2]
        - 4.0 * centre(field)
    )


def advance(height, east, north, coriolis):
    absolute = coriolis + along_x(north) - along_y(east)
    depth = DEPTH + height
    divergence = along_x(depth * east) + along_y(depth * north)
    new_height = centre(height) - DT_STEP * divergence
    new_east = centre(east) + DT_STEP * (
        absolute * centre(north) - GRAVITY * along_x(height) + DAMPING * laplacian(east)
    )
    new_north = centre(north) + DT_STEP * (
        -absolute * centre(east) - GRAVITY * along_y(height) + DAMPING * laplacian(north)
    )
    return (new_height, new_east, new_north)


def padded_field(field, west, east, south, north):
    rows = jnp.concatenate([west[:, None, :], field, east[:, None, :]], axis=1)
    zero = jnp.zeros_like(south[:, :1])
    low = jnp.concatenate([zero, south, zero], axis=1)[:, :, None]
    high = jnp.concatenate([zero, north, zero], axis=1)[:, :, None]
    return jnp.concatenate([low, rows, high], axis=2)


def substep(fields, coriolis, codes, flags):
    nx = lax.axis_size("gx")
    ny = lax.axis_size("gy")
    first_rows = jnp.stack([f[:, 0, :] for f in fields], axis=0)
    last_rows = jnp.stack([f[:, -1, :] for f in fields], axis=0)
    first_cols = jnp.stack([f[:, :, 0] for f in fields], axis=0)
    last_cols = jnp.stack([f[:, :, -1] for f in fields], axis=0)
    from_west = lax.ppermute(last_rows, "gx", shift_pairs(nx, 1))
    from_east = lax.ppermute(first_rows, "gx", shift_pairs(nx, -1))
    from_south = lax.ppermute(last_cols, "gy", shift_pairs(ny, 1))
    from_north = lax.ppermute(first_cols, "gy", shift_pairs(ny, -1))
    strips = jnp.stack([first_rows, last_rows, first_cols, last_cols], axis=0)
    partner = lax.ppermute(strips, "panel", [(0, 1), (1, 0)])
    halos = []
    for side, neighbour in enumerate((from_west, from_east, from_south, from_north)):
        strip = partner[side]
        east_rot, north_rot = rotated(codes[side], strip[1], strip[2])
        strip = jnp.stack([strip[0], east_rot, north_rot], axis=0)
        halos.append(jnp.where(flags[side], strip, neighbour))
    padded = [padded_field(fields[c], *(h[c] for h in halos)) for c in range(3)]
    return advance(padded[0], padded[1], padded[2], coriolis)


def body(state, coriolis, edge_rotation, nest_block_state, parent_tile_index, parent_spot_index):
    devices_y = lax.axis_size("gy")
    slots = nest_block_state.shape[2]
    capacity = 2
    width = devices_y * capacity
    my_row = lax.axis_index("gy")
    my_column = lax.axis_index("gx")
    tile = state[0]
    level_stack = tile.shape[1]
    side_x = tile.shape[2]
    side_y = tile.shape[3]
    qy = side_y // PATCH
    cells = 3 * level_stack * PATCH * PATCH

    mine = parent_tile_index.reshape(slots)
    spots = parent_spot_index.reshape(slots)
    local = jnp.arange(slots, dtype=jnp.int32)
    rank = jnp.sum(
        ((mine[:, None] == mine[None, :]) & (local[None, :] < local[:, None])).astype(jnp.int32),
        axis=1,
    )
    slot_of = mine * capacity + rank
    slot_hit = jnp.arange(width, dtype=jnp.int32)[:, None] == slot_of[None, :]
    request = jnp.sum(jnp.where(slot_hit, spots[None, :] + 1, 0), axis=1) - 1
    asked = lax.all_to_all(
        request.reshape(devices_y, capacity), "gy", split_axis=0, concat_axis=0, tiled=True
    ).reshape(width)

    valid = asked >= 0
    row0 = (asked // qy) * PATCH
    col0 = (asked % qy) * PATCH
    offs = jnp.arange(PATCH, dtype=jnp.int32)
    rows_at = jnp.arange(side_x, dtype=jnp.int32)
    cols_at = jnp.arange(side_y, dtype=jnp.int32)
    row_sel = (
        (rows_at[None, None, :] == (row0[:, None, None] + offs[None, :, None]))
        & valid[:, None, None]
    ).astype(jnp.float32)
    col_sel = (cols_at[None, None, :] == (col0[:, None, None] + offs[None, :, None])).astype(
        jnp.float32
    )
    picked_rows = jnp.einsum("kar,flrc->kflac", row_sel, tile, precision=HI)
    picked = jnp.einsum("kflac,kbc->kflab", picked_rows, col_sel, precision=HI)
    incoming = lax.all_to_all(
        picked.reshape(devices_y, capacity, cells), "gy", split_axis=0, concat_axis=0, tiled=True
    ).reshape(width, cells)

    parent = jnp.take(incoming, slot_of, axis=0)
    fine_cells = FINE * FINE
    coarse_cells = PATCH * PATCH
    n_idx = jnp.arange(fine_cells, dtype=jnp.int32)
    fi = n_idx // FINE
    fj = n_idx % FINE
    coarse_of = (fi // RATIO) * PATCH + (fj // RATIO)
    m_idx = jnp.arange(coarse_cells, dtype=jnp.int32)
    spread = (m_idx[:, None] == coarse_of[None, :]).astype(jnp.float32)
    coarse = parent.reshape(slots * 3 * level_stack, coarse_cells)
    upsampled = jnp.dot(coarse, spread, precision=HI)
    blocks = nest_block_state[0, 0].reshape(slots * 3 * level_stack, fine_cells)
    pad_lo = jnp.concatenate([blocks[:, :FINE], blocks[:, :-FINE]], axis=1)
    pad_hi = jnp.concatenate([blocks[:, FINE:], blocks[:, -FINE:]], axis=1)
    left = jnp.concatenate([blocks[:, :1], blocks[:, :-1]], axis=1)
    right = jnp.concatenate([blocks[:, 1:], blocks[:, -1:]], axis=1)
    left = jnp.where((fj == 0)[None, :], blocks, left)
    right = jnp.where((fj == FINE - 1)[None, :], blocks, right)
    lap = pad_hi + pad_lo + right + left - 4.0 * blocks
    smoothed = blocks + KAPPA * lap
    blended = smoothed + ALPHA * (upsampled - smoothed)
    sums = jnp.dot(blended, spread.T, precision=HI)
    means = (sums / float(RATIO * RATIO)).reshape(slots, cells)
    back = jnp.dot(slot_hit.astype(jnp.float32), means, precision=HI)
    returned = lax.all_to_all(
        back.reshape(devices_y, capacity, cells), "gy", split_axis=0, concat_axis=0, tiled=True
    ).reshape(width, 3, level_stack, PATCH, PATCH)

    codes = edge_rotation[0]
    flags = [
        my_column == 0,
        my_column == lax.axis_size("gx") - 1,
        my_row == 0,
        my_row == devices_y - 1,
    ]
    fields = (tile[0], tile[1], tile[2])
    cell_coriolis = coriolis[0][None]
    for sub in range(NSUB):
        fields = substep(fields, cell_coriolis, codes, flags)

    spread_cols = jnp.einsum("kflab,kbc->kflac", returned, col_sel, precision=HI)
    dense = jnp.einsum("kar,kflac->flrc", row_sel, spread_cols, precision=HI)
    row_mask = jnp.sum(row_sel, axis=1)
    col_mask = jnp.sum(col_sel, axis=1)
    count = jnp.dot(row_mask.T, col_mask, precision=HI)
    after = jnp.stack(fields, axis=0)
    final_result = after + BETA * (dense - count[None, None] * after)
    return (final_result[None], blended.reshape(1, 1, slots, 3, level_stack, fine_cells))


def solution(mesh):
    in_specs = (
        P("panel", None, None, "gx", "gy"),
        P("panel", "gx", "gy"),
        P("panel", None),
        P("panel", "gx", "gy", None, None, None),
        P("panel", "gx", "gy", None),
        P("panel", "gx", "gy"),
    )
    out_specs = (P("panel", None, None, "gx", "gy"), P("panel", "gx", "gy", None, None, None))
    return jax.shard_map(body, mesh=mesh, in_specs=in_specs, out_specs=out_specs, check_vma=False)
```

time: 192 us -> 103 us (0.54)
  the two profiles are of different devices: /device:TPU:7 before, /device:TPU:57 now
where the time goes in v1:
time: 103 us
  starting transfers between devices  61.7 us (60%)
  waiting for transfers between devices  11.7 us (11%)
  between operations  11.4 us (11%)
  local copies, waits for them, and re-layouts  9.47 us (9%)
  other arithmetic  5.2 us (5%)
  matrix products  2.98 us (3%)
    ppermute x2, starting transfers between devices, substep(): partner = lax.ppermute(strips, 'panel', [(0, 1), (1, 0)])  11.3 us
    all_to_all x1, starting transfers between devices, body(): lax.all_to_all(request.reshape(devices_y, capacity), 'gy', split_axis=0,...  9.53 us
    ppermute x2, starting transfers between devices, substep(): from_west = lax.ppermute(last_rows, 'gx', shift_pairs(nx, 1))  8.84 us
    all_to_all x1, starting transfers between devices, body(): lax.all_to_all(back.reshape(devices_y, capacity, cells), 'gy', split_axis...  7.64 us
    ppermute x2, starting transfers between devices, substep(): from_south = lax.ppermute(last_cols, 'gy', shift_pairs(ny, 1))  7.63 us
    all_to_all x1, starting transfers between devices, body(): lax.all_to_all(picked.reshape(devices_y, capacity, cells), 'gy', split_ax...  7.23 us
    all_to_all x1, waiting for transfers between devices, body(): lax.all_to_all(back.reshape(devices_y, capacity, cells), 'gy', split_axis...  6.5 us
    ppermute x2, waiting for transfers between devices, substep(): from_east = lax.ppermute(first_rows, 'gx', shift_pairs(nx, -1))  5.18 us
  transfers between devices with their start and end apart: 13, of which 2 were waited for; matrix products, arithmetic and copies ran while one was open for 11% of the time, Pallas kernels for 0%

profile of v1, /device:TPU:57, one launch (start us, length us, event | category | flops | bytes accessed | tf_op | source)
XLA Modules:
  0.0 102.5 jit_solution(2504000517010720010)
XLA Ops:
  0.6 0.9 fusion.129
  1.6 0.1 copy.366
  1.7 0.1 copy.367
  1.9 0.1 copy.368
  2.1 0.2 pad_maximum_fusion
  2.3 0.1 pad_maximum_fusion.1
  2.5 4.4 %collective-permute-start = (f32[4,3,1,128]{3,0,1,2:T(4,128)S(1)}, f32[4,3,1,128]{3,0,1,2:T(4,128)S(1)}, u32[]{:S(2)}, u32[]{:S(2)}) collective-permute-start(f32[4,3,1,128]{3,0,1,2:T(4,128)S(1)} %pad_maximum_fusion.53), channel_id=1, source_target_pairs={{0,256},{256,0},{1,257},{257,1},{2,258},{258,2},{3,259},{259,3},{4... | collective-permute-start | bytes 18440 | tf_op jit(solution)/shard_map/ppermute | solution.py:89
  7.0 2.9 %collective-permute-start.4 = (f32[3,1,128]{2,1,0:T(1,128)S(1)}, f32[3,1,128]{2,1,0:T(1,128)S(1)}, u32[]{:S(2)}, u32[]{:S(2)}) collective-permute-start(f32[3,1,128]{2,1,0:T(1,128)S(1)} %pad_maximum_fusion.55), channel_id=1, source_target_pairs={{1,0},{2,1},{3,2},{4,3},{5,4},{6,5},{7,6},{8,7},{9,8},{10,9},{11,1... | collective-permute-start | bytes 4616 | tf_op jit(solution)/shard_map/ppermute | solution.py:87
  9.9 3.9 %collective-permute-start.1 = (f32[3,1,128]{2,1,0:T(1,128)S(1)}, f32[3,1,128]{2,1,0:T(1,128)S(1)}, u32[]{:S(2)}, u32[]{:S(2)}) collective-permute-start(f32[3,1,128]{2,1,0:T(1,128)S(1)} %pad_maximum_fusion.56), channel_id=1, source_target_pairs={{0,1},{1,2},{2,3},{3,4},{4,5},{5,6},{6,7},{7,8},{8,9},{9,10},{10,1... | collective-permute-start | bytes 4616 | tf_op jit(solution)/shard_map/ppermute | solution.py:86
  13.8 2.8 %collective-permute-start.2 = (f32[3,1,128]{1,2,0:T(8,128)S(1)}, f32[3,1,128]{1,2,0:T(8,128)S(1)}, u32[]{:S(2)}, u32[]{:S(2)}) collective-permute-start(f32[3,1,128]{1,2,0:T(8,128)S(1)} %get-tuple-element.34), channel_id=1, source_target_pairs={{0,16},{16,32},{32,48},{48,64},{64,80},{80,96},{96,112},{112,128},... | collective-permute-start | bytes 4616 | tf_op jit(solution)/shard_map/ppermute | solution.py:84
  16.6 2.5 %collective-permute-start.3 = (f32[3,1,128]{1,2,0:T(8,128)S(1)}, f32[3,1,128]{1,2,0:T(8,128)S(1)}, u32[]{:S(2)}, u32[]{:S(2)}) collective-permute-start(f32[3,1,128]{1,2,0:T(8,128)S(1)} %get-tuple-element.36), channel_id=1, source_target_pairs={{16,0},{32,16},{48,32},{64,48},{80,64},{96,80},{112,96},{128,112},... | collective-permute-start | bytes 4616 | tf_op jit(solution)/shard_map/ppermute | solution.py:85
  19.1 0.2 convert_reduce_fusion.2
  19.3 0.1 select_reduce_fusion
  19.4 0.7 sub.347
  20.1 9.5 %all-to-all-start = ((s32[16,1,2]{2,1,0:T(1,128)}), s32[16,1,2]{2,1,0:T(1,128)S(1)}, u32[]{:S(2)}, u32[]{:S(2)}) async-start(s32[16,1,2]{2,1,0:T(1,128)} %bitcast.84), calls=%async_computation | async-start | bytes 16384 | tf_op jit(solution)/shard_map/all_to_all | solution.py:124
  29.6 0.6 fusion.140
  40.1 0.3 reduce.4
  40.5 0.1 fusion.131
  40.6 0.1 fusion.133
  41.0 0.5 copy-done.2
  41.7 0.1 broadcast_in_dim.44
  41.9 0.5 broadcast.781
  42.4 0.7 reduce.12
  43.3 0.4 convolution_bitcast_fusion
  43.6 0.1 convert_reduce_fusion.1
  43.8 0.1 convert_reduce_fusion
  43.9 0.5 fusion.10
  44.4 0.8 reshape.1371
  45.3 7.2 %all-to-all-start.1 = ((f32[16,2,192]{2,1,0:T(2,128)}), f32[16,2,192]{2,1,0:T(2,128)S(1)}, u32[]{:S(2)}, u32[]{:S(2)}) async-start(f32[16,2,192]{2,1,0:T(2,128)} %reshape.1371), calls=%async_computation.1 | async-start | bytes 65536 | tf_op jit(solution)/shard_map/all_to_all | solution.py:143
  52.5 0.3 fusion.141
  52.9 0.1 copy.349
  53.2 0.1 copy.350
  53.6 0.2 maximum_multiply_fusion
  53.8 0.3 fusion.70
  54.1 0.2 maximum_multiply_fusion.1
  54.2 0.2 fusion.58
  54.5 0.1 fusion.79
  54.9 0.1 pad_maximum_fusion.2
  55.1 0.2 pad_maximum_fusion.3
  55.3 6.9 %collective-permute-start.5 = (f32[4,3,1,128]{3,0,1,2:T(4,128)S(1)}, f32[4,3,1,128]{3,0,1,2:T(4,128)S(1)}, u32[]{:S(2)}, u32[]{:S(2)}) collective-permute-start(f32[4,3,1,128]{3,0,1,2:T(4,128)S(1)} %pad_maximum_fusion.54), channel_id=1, source_target_pairs={{0,256},{256,0},{1,257},{257,1},{2,258},{258,2},{3,259},{259,3},{4... | collective-permute-start | bytes 18440 | tf_op jit(solution)/shard_map/ppermute | solution.py:89
  62.1 2.3 %collective-permute-start.9 = (f32[3,1,128]{2,1,0:T(1,128)S(1)}, f32[3,1,128]{2,1,0:T(1,128)S(1)}, u32[]{:S(2)}, u32[]{:S(2)}) collective-permute-start(f32[3,1,128]{2,1,0:T(1,128)S(1)} %pad_maximum_fusion.59), channel_id=1, source_target_pairs={{1,0},{2,1},{3,2},{4,3},{5,4},{6,5},{7,6},{8,7},{9,8},{10,9},{11,1... | collective-permute-start | bytes 4616 | tf_op jit(solution)/shard_map/ppermute | solution.py:87
  64.4 6.1 %collective-permute-start.7 = (f32[3,1,128]{1,2,0:T(8,128)S(1)}, f32[3,1,128]{1,2,0:T(8,128)S(1)}, u32[]{:S(2)}, u32[]{:S(2)}) collective-permute-start(f32[3,1,128]{1,2,0:T(8,128)S(1)} %get-tuple-element.24), channel_id=1, source_target_pairs={{0,16},{16,32},{32,48},{48,64},{64,80},{80,96},{96,112},{112,128},... | collective-permute-start | bytes 4616 | tf_op jit(solution)/shard_map/ppermute | solution.py:84
  70.5 1.9 %collective-permute-start.8 = (f32[3,1,128]{1,2,0:T(8,128)S(1)}, f32[3,1,128]{1,2,0:T(8,128)S(1)}, u32[]{:S(2)}, u32[]{:S(2)}) collective-permute-start(f32[3,1,128]{1,2,0:T(8,128)S(1)} %get-tuple-element.26), channel_id=1, source_target_pairs={{16,0},{32,16},{48,32},{64,48},{80,64},{96,80},{112,96},{128,112},... | collective-permute-start | bytes 4616 | tf_op jit(solution)/shard_map/ppermute | solution.py:85
  72.4 3.7 %collective-permute-start.6 = (f32[3,1,128]{2,1,0:T(1,128)S(1)}, f32[3,1,128]{2,1,0:T(1,128)S(1)}, u32[]{:S(2)}, u32[]{:S(2)}) collective-permute-start(f32[3,1,128]{2,1,0:T(1,128)S(1)} %pad_maximum_fusion.60), channel_id=1, source_target_pairs={{0,1},{1,2},{2,3},{3,4},{4,5},{5,6},{6,7},{7,8},{8,9},{9,10},{10,1... | collective-permute-start | bytes 4616 | tf_op jit(solution)/shard_map/ppermute | solution.py:86
  76.3 0.1 copy.352
  76.6 0.1 copy.353
  76.7 5.2 %collective-permute-done.8 = f32[3,1,128]{1,2,0:T(8,128)S(1)} collective-permute-done((f32[3,1,128]{1,2,0:T(8,128)S(1)}, f32[3,1,128]{1,2,0:T(8,128)S(1)}, u32[]{:S(2)}, u32[]{:S(2)}) %collective-permute-start.8) | collective-permute-done | bytes 1568 | tf_op jit(solution)/shard_map/ppermute | solution.py:85
  82.3 0.2 maximum_multiply_fusion.2
  82.5 0.3 fusion.42
  82.8 0.2 fusion.29
  83.0 0.2 maximum_multiply_fusion.3
  83.3 0.6 gather_fusion
  83.9 0.3 fusion.5
  84.2 0.2 convolution_multiply_fusion
  84.5 0.2 fusion.87
  84.7 0.6 copy.358
  85.3 7.6 %all-to-all-start.2 = ((f32[16,2,192]{2,1,0:T(2,128)}), f32[16,2,192]{2,1,0:T(2,128)S(1)}, u32[]{:S(2)}, u32[]{:S(2)}) async-start(f32[16,2,192]{2,1,0:T(2,128)} %copy.358), calls=%async_computation.2 | async-start | bytes 65536 | tf_op jit(solution)/shard_map/all_to_all | solution.py:171
  93.0 0.1 fusion.52
  93.1 0.8 reshape.1390
  93.9 6.5 %all-to-all-done.2 = f32[16,2,192]{2,1,0:T(2,128)S(1)} async-done(((f32[16,2,192]{2,1,0:T(2,128)}), f32[16,2,192]{2,1,0:T(2,128)S(1)}, u32[]{:S(2)}, u32[]{:S(2)}) %all-to-all-start.2) | async-done | bytes 24608 | tf_op jit(solution)/shard_map/all_to_all | solution.py:171
  100.4 0.2 reshape.1374
  100.6 0.5 fusion.8
  101.1 0.6 fusion.3
  101.7 0.8 copy.360
  (101 shorter events, 2.4 us)
Async XLA Ops:
  2.3 16.8 %copy-start.4 = (s32[1,1,16,1]{2,3,1,0:T(1,128)S(1)}, s32[1,1,16,1]{2,3,1,0:T(1,128)}, u32[]{:S(2)}) copy-start(s32[1,1,16,1]{2,3,1,0:T(1,128)} %param.10) | copy-start | bytes 196
  2.3 17.0 %copy-start.5 = (s32[1,1,16]{2,1,0:T(1,128)S(1)}, s32[1,1,16]{2,1,0:T(1,128)}, u32[]{:S(2)}) copy-start(s32[1,1,16]{2,1,0:T(1,128)} %param.11) | copy-start | bytes 196
  2.3 27.3 %copy-start.3 = (s32[1,4]{1,0:T(1,128)S(1)}, s32[1,4]{1,0:T(1,128)}, u32[]{:S(2)}) copy-start(s32[1,4]{1,0:T(1,128)} %param.8) | copy-start | bytes 52
  2.5 37.6 %copy-start.1 = (f32[1,1,16,3,1,576]{5,4,3,2,1,0:T(1,128)S(1)}, f32[1,1,16,3,1,576]{5,4,3,2,1,0:T(1,128)}, u32[]{:S(2)}) copy-start(f32[1,1,16,3,1,576]{5,4,3,2,1,0:T(1,128)} %param.9) | copy-start | bytes 331780
  2.5 50.3 %collective-permute-start = (f32[4,3,1,128]{3,0,1,2:T(4,128)S(1)}, f32[4,3,1,128]{3,0,1,2:T(4,128)S(1)}, u32[]{:S(2)}, u32[]{:S(2)}) collective-permute-start(f32[4,3,1,128]{3,0,1,2:T(4,128)S(1)} %pad_maximum_fusion.53), channel_id=1, source_target_pairs={{0,256},{256,0},{1,257},{257,1},{2,258},{258,2},{3,259},{259,3},{4... | collective-permute-start | bytes 18440 | tf_op jit(solution)/shard_map/ppermute | solution.py:89
  7.0 45.9 %collective-permute-start.4 = (f32[3,1,128]{2,1,0:T(1,128)S(1)}, f32[3,1,128]{2,1,0:T(1,128)S(1)}, u32[]{:S(2)}, u32[]{:S(2)}) collective-permute-start(f32[3,1,128]{2,1,0:T(1,128)S(1)} %pad_maximum_fusion.55), channel_id=1, source_target_pairs={{1,0},{2,1},{3,2},{4,3},{5,4},{6,5},{7,6},{8,7},{9,8},{10,9},{11,1... | collective-permute-start | bytes 4616 | tf_op jit(solution)/shard_map/ppermute | solution.py:87
  9.9 43.0 %collective-permute-start.1 = (f32[3,1,128]{2,1,0:T(1,128)S(1)}, f32[3,1,128]{2,1,0:T(1,128)S(1)}, u32[]{:S(2)}, u32[]{:S(2)}) collective-permute-start(f32[3,1,128]{2,1,0:T(1,128)S(1)} %pad_maximum_fusion.56), channel_id=1, source_target_pairs={{0,1},{1,2},{2,3},{3,4},{4,5},{5,6},{6,7},{7,8},{8,9},{9,10},{10,1... | collective-permute-start | bytes 4616 | tf_op jit(solution)/shard_map/ppermute | solution.py:86
  13.8 39.3 %collective-permute-start.2 = (f32[3,1,128]{1,2,0:T(8,128)S(1)}, f32[3,1,128]{1,2,0:T(8,128)S(1)}, u32[]{:S(2)}, u32[]{:S(2)}) collective-permute-start(f32[3,1,128]{1,2,0:T(8,128)S(1)} %get-tuple-element.34), channel_id=1, source_target_pairs={{0,16},{16,32},{32,48},{48,64},{64,80},{80,96},{96,112},{112,128},... | collective-permute-start | bytes 4616 | tf_op jit(solution)/shard_map/ppermute | solution.py:84
  16.6 36.7 %collective-permute-start.3 = (f32[3,1,128]{1,2,0:T(8,128)S(1)}, f32[3,1,128]{1,2,0:T(8,128)S(1)}, u32[]{:S(2)}, u32[]{:S(2)}) collective-permute-start(f32[3,1,128]{1,2,0:T(8,128)S(1)} %get-tuple-element.36), channel_id=1, source_target_pairs={{16,0},{32,16},{48,32},{64,48},{80,64},{96,80},{112,96},{128,112},... | collective-permute-start | bytes 4616 | tf_op jit(solution)/shard_map/ppermute | solution.py:85
  20.1 21.8 %all-to-all-start = ((s32[16,1,2]{2,1,0:T(1,128)}), s32[16,1,2]{2,1,0:T(1,128)S(1)}, u32[]{:S(2)}, u32[]{:S(2)}) async-start(s32[16,1,2]{2,1,0:T(1,128)} %bitcast.84), calls=%async_computation | async-start | bytes 16384 | tf_op jit(solution)/shard_map/all_to_all | solution.py:124
  40.7 0.8 copy-start.2
  40.8 2.5 %copy-start = (f32[1,3,1,128,128]{4,3,2,1,0:T(8,128)S(1)}, f32[1,3,1,128,128]{4,3,2,1,0:T(8,128)}, u32[]{:S(2)}) copy-start(f32[1,3,1,128,128]{4,3,2,1,0:T(8,128)} %param.6) | copy-start | bytes 589828
  45.3 37.9 %all-to-all-start.1 = ((f32[16,2,192]{2,1,0:T(2,128)}), f32[16,2,192]{2,1,0:T(2,128)S(1)}, u32[]{:S(2)}, u32[]{:S(2)}) async-start(f32[16,2,192]{2,1,0:T(2,128)} %reshape.1371), calls=%async_computation.1 | async-start | bytes 65536 | tf_op jit(solution)/shard_map/all_to_all | solution.py:143
  55.3 20.9 %collective-permute-start.5 = (f32[4,3,1,128]{3,0,1,2:T(4,128)S(1)}, f32[4,3,1,128]{3,0,1,2:T(4,128)S(1)}, u32[]{:S(2)}, u32[]{:S(2)}) collective-permute-start(f32[4,3,1,128]{3,0,1,2:T(4,128)S(1)} %pad_maximum_fusion.54), channel_id=1, source_target_pairs={{0,256},{256,0},{1,257},{257,1},{2,258},{258,2},{3,259},{259,3},{4... | collective-permute-start | bytes 18440 | tf_op jit(solution)/shard_map/ppermute | solution.py:89
  62.1 14.1 %collective-permute-start.9 = (f32[3,1,128]{2,1,0:T(1,128)S(1)}, f32[3,1,128]{2,1,0:T(1,128)S(1)}, u32[]{:S(2)}, u32[]{:S(2)}) collective-permute-start(f32[3,1,128]{2,1,0:T(1,128)S(1)} %pad_maximum_fusion.59), channel_id=1, source_target_pairs={{1,0},{2,1},{3,2},{4,3},{5,4},{6,5},{7,6},{8,7},{9,8},{10,9},{11,1... | collective-permute-start | bytes 4616 | tf_op jit(solution)/shard_map/ppermute | solution.py:87
  64.4 12.0 %collective-permute-start.7 = (f32[3,1,128]{1,2,0:T(8,128)S(1)}, f32[3,1,128]{1,2,0:T(8,128)S(1)}, u32[]{:S(2)}, u32[]{:S(2)}) collective-permute-start(f32[3,1,128]{1,2,0:T(8,128)S(1)} %get-tuple-element.24), channel_id=1, source_target_pairs={{0,16},{16,32},{32,48},{48,64},{64,80},{80,96},{96,112},{112,128},... | collective-permute-start | bytes 4616 | tf_op jit(solution)/shard_map/ppermute | solution.py:84
  70.5 11.4 %collective-permute-start.8 = (f32[3,1,128]{1,2,0:T(8,128)S(1)}, f32[3,1,128]{1,2,0:T(8,128)S(1)}, u32[]{:S(2)}, u32[]{:S(2)}) collective-permute-start(f32[3,1,128]{1,2,0:T(8,128)S(1)} %get-tuple-element.26), channel_id=1, source_target_pairs={{16,0},{32,16},{48,32},{64,48},{80,64},{96,80},{112,96},{128,112},... | collective-permute-start | bytes 4616 | tf_op jit(solution)/shard_map/ppermute | solution.py:85
  72.4 9.6 %collective-permute-start.6 = (f32[3,1,128]{2,1,0:T(1,128)S(1)}, f32[3,1,128]{2,1,0:T(1,128)S(1)}, u32[]{:S(2)}, u32[]{:S(2)}) collective-permute-start(f32[3,1,128]{2,1,0:T(1,128)S(1)} %pad_maximum_fusion.60), channel_id=1, source_target_pairs={{0,1},{1,2},{2,3},{3,4},{4,5},{5,6},{6,7},{7,8},{8,9},{9,10},{10,1... | collective-permute-start | bytes 4616 | tf_op jit(solution)/shard_map/ppermute | solution.py:86
  85.3 15.0 %all-to-all-start.2 = ((f32[16,2,192]{2,1,0:T(2,128)}), f32[16,2,192]{2,1,0:T(2,128)S(1)}, u32[]{:S(2)}, u32[]{:S(2)}) async-start(f32[16,2,192]{2,1,0:T(2,128)} %copy.358), calls=%async_computation.2 | async-start | bytes 65536 | tf_op jit(solution)/shard_map/all_to_all | solution.py:171

commit v2 on v1

--- a/solution.py
+++ b/solution.py
@@ -74,25 +74,44 @@
     return jnp.concatenate([low, rows, high], axis=2)
 
 
-def substep(fields, coriolis, codes, flags):
-    nx = lax.axis_size("gx")
-    ny = lax.axis_size("gy")
+def ring_pairs(count):
+    pairs = [(g, g + 1) for g in range(count - 1)]
+    pairs.append((count - 1, 2 * count - 1))
+    pairs += [(count + g, count + g - 1) for g in range(1, count)]
+    pairs.append((count, 0))
+    return pairs
+
+
+def ring_exchange(first, last, axis, on_first_panel):
+    count = lax.axis_size(axis)
+    forward = ring_pairs(count)
+    backward = [(target, source) for source, target in forward]
+    sent_forward = jnp.where(on_first_panel, last, first)
+    sent_backward = jnp.where(on_first_panel, first, last)
+    got_forward = lax.ppermute(sent_forward, ("panel", axis), forward)
+    got_backward = lax.ppermute(sent_backward, ("panel", axis), backward)
+    low = jnp.where(on_first_panel, got_forward, got_backward)
+    high = jnp.where(on_first_panel, got_backward, got_forward)
+    return low, high
+
+
+def edge_fix(strip, code, flag):
+    east_rot, north_rot = rotated(code, strip[1], strip[2])
+    turned = jnp.stack([strip[0], east_rot, north_rot], axis=0)
+    return jnp.where(flag, turned, strip)
+
+
+def substep(fields, coriolis, codes, flags, on_first_panel):
     first_rows = jnp.stack([f[:, 0, :] for f in fields], axis=0)
     last_rows = jnp.stack([f[:, -1, :] for f in fields], axis=0)
     first_cols = jnp.stack([f[:, :, 0] for f in fields], axis=0)
     last_cols = jnp.stack([f[:, :, -1] for f in fields], axis=0)
-    from_west = lax.ppermute(last_rows, "gx", shift_pairs(nx, 1))
-    from_east = lax.ppermute(first_rows, "gx", shift_pairs(nx, -1))
-    from_south = lax.ppermute(last_cols, "gy", shift_pairs(ny, 1))
-    from_north = lax.ppermute(first_cols, "gy", shift_pairs(ny, -1))
-    strips = jnp.stack([first_rows, last_rows, first_cols, last_cols], axis=0)
-    partner = lax.ppermute(strips, "panel", [(0, 1), (1, 0)])
-    halos = []
-    for side, neighbour in enumerate((from_west, from_east, from_south, from_north)):
-        strip = partner[side]
-        east_rot, north_rot = rotated(codes[side], strip[1], strip[2])
-        strip = jnp.stack([strip[0], east_rot, north_rot], axis=0)
-        halos.append(jnp.where(flags[side], strip, neighbour))
+    west, east = ring_exchange(first_rows, last_rows, "gx", on_first_panel)
+    south, north = ring_exchange(first_cols, last_cols, "gy", on_first_panel)
+    halos = [
+        edge_fix(strip, codes[side], flags[side])
+        for side, strip in enumerate((west, east, south, north))
+    ]
     padded = [padded_field(fields[c], *(h[c] for h in halos)) for c in range(3)]
     return advance(padded[0], padded[1], padded[2], coriolis)
 
@@ -104,12 +123,34 @@
     width = devices_y * capacity
     my_row = lax.axis_index("gy")
     my_column = lax.axis_index("gx")
+    on_first_panel = lax.axis_index("panel") == 0
     tile = state[0]
     level_stack = tile.shape[1]
     side_x = tile.shape[2]
     side_y = tile.shape[3]
     qy = side_y // PATCH
     cells = 3 * level_stack * PATCH * PATCH
+    fine_cells = FINE * FINE
+    coarse_cells = PATCH * PATCH
+
+    n_idx = jnp.arange(fine_cells, dtype=jnp.int32)
+    fi = n_idx // FINE
+    fj = n_idx % FINE
+    coarse_of = (fi // RATIO) * PATCH + (fj // RATIO)
+    m_idx = jnp.arange(coarse_cells, dtype=jnp.int32)
+    spread = (m_idx[:, None] == coarse_of[None, :]).astype(jnp.float32)
+    blocks = nest_block_state[0, 0].reshape(slots * 3 * level_stack, fine_cells)
+    pad_lo = jnp.concatenate([blocks[:, :FINE], blocks[:, :-FINE]], axis=1)
+    pad_hi = jnp.concatenate([blocks[:, FINE:], blocks[:, -FINE:]], axis=1)
+    left = jnp.concatenate([blocks[:, :1], blocks[:, :-1]], axis=1)
+    right = jnp.concatenate([blocks[:, 1:], blocks[:, -1:]], axis=1)
+    left = jnp.where((fj == 0)[None, :], blocks, left)
+    right = jnp.where((fj == FINE - 1)[None, :], blocks, right)
+    lap = pad_hi + pad_lo + right + left - 4.0 * blocks
+    smoothed = blocks + KAPPA * lap
+    smooth_means = (jnp.dot(smoothed, spread.T, precision=HI) / float(RATIO * RATIO)).reshape(
+        slots, cells
+    )
 
     mine = parent_tile_index.reshape(slots)
     spots = parent_spot_index.reshape(slots)
@@ -119,11 +160,19 @@
         axis=1,
     )
     slot_of = mine * capacity + rank
-    slot_hit = jnp.arange(width, dtype=jnp.int32)[:, None] == slot_of[None, :]
-    request = jnp.sum(jnp.where(slot_hit, spots[None, :] + 1, 0), axis=1) - 1
-    asked = lax.all_to_all(
-        request.reshape(devices_y, capacity), "gy", split_axis=0, concat_axis=0, tiled=True
-    ).reshape(width)
+    slot_hit = (jnp.arange(width, dtype=jnp.int32)[:, None] == slot_of[None, :]).astype(
+        jnp.float32
+    )
+    payload = jnp.concatenate(
+        [(spots + 1).astype(jnp.float32)[:, None], smooth_means], axis=1
+    )
+    outgoing = jnp.dot(slot_hit, payload, precision=HI)
+    asked_payload = lax.all_to_all(
+        outgoing.reshape(devices_y, capacity, cells + 1), "gy", split_axis=0, concat_axis=0,
+        tiled=True,
+    ).reshape(width, cells + 1)
+    asked = asked_payload[:, 0].astype(jnp.int32) - 1
+    asked_means = asked_payload[:, 1:].reshape(width, 3, level_stack, PATCH, PATCH)
 
     valid = asked >= 0
     row0 = (asked // qy) * PATCH
@@ -145,32 +194,9 @@
     ).reshape(width, cells)
 
     parent = jnp.take(incoming, slot_of, axis=0)
-    fine_cells = FINE * FINE
-    coarse_cells = PATCH * PATCH
-    n_idx = jnp.arange(fine_cells, dtype=jnp.int32)
-    fi = n_idx // FINE
-    fj = n_idx % FINE
-    coarse_of = (fi // RATIO) * PATCH + (fj // RATIO)
-    m_idx = jnp.arange(coarse_cells, dtype=jnp.int32)
-    spread = (m_idx[:, None] == coarse_of[None, :]).astype(jnp.float32)
     coarse = parent.reshape(slots * 3 * level_stack, coarse_cells)
     upsampled = jnp.dot(coarse, spread, precision=HI)
-    blocks = nest_block_state[0, 0].reshape(slots * 3 * level_stack, fine_cells)
-    pad_lo = jnp.concatenate([blocks[:, :FINE], blocks[:, :-FINE]], axis=1)
-    pad_hi = jnp.concatenate([blocks[:, FINE:], blocks[:, -FINE:]], axis=1)
-    left = jnp.concatenate([blocks[:, :1], blocks[:, :-1]], axis=1)
-    right = jnp.concatenate([blocks[:, 1:], blocks[:, -1:]], axis=1)
-    left = jnp.where((fj == 0)[None, :], blocks, left)
-    right = jnp.where((fj == FINE - 1)[None, :], blocks, right)
-    lap = pad_hi + pad_lo + right + left - 4.0 * blocks
-    smoothed = blocks + KAPPA * lap
     blended = smoothed + ALPHA * (upsampled - smoothed)
-    sums = jnp.dot(blended, spread.T, precision=HI)
-    means = (sums / float(RATIO * RATIO)).reshape(slots, cells)
-    back = jnp.dot(slot_hit.astype(jnp.float32), means, precision=HI)
-    returned = lax.all_to_all(
-        back.reshape(devices_y, capacity, cells), "gy", split_axis=0, concat_axis=0, tiled=True
-    ).reshape(width, 3, level_stack, PATCH, PATCH)
 
     codes = edge_rotation[0]
     flags = [
@@ -182,9 +208,10 @@
     fields = (tile[0], tile[1], tile[2])
     cell_coriolis = coriolis[0][None]
     for sub in range(NSUB):
-        fields = substep(fields, cell_coriolis, codes, flags)
-
-    spread_cols = jnp.einsum("kflab,kbc->kflac", returned, col_sel, precision=HI)
+        fields = substep(fields, cell_coriolis, codes, flags, on_first_panel)
+
+    block_mean = asked_means + ALPHA * (picked - asked_means)
+    spread_cols = jnp.einsum("kflab,kbc->kflac", block_mean, col_sel, precision=HI)
     dense = jnp.einsum("kar,kflac->flrc", row_sel, spread_cols, precision=HI)
     row_mask = jnp.sum(row_sel, axis=1)
     col_mask = jnp.sum(col_sel, axis=1)

time: 103 us -> 91.5 us (0.89)
  the two profiles are of different devices: /device:TPU:57 before, /device:TPU:31 now
where the time goes in v2:
time: 91.5 us; the launch traced here: 90.8 us
  starting transfers between devices  49.1 us (54%)
  waiting for transfers between devices  11.9 us (13%)
  between operations  11.7 us (13%)
  local copies, waits for them, and re-layouts  10.5 us (11%)
  other arithmetic  4.11 us (4%)
  matrix products  3.5 us (4%)
    ppermute x4, starting transfers between devices, ring_exchange(): got_forward = lax.ppermute(sent_forward, ('panel', axis), forward)  20.2 us
    all_to_all x1, starting transfers between devices, body(): lax.all_to_all(outgoing.reshape(devices_y, capacity, cells + 1), 'gy', sp...  13.3 us
    all_to_all x1, starting transfers between devices, body(): lax.all_to_all(picked.reshape(devices_y, capacity, cells), 'gy', split_ax...  7.89 us
    ppermute x4, starting transfers between devices, ring_exchange(): got_backward = lax.ppermute(sent_backward, ('panel', axis), backward)  7.68 us
    all_to_all x1, waiting for transfers between devices, body(): lax.all_to_all(picked.reshape(devices_y, capacity, cells), 'gy', split_ax...  5.99 us
    ppermute x4, waiting for transfers between devices, ring_exchange(): got_backward = lax.ppermute(sent_backward, ('panel', axis), backward)  5.85 us
    unnamed x12, local copies, waits for them, and re-layouts  2.63 us
  transfers between devices with their start and end apart: 10, of which 2 were waited for; matrix products, arithmetic and copies ran while one was open for 10% of the time, Pallas kernels for 0%

profile of v2, /device:TPU:31, one launch (start us, length us, event | category | flops | bytes accessed | tf_op | source)
XLA Modules:
  0.0 90.8 jit_solution(15675846272781949309)
XLA Ops:
  0.6 0.9 %slice_bitcast_fusion.2 = (f32[1,128,128]{2,1,0:T(8,128)S(1)}, f32[1,128,128]{2,1,0:T(8,128)S(1)}, f32[1,128,128]{2,1,0:T(8,128)S(1)}) fusion(f32[1,3,1,128,128]{4,3,2,1,0:T(8,128)} %param.6), kind=kLoop, calls=%fused_computation.166 | loop fusion | bytes 393216 | tf_op jit(solution)/shard_map/squeeze | solution.py:208
  1.6 0.2 slice_reduce_fusion.11
  1.8 0.2 slice_reduce_fusion.9
  2.0 4.6 %collective-permute-start = (f32[3,1,128]{2,1,0:T(1,128)S(1)}, f32[3,1,128]{2,1,0:T(1,128)S(1)}, u32[]{:S(2)}, u32[]{:S(2)}) collective-permute-start(f32[3,1,128]{2,1,0:T(1,128)S(1)} %get-tuple-element.68), channel_id=1, source_target_pairs={{0,1},{1,2},{2,3},{3,4},{4,5},{5,6},{6,7},{7,8},{8,9},{9,10},{10,1... | collective-permute-start | bytes 4616 | tf_op jit(solution)/shard_map/ppermute | solution.py:91
  6.6 1.9 %collective-permute-start.1 = (f32[3,1,128]{2,1,0:T(1,128)S(1)}, f32[3,1,128]{2,1,0:T(1,128)S(1)}, u32[]{:S(2)}, u32[]{:S(2)}) collective-permute-start(f32[3,1,128]{2,1,0:T(1,128)S(1)} %get-tuple-element.67), channel_id=1, source_target_pairs={{1,0},{2,1},{3,2},{4,3},{5,4},{6,5},{7,6},{8,7},{9,8},{10,9},{11,1... | collective-permute-start | bytes 4616 | tf_op jit(solution)/shard_map/ppermute | solution.py:92
  8.5 4.8 %collective-permute-start.2 = (f32[3,1,128]{2,1,0:T(1,128)S(1)}, f32[3,1,128]{2,1,0:T(1,128)S(1)}, u32[]{:S(2)}, u32[]{:S(2)}) collective-permute-start(f32[3,1,128]{2,1,0:T(1,128)S(1)} %get-tuple-element.65), channel_id=1, source_target_pairs={{0,16},{16,32},{32,48},{48,64},{64,80},{80,96},{96,112},{112,128},... | collective-permute-start | bytes 4616 | tf_op jit(solution)/shard_map/ppermute | solution.py:91
  13.3 1.9 %collective-permute-start.3 = (f32[3,1,128]{2,1,0:T(1,128)S(1)}, f32[3,1,128]{2,1,0:T(1,128)S(1)}, u32[]{:S(2)}, u32[]{:S(2)}) collective-permute-start(f32[3,1,128]{2,1,0:T(1,128)S(1)} %get-tuple-element.66), channel_id=1, source_target_pairs={{16,0},{32,16},{48,32},{64,48},{80,64},{96,80},{112,96},{128,112},... | collective-permute-start | bytes 4616 | tf_op jit(solution)/shard_map/ppermute | solution.py:92
  15.2 0.3 reduce.12
  16.0 0.2 fusion.22
  16.2 0.2 convolution_multiply_fusion
  16.5 0.7 copy-done.4
  17.2 0.2 convert_reduce_fusion.2
  17.4 0.6 copy-done.5
  18.1 0.2 fusion.87
  18.3 0.6 reshape.1551
  18.9 13.3 %all-to-all-start = ((f32[16,2,193]{2,1,0:T(2,128)}), f32[16,2,193]{2,1,0:T(2,128)S(1)}, u32[]{:S(2)}, u32[]{:S(2)}) async-start(f32[16,2,193]{2,1,0:T(2,128)} %reshape.1551), calls=%async_computation | async-start | bytes 65536 | tf_op jit(solution)/shard_map/all_to_all | solution.py:170
  32.2 0.7 fusion.146
  43.6 0.1 copy.257
  43.7 0.1 copy.259
  44.1 0.1 copy.256
  44.3 0.1 copy.258
  44.5 0.1 copy.261
  44.7 0.1 copy.260
  44.8 0.2 maximum_multiply_fusion
  45.0 0.6 copy-done.1
  45.6 0.1 fusion.71
  45.8 0.2 maximum_multiply_fusion.1
  46.0 0.2 fusion.59
  46.2 0.7 copy-done
  46.9 0.1 fusion.77
  47.0 0.2 slice_reduce_fusion.5
  47.2 0.2 slice_reduce_fusion.4
  47.4 0.2 slice_reduce_fusion.3
  47.6 3.5 %collective-permute-start.4 = (f32[3,1,128]{2,1,0:T(1,128)S(1)}, f32[3,1,128]{2,1,0:T(1,128)S(1)}, u32[]{:S(2)}, u32[]{:S(2)}) collective-permute-start(f32[3,1,128]{2,1,0:T(1,128)S(1)} %get-tuple-element.60), channel_id=1, source_target_pairs={{0,1},{1,2},{2,3},{3,4},{4,5},{5,6},{6,7},{7,8},{8,9},{9,10},{10,1... | collective-permute-start | bytes 4616 | tf_op jit(solution)/shard_map/ppermute | solution.py:91
  51.2 1.9 %collective-permute-start.5 = (f32[3,1,128]{2,1,0:T(1,128)S(1)}, f32[3,1,128]{2,1,0:T(1,128)S(1)}, u32[]{:S(2)}, u32[]{:S(2)}) collective-permute-start(f32[3,1,128]{2,1,0:T(1,128)S(1)} %get-tuple-element.59), channel_id=1, source_target_pairs={{1,0},{2,1},{3,2},{4,3},{5,4},{6,5},{7,6},{8,7},{9,8},{10,9},{11,1... | collective-permute-start | bytes 4616 | tf_op jit(solution)/shard_map/ppermute | solution.py:92
  53.1 7.4 %collective-permute-start.6 = (f32[3,1,128]{2,1,0:T(1,128)S(1)}, f32[3,1,128]{2,1,0:T(1,128)S(1)}, u32[]{:S(2)}, u32[]{:S(2)}) collective-permute-start(f32[3,1,128]{2,1,0:T(1,128)S(1)} %get-tuple-element.57), channel_id=1, source_target_pairs={{0,16},{16,32},{32,48},{48,64},{64,80},{80,96},{96,112},{112,128},... | collective-permute-start | bytes 4616 | tf_op jit(solution)/shard_map/ppermute | solution.py:91
  60.5 1.9 %collective-permute-start.7 = (f32[3,1,128]{2,1,0:T(1,128)S(1)}, f32[3,1,128]{2,1,0:T(1,128)S(1)}, u32[]{:S(2)}, u32[]{:S(2)}) collective-permute-start(f32[3,1,128]{2,1,0:T(1,128)S(1)} %get-tuple-element.58), channel_id=1, source_target_pairs={{16,0},{32,16},{48,32},{64,48},{80,64},{96,80},{112,96},{128,112},... | collective-permute-start | bytes 4616 | tf_op jit(solution)/shard_map/ppermute | solution.py:92
  62.6 0.1 copy.269
  62.7 0.1 copy.271
  62.9 5.8 %collective-permute-done.7 = f32[3,1,128]{2,1,0:T(1,128)S(1)} collective-permute-done((f32[3,1,128]{2,1,0:T(1,128)S(1)}, f32[3,1,128]{2,1,0:T(1,128)S(1)}, u32[]{:S(2)}, u32[]{:S(2)}) %collective-permute-start.7) | collective-permute-done | bytes 1568 | tf_op jit(solution)/shard_map/ppermute | solution.py:92
  68.9 0.1 copy.268
  69.1 0.1 copy.270
  69.3 0.1 copy.273
  69.5 0.1 copy.272
  69.6 0.2 maximum_multiply_fusion.2
  69.8 0.1 fusion.46
  69.9 0.2 maximum_multiply_fusion.3
  70.1 0.2 fusion.33
  70.4 0.1 fusion.53
  70.6 0.1 fusion.86
  70.8 0.4 convolution_bitcast_fusion
  71.2 0.1 convert_reduce_fusion.1
  71.5 0.1 convert_reduce_fusion
  71.6 0.5 fusion.14
  72.2 0.2 copy.283
  72.4 0.8 reshape.1556
  73.2 0.5 fusion.6
  73.8 7.9 %all-to-all-start.1 = ((f32[16,2,192]{2,1,0:T(2,128)}), f32[16,2,192]{2,1,0:T(2,128)S(1)}, u32[]{:S(2)}, u32[]{:S(2)}) async-start(f32[16,2,192]{2,1,0:T(2,128)} %reshape.1556), calls=%async_computation.1 | async-start | bytes 65536 | tf_op jit(solution)/shard_map/all_to_all | solution.py:192
  81.7 0.3 fusion.147
  82.0 1.1 %fusion.3 = f32[1,3,1,128,128]{4,3,2,1,0:T(8,128)} fusion(f32[32,3,8,128]{3,2,1,0:T(8,128)S(1)} %fusion.6, f32[1,1,128,128]{3,2,1,0:T(8,128)S(1)} %fusion.33, f32[1,1,128,128]{3,2,1,0:T(8,128)S(1)} %fusion.46, f32[1,1,128,128]{3,2,1,0:T(8,128)S(1)} %fusion.53, f32[128,128]{1,0:T(8,128)S(1)} %fusion.147, s32[32,8]{1,0:T(8,128)S(1)} %iota_add_fusion.1, ...), kind=kOutput, calls=%fused_computation.6 | convolution fusion | flops 151355392 | bytes 853024 | tf_op jit(solution)/shard_map/kar,kflac->flrc/dot_general | solution.py:215
  83.1 6.0 %all-to-all-done.1 = f32[16,2,192]{2,1,0:T(2,128)S(1)} async-done(((f32[16,2,192]{2,1,0:T(2,128)}), f32[16,2,192]{2,1,0:T(2,128)S(1)}, u32[]{:S(2)}, u32[]{:S(2)}) %all-to-all-start.1) | async-done | bytes 24608 | tf_op jit(solution)/shard_map/all_to_all | solution.py:192
  89.1 0.6 gather_fusion
  89.7 0.3 fusion.5
  90.0 0.8 reshape.1571
  (89 shorter events, 2.4 us)
Async XLA Ops:
  1.7 13.5 %copy-start.2 = (f32[1,1,16,3,1,576]{5,4,3,2,1,0:T(1,128)S(1)}, f32[1,1,16,3,1,576]{5,4,3,2,1,0:T(1,128)}, u32[]{:S(2)}) copy-start(f32[1,1,16,3,1,576]{5,4,3,2,1,0:T(1,128)} %param.9) | copy-start | bytes 331780
  2.0 41.4 %collective-permute-start = (f32[3,1,128]{2,1,0:T(1,128)S(1)}, f32[3,1,128]{2,1,0:T(1,128)S(1)}, u32[]{:S(2)}, u32[]{:S(2)}) collective-permute-start(f32[3,1,128]{2,1,0:T(1,128)S(1)} %get-tuple-element.68), channel_id=1, source_target_pairs={{0,1},{1,2},{2,3},{3,4},{4,5},{5,6},{6,7},{7,8},{8,9},{9,10},{10,1... | collective-permute-start | bytes 4616 | tf_op jit(solution)/shard_map/ppermute | solution.py:91
  6.6 36.9 %collective-permute-start.1 = (f32[3,1,128]{2,1,0:T(1,128)S(1)}, f32[3,1,128]{2,1,0:T(1,128)S(1)}, u32[]{:S(2)}, u32[]{:S(2)}) collective-permute-start(f32[3,1,128]{2,1,0:T(1,128)S(1)} %get-tuple-element.67), channel_id=1, source_target_pairs={{1,0},{2,1},{3,2},{4,3},{5,4},{6,5},{7,6},{8,7},{9,8},{10,9},{11,1... | collective-permute-start | bytes 4616 | tf_op jit(solution)/shard_map/ppermute | solution.py:92
  8.5 35.3 %collective-permute-start.2 = (f32[3,1,128]{2,1,0:T(1,128)S(1)}, f32[3,1,128]{2,1,0:T(1,128)S(1)}, u32[]{:S(2)}, u32[]{:S(2)}) collective-permute-start(f32[3,1,128]{2,1,0:T(1,128)S(1)} %get-tuple-element.65), channel_id=1, source_target_pairs={{0,16},{16,32},{32,48},{48,64},{64,80},{80,96},{96,112},{112,128},... | collective-permute-start | bytes 4616 | tf_op jit(solution)/shard_map/ppermute | solution.py:91
  13.3 30.6 %collective-permute-start.3 = (f32[3,1,128]{2,1,0:T(1,128)S(1)}, f32[3,1,128]{2,1,0:T(1,128)S(1)}, u32[]{:S(2)}, u32[]{:S(2)}) collective-permute-start(f32[3,1,128]{2,1,0:T(1,128)S(1)} %get-tuple-element.66), channel_id=1, source_target_pairs={{16,0},{32,16},{48,32},{64,48},{80,64},{96,80},{112,96},{128,112},... | collective-permute-start | bytes 4616 | tf_op jit(solution)/shard_map/ppermute | solution.py:92
  16.5 0.7 copy-start.4
  17.3 0.7 copy-start.5
  18.9 13.3 %copy-start.3 = (s32[1,4]{1,0:T(1,128)S(1)}, s32[1,4]{1,0:T(1,128)}, u32[]{:S(2)}) copy-start(s32[1,4]{1,0:T(1,128)} %param.8) | copy-start | bytes 52
  18.9 51.6 %all-to-all-start = ((f32[16,2,193]{2,1,0:T(2,128)}), f32[16,2,193]{2,1,0:T(2,128)S(1)}, u32[]{:S(2)}, u32[]{:S(2)}) async-start(f32[16,2,193]{2,1,0:T(2,128)} %reshape.1551), calls=%async_computation | async-start | bytes 65536 | tf_op jit(solution)/shard_map/all_to_all | solution.py:170
  44.8 0.8 copy-start.1
  46.0 0.9 %copy-start = (f32[1,3,1,128,128]{4,3,2,1,0:T(8,128)S(1)}, f32[1,3,1,128,128]{4,3,2,1,0:T(8,128)}, u32[]{:S(2)}) copy-start(f32[1,3,1,128,128]{4,3,2,1,0:T(8,128)} %param.6) | copy-start | bytes 589828
  47.6 14.8 %collective-permute-start.4 = (f32[3,1,128]{2,1,0:T(1,128)S(1)}, f32[3,1,128]{2,1,0:T(1,128)S(1)}, u32[]{:S(2)}, u32[]{:S(2)}) collective-permute-start(f32[3,1,128]{2,1,0:T(1,128)S(1)} %get-tuple-element.60), channel_id=1, source_target_pairs={{0,1},{1,2},{2,3},{3,4},{4,5},{5,6},{6,7},{7,8},{8,9},{9,10},{10,1... | collective-permute-start | bytes 4616 | tf_op jit(solution)/shard_map/ppermute | solution.py:91
  51.2 11.3 %collective-permute-start.5 = (f32[3,1,128]{2,1,0:T(1,128)S(1)}, f32[3,1,128]{2,1,0:T(1,128)S(1)}, u32[]{:S(2)}, u32[]{:S(2)}) collective-permute-start(f32[3,1,128]{2,1,0:T(1,128)S(1)} %get-tuple-element.59), channel_id=1, source_target_pairs={{1,0},{2,1},{3,2},{4,3},{5,4},{6,5},{7,6},{8,7},{9,8},{10,9},{11,1... | collective-permute-start | bytes 4616 | tf_op jit(solution)/shard_map/ppermute | solution.py:92
  53.1 9.8 %collective-permute-start.6 = (f32[3,1,128]{2,1,0:T(1,128)S(1)}, f32[3,1,128]{2,1,0:T(1,128)S(1)}, u32[]{:S(2)}, u32[]{:S(2)}) collective-permute-start(f32[3,1,128]{2,1,0:T(1,128)S(1)} %get-tuple-element.57), channel_id=1, source_target_pairs={{0,16},{16,32},{32,48},{48,64},{64,80},{80,96},{96,112},{112,128},... | collective-permute-start | bytes 4616 | tf_op jit(solution)/shard_map/ppermute | solution.py:91
  60.5 8.2 %collective-permute-start.7 = (f32[3,1,128]{2,1,0:T(1,128)S(1)}, f32[3,1,128]{2,1,0:T(1,128)S(1)}, u32[]{:S(2)}, u32[]{:S(2)}) collective-permute-start(f32[3,1,128]{2,1,0:T(1,128)S(1)} %get-tuple-element.58), channel_id=1, source_target_pairs={{16,0},{32,16},{48,32},{64,48},{80,64},{96,80},{112,96},{128,112},... | collective-permute-start | bytes 4616 | tf_op jit(solution)/shard_map/ppermute | solution.py:92
  73.8 15.3 %all-to-all-start.1 = ((f32[16,2,192]{2,1,0:T(2,128)}), f32[16,2,192]{2,1,0:T(2,128)S(1)}, u32[]{:S(2)}, u32[]{:S(2)}) async-start(f32[16,2,192]{2,1,0:T(2,128)} %reshape.1556), calls=%async_computation.1 | async-start | bytes 65536 | tf_op jit(solution)/shard_map/all_to_all | solution.py:192

commit v3 on v2

--- a/solution.py
+++ b/solution.py
@@ -95,23 +95,33 @@
     return low, high
 
 
-def edge_fix(strip, code, flag):
-    east_rot, north_rot = rotated(code, strip[1], strip[2])
-    turned = jnp.stack([strip[0], east_rot, north_rot], axis=0)
-    return jnp.where(flag, turned, strip)
-
-
-def substep(fields, coriolis, codes, flags, on_first_panel):
+def edge_turns(codes, flags):
+    along = (codes == 0).astype(jnp.float32) - (codes == 2).astype(jnp.float32)
+    across = (codes == 3).astype(jnp.float32) - (codes == 1).astype(jnp.float32)
+    crossing = jnp.stack(flags)
+    along = jnp.where(crossing, along, 1.0)
+    across = jnp.where(crossing, across, 0.0)
+    one = jnp.ones_like(along)
+    zero = jnp.zeros_like(along)
+    return jnp.stack(
+        [
+            jnp.stack([one, zero, zero], axis=1),
+            jnp.stack([zero, along, across], axis=1),
+            jnp.stack([zero, -across, along], axis=1),
+        ],
+        axis=1,
+    )
+
+
+def substep(fields, coriolis, turns, on_first_panel):
     first_rows = jnp.stack([f[:, 0, :] for f in fields], axis=0)
     last_rows = jnp.stack([f[:, -1, :] for f in fields], axis=0)
     first_cols = jnp.stack([f[:, :, 0] for f in fields], axis=0)
     last_cols = jnp.stack([f[:, :, -1] for f in fields], axis=0)
     west, east = ring_exchange(first_rows, last_rows, "gx", on_first_panel)
     south, north = ring_exchange(first_cols, last_cols, "gy", on_first_panel)
-    halos = [
-        edge_fix(strip, codes[side], flags[side])
-        for side, strip in enumerate((west, east, south, north))
-    ]
+    strips = jnp.stack([west, east, south, north], axis=0)
+    halos = jnp.einsum("sij,sjlc->silc", turns, strips, precision=HI)
     padded = [padded_field(fields[c], *(h[c] for h in halos)) for c in range(3)]
     return advance(padded[0], padded[1], padded[2], coriolis)
 
@@ -205,10 +215,11 @@
         my_row == 0,
         my_row == devices_y - 1,
     ]
+    turns = edge_turns(codes, flags)
     fields = (tile[0], tile[1], tile[2])
     cell_coriolis = coriolis[0][None]
     for sub in range(NSUB):
-        fields = substep(fields, cell_coriolis, codes, flags, on_first_panel)
+        fields = substep(fields, cell_coriolis, turns, on_first_panel)
 
     block_mean = asked_means + ALPHA * (picked - asked_means)
     spread_cols = jnp.einsum("kflab,kbc->kflac", block_mean, col_sel, precision=HI)

time: 91.5 us -> 82.4 us (0.901)
  between operations: 11.7 us -> 1.26 us
  starting transfers between devices: 49.1 us -> 52 us
  waiting for transfers between devices: 11.9 us -> 9.25 us
    all_to_all x1, starting transfers between devices: 7.89 us -> 10.7 us  [body(): lax.all_to_all(picked.reshape(devices_y, capacity, cells), 'gy', split_ax...]
    ppermute x4, waiting for transfers between devices: 5.85 us -> 3.25 us  [ring_exchange(): got_backward = lax.ppermute(sent_backward, ('panel', axis), backward)]
    unnamed x12 -> x14, local copies, waits for them, and re-layouts: 2.63 us -> 3.94 us
  transfers between devices with their start and end apart: 10 -> 10, of which waited for: 2 -> 3; matrix products, arithmetic and copies ran while one was open for 10% -> 12% of each run, Pallas kernels for 0% -> 0%
where the time goes in v3:
time: 82.4 us; the launch traced here: 81.8 us
  starting transfers between devices  52 us (63%)
  local copies, waits for them, and re-layouts  11.4 us (14%)
  waiting for transfers between devices  9.25 us (11%)
  other arithmetic  4.12 us (5%)
  matrix products  3.82 us (5%)
  between operations  1.26 us (2%)
    ppermute x4, starting transfers between devices, ring_exchange(): got_forward = lax.ppermute(sent_forward, ('panel', axis), forward)  20.7 us
    all_to_all x1, starting transfers between devices, body(): lax.all_to_all(outgoing.reshape(devices_y, capacity, cells + 1), 'gy', sp...  12.9 us
    all_to_all x1, starting transfers between devices, body(): lax.all_to_all(picked.reshape(devices_y, capacity, cells), 'gy', split_ax...  10.7 us
    ppermute x4, starting transfers between devices, ring_exchange(): got_backward = lax.ppermute(sent_backward, ('panel', axis), backward)  7.68 us
    all_to_all x1, waiting for transfers between devices, body(): lax.all_to_all(picked.reshape(devices_y, capacity, cells), 'gy', split_ax...  5.99 us
    unnamed x14, local copies, waits for them, and re-layouts  3.94 us
    ppermute x4, waiting for transfers between devices, ring_exchange(): got_backward = lax.ppermute(sent_backward, ('panel', axis), backward)  3.25 us
  transfers between devices with their start and end apart: 10, of which 3 were waited for; matrix products, arithmetic and copies ran while one was open for 12% of the time, Pallas kernels for 0%

profile of v3, /device:TPU:31, one launch (start us, length us, event | category | flops | bytes accessed | tf_op | source)
XLA Modules:
  0.0 81.8 jit_solution(11353242119907558383)
XLA Ops:
  0.6 0.9 %slice_bitcast_fusion.2 = (f32[1,128,128]{2,1,0:T(8,128)S(1)}, f32[1,128,128]{2,1,0:T(8,128)S(1)}, f32[1,128,128]{2,1,0:T(8,128)S(1)}) fusion(f32[1,3,1,128,128]{4,3,2,1,0:T(8,128)} %param.6), kind=kLoop, calls=%fused_computation.166 | loop fusion | bytes 393216 | tf_op jit(solution)/shard_map/squeeze | solution.py:219
  1.6 4.8 %collective-permute-start = (f32[3,1,128]{2,1,0:T(1,128)S(1)}, f32[3,1,128]{2,1,0:T(1,128)S(1)}, u32[]{:S(2)}, u32[]{:S(2)}) collective-permute-start(f32[3,1,128]{2,1,0:T(1,128)S(1)} %get-tuple-element.88), channel_id=1, source_target_pairs={{0,16},{16,32},{32,48},{48,64},{64,80},{80,96},{96,112},{112,128},... | collective-permute-start | bytes 4616 | tf_op jit(solution)/shard_map/ppermute | solution.py:91
  6.4 1.9 %collective-permute-start.1 = (f32[3,1,128]{2,1,0:T(1,128)S(1)}, f32[3,1,128]{2,1,0:T(1,128)S(1)}, u32[]{:S(2)}, u32[]{:S(2)}) collective-permute-start(f32[3,1,128]{2,1,0:T(1,128)S(1)} %get-tuple-element.89), channel_id=1, source_target_pairs={{16,0},{32,16},{48,32},{64,48},{80,64},{96,80},{112,96},{128,112},... | collective-permute-start | bytes 4616 | tf_op jit(solution)/shard_map/ppermute | solution.py:92
  8.3 0.2 slice_reduce_fusion.9
  8.5 0.2 slice_reduce_fusion.11
  8.7 4.8 %collective-permute-start.2 = (f32[3,1,128]{2,1,0:T(1,128)S(1)}, f32[3,1,128]{2,1,0:T(1,128)S(1)}, u32[]{:S(2)}, u32[]{:S(2)}) collective-permute-start(f32[3,1,128]{2,1,0:T(1,128)S(1)} %get-tuple-element.92), channel_id=1, source_target_pairs={{0,1},{1,2},{2,3},{3,4},{4,5},{5,6},{6,7},{7,8},{8,9},{9,10},{10,1... | collective-permute-start | bytes 4616 | tf_op jit(solution)/shard_map/ppermute | solution.py:91
  13.6 1.9 %collective-permute-start.3 = (f32[3,1,128]{2,1,0:T(1,128)S(1)}, f32[3,1,128]{2,1,0:T(1,128)S(1)}, u32[]{:S(2)}, u32[]{:S(2)}) collective-permute-start(f32[3,1,128]{2,1,0:T(1,128)S(1)} %get-tuple-element.93), channel_id=1, source_target_pairs={{1,0},{2,1},{3,2},{4,3},{5,4},{6,5},{7,6},{8,7},{9,8},{10,9},{11,1... | collective-permute-start | bytes 4616 | tf_op jit(solution)/shard_map/ppermute | solution.py:92
  15.5 0.3 reduce.12
  16.3 0.2 fusion.22
  16.5 0.2 convolution_multiply_fusion
  16.8 0.7 copy-done.3
  17.4 0.2 convert_reduce_fusion.2
  17.6 0.6 copy-done.5
  18.4 0.2 fusion.87
  18.6 0.6 reshape.1667
  19.2 12.9 %all-to-all-start = ((f32[16,2,193]{2,1,0:T(2,128)}), f32[16,2,193]{2,1,0:T(2,128)S(1)}, u32[]{:S(2)}, u32[]{:S(2)}) async-start(f32[16,2,193]{2,1,0:T(2,128)} %reshape.1667), calls=%async_computation | async-start | bytes 65536 | tf_op jit(solution)/shard_map/all_to_all | solution.py:180
  32.1 0.6 copy-done.4
  33.3 0.7 copy-done.6
  34.0 0.2 fusion.96
  34.4 0.1 copy.293
  34.6 0.1 copy.294
  34.8 0.1 copy.295
  35.0 0.1 copy.296
  35.2 0.1 copy.297
  35.4 0.2 maximum_multiply_fusion
  35.6 0.6 copy-done.1
  36.2 0.1 fusion.71
  36.3 0.2 maximum_multiply_fusion.1
  36.5 0.2 fusion.59
  36.8 0.7 copy-done
  37.5 0.1 fusion.77
  37.6 0.2 slice_reduce_fusion.5
  37.8 0.2 slice_reduce_fusion.4
  38.0 0.2 slice_reduce_fusion.3
  38.2 7.3 %collective-permute-start.4 = (f32[3,1,128]{2,1,0:T(1,128)S(1)}, f32[3,1,128]{2,1,0:T(1,128)S(1)}, u32[]{:S(2)}, u32[]{:S(2)}) collective-permute-start(f32[3,1,128]{2,1,0:T(1,128)S(1)} %get-tuple-element.80), channel_id=1, source_target_pairs={{0,16},{16,32},{32,48},{48,64},{64,80},{80,96},{96,112},{112,128},... | collective-permute-start | bytes 4616 | tf_op jit(solution)/shard_map/ppermute | solution.py:91
  45.5 1.9 %collective-permute-start.5 = (f32[3,1,128]{2,1,0:T(1,128)S(1)}, f32[3,1,128]{2,1,0:T(1,128)S(1)}, u32[]{:S(2)}, u32[]{:S(2)}) collective-permute-start(f32[3,1,128]{2,1,0:T(1,128)S(1)} %get-tuple-element.81), channel_id=1, source_target_pairs={{16,0},{32,16},{48,32},{64,48},{80,64},{96,80},{112,96},{128,112},... | collective-permute-start | bytes 4616 | tf_op jit(solution)/shard_map/ppermute | solution.py:92
  47.4 3.8 %collective-permute-start.6 = (f32[3,1,128]{2,1,0:T(1,128)S(1)}, f32[3,1,128]{2,1,0:T(1,128)S(1)}, u32[]{:S(2)}, u32[]{:S(2)}) collective-permute-start(f32[3,1,128]{2,1,0:T(1,128)S(1)} %get-tuple-element.84), channel_id=1, source_target_pairs={{0,1},{1,2},{2,3},{3,4},{4,5},{5,6},{6,7},{7,8},{8,9},{9,10},{10,1... | collective-permute-start | bytes 4616 | tf_op jit(solution)/shard_map/ppermute | solution.py:91
  51.2 1.9 %collective-permute-start.7 = (f32[3,1,128]{2,1,0:T(1,128)S(1)}, f32[3,1,128]{2,1,0:T(1,128)S(1)}, u32[]{:S(2)}, u32[]{:S(2)}) collective-permute-start(f32[3,1,128]{2,1,0:T(1,128)S(1)} %get-tuple-element.85), channel_id=1, source_target_pairs={{1,0},{2,1},{3,2},{4,3},{5,4},{6,5},{7,6},{8,7},{9,8},{10,9},{11,1... | collective-permute-start | bytes 4616 | tf_op jit(solution)/shard_map/ppermute | solution.py:92
  53.2 0.5 collective-permute-done.5
  53.7 2.7 %collective-permute-done.7 = f32[3,1,128]{2,1,0:T(1,128)S(1)} collective-permute-done((f32[3,1,128]{2,1,0:T(1,128)S(1)}, f32[3,1,128]{2,1,0:T(1,128)S(1)}, u32[]{:S(2)}, u32[]{:S(2)}) %collective-permute-start.7) | collective-permute-done | bytes 1568 | tf_op jit(solution)/shard_map/ppermute | solution.py:92
  56.4 0.2 fusion.93
  56.9 0.1 copy.307
  57.1 0.1 copy.308
  57.3 0.1 copy.309
  57.8 0.2 maximum_multiply_fusion.2
  58.0 0.1 fusion.46
  58.1 0.2 maximum_multiply_fusion.3
  58.3 0.2 fusion.33
  58.6 0.1 fusion.53
  58.7 0.1 fusion.86
  59.0 0.4 convolution_bitcast_fusion
  59.4 0.1 convert_reduce_fusion.1
  59.6 0.1 convert_reduce_fusion
  59.8 0.5 fusion.14
  60.4 0.2 copy.321
  60.6 0.8 %reshape.1672 = f32[16,2,192]{2,1,0:T(2,128)} reshape(f32[32,3,8,8]{3,2,1,0:T(8,128)S(1)} %fusion.14) | data formatting | bytes 49152 | tf_op jit(solution)/shard_map/reshape | solution.py:203
  61.4 0.5 fusion.6
  61.9 10.7 %all-to-all-start.1 = ((f32[16,2,192]{2,1,0:T(2,128)}), f32[16,2,192]{2,1,0:T(2,128)S(1)}, u32[]{:S(2)}, u32[]{:S(2)}) async-start(f32[16,2,192]{2,1,0:T(2,128)} %reshape.1672), calls=%async_computation.1 | async-start | bytes 65536 | tf_op jit(solution)/shard_map/all_to_all | solution.py:202
  72.7 0.3 fusion.162
  73.0 1.1 %fusion.3 = f32[1,3,1,128,128]{4,3,2,1,0:T(8,128)} fusion(f32[32,3,8,128]{3,2,1,0:T(8,128)S(1)} %fusion.6, f32[1,1,128,128]{3,2,1,0:T(8,128)S(1)} %fusion.33, f32[1,1,128,128]{3,2,1,0:T(8,128)S(1)} %fusion.46, f32[1,1,128,128]{3,2,1,0:T(8,128)S(1)} %fusion.53, f32[128,128]{1,0:T(8,128)S(1)} %fusion.162, s32[32,8]{1,0:T(8,128)S(1)} %iota_add_fusion.1, ...), kind=kOutput, calls=%fused_computation.6 | convolution fusion | flops 151355392 | bytes 853024 | tf_op jit(solution)/shard_map/kar,kflac->flrc/dot_general | solution.py:226
  74.1 6.0 %all-to-all-done.1 = f32[16,2,192]{2,1,0:T(2,128)S(1)} async-done(((f32[16,2,192]{2,1,0:T(2,128)}), f32[16,2,192]{2,1,0:T(2,128)S(1)}, u32[]{:S(2)}, u32[]{:S(2)}) %all-to-all-start.1) | async-done | bytes 24608 | tf_op jit(solution)/shard_map/all_to_all | solution.py:202
  80.1 0.6 gather_fusion
  80.8 0.3 fusion.5
  81.0 0.8 reshape.1687
  (78 shorter events, 3.0 us)
Async XLA Ops:
  1.6 31.6 %collective-permute-start = (f32[3,1,128]{2,1,0:T(1,128)S(1)}, f32[3,1,128]{2,1,0:T(1,128)S(1)}, u32[]{:S(2)}, u32[]{:S(2)}) collective-permute-start(f32[3,1,128]{2,1,0:T(1,128)S(1)} %get-tuple-element.88), channel_id=1, source_target_pairs={{0,16},{16,32},{32,48},{48,64},{64,80},{80,96},{96,112},{112,128},... | collective-permute-start | bytes 4616 | tf_op jit(solution)/shard_map/ppermute | solution.py:91
  6.4 26.9 %collective-permute-start.1 = (f32[3,1,128]{2,1,0:T(1,128)S(1)}, f32[3,1,128]{2,1,0:T(1,128)S(1)}, u32[]{:S(2)}, u32[]{:S(2)}) collective-permute-start(f32[3,1,128]{2,1,0:T(1,128)S(1)} %get-tuple-element.89), channel_id=1, source_target_pairs={{16,0},{32,16},{48,32},{64,48},{80,64},{96,80},{112,96},{128,112},... | collective-permute-start | bytes 4616 | tf_op jit(solution)/shard_map/ppermute | solution.py:92
  8.5 7.0 %copy-start.2 = (f32[1,1,16,3,1,576]{5,4,3,2,1,0:T(1,128)S(1)}, f32[1,1,16,3,1,576]{5,4,3,2,1,0:T(1,128)}, u32[]{:S(2)}) copy-start(f32[1,1,16,3,1,576]{5,4,3,2,1,0:T(1,128)} %param.9) | copy-start | bytes 331780
  8.7 24.6 %collective-permute-start.2 = (f32[3,1,128]{2,1,0:T(1,128)S(1)}, f32[3,1,128]{2,1,0:T(1,128)S(1)}, u32[]{:S(2)}, u32[]{:S(2)}) collective-permute-start(f32[3,1,128]{2,1,0:T(1,128)S(1)} %get-tuple-element.92), channel_id=1, source_target_pairs={{0,1},{1,2},{2,3},{3,4},{4,5},{5,6},{6,7},{7,8},{8,9},{9,10},{10,1... | collective-permute-start | bytes 4616 | tf_op jit(solution)/shard_map/ppermute | solution.py:91
  13.6 19.7 %collective-permute-start.3 = (f32[3,1,128]{2,1,0:T(1,128)S(1)}, f32[3,1,128]{2,1,0:T(1,128)S(1)}, u32[]{:S(2)}, u32[]{:S(2)}) collective-permute-start(f32[3,1,128]{2,1,0:T(1,128)S(1)} %get-tuple-element.93), channel_id=1, source_target_pairs={{1,0},{2,1},{3,2},{4,3},{5,4},{6,5},{7,6},{8,7},{9,8},{10,9},{11,1... | collective-permute-start | bytes 4616 | tf_op jit(solution)/shard_map/ppermute | solution.py:92
  16.8 0.7 copy-start.3
  17.6 0.7 copy-start.5
  19.2 39.5 %all-to-all-start = ((f32[16,2,193]{2,1,0:T(2,128)}), f32[16,2,193]{2,1,0:T(2,128)S(1)}, u32[]{:S(2)}, u32[]{:S(2)}) async-start(f32[16,2,193]{2,1,0:T(2,128)} %reshape.1667), calls=%async_computation | async-start | bytes 65536 | tf_op jit(solution)/shard_map/all_to_all | solution.py:180
  32.1 0.7 copy-start.4
  33.3 0.7 copy-start.6
  35.3 0.8 %copy-start.1 = (f32[1,128,128]{2,1,0:T(8,128)S(1)}, f32[1,128,128]{2,1,0:T(8,128)}, u32[]{:S(2)}) copy-start(f32[1,128,128]{2,1,0:T(8,128)} %param.7) | copy-start | bytes 196612
  36.5 0.9 %copy-start = (f32[1,3,1,128,128]{4,3,2,1,0:T(8,128)S(1)}, f32[1,3,1,128,128]{4,3,2,1,0:T(8,128)}, u32[]{:S(2)}) copy-start(f32[1,3,1,128,128]{4,3,2,1,0:T(8,128)} %param.6) | copy-start | bytes 589828
  38.2 15.0 %collective-permute-start.4 = (f32[3,1,128]{2,1,0:T(1,128)S(1)}, f32[3,1,128]{2,1,0:T(1,128)S(1)}, u32[]{:S(2)}, u32[]{:S(2)}) collective-permute-start(f32[3,1,128]{2,1,0:T(1,128)S(1)} %get-tuple-element.80), channel_id=1, source_target_pairs={{0,16},{16,32},{32,48},{48,64},{64,80},{80,96},{96,112},{112,128},... | collective-permute-start | bytes 4616 | tf_op jit(solution)/shard_map/ppermute | solution.py:91
  45.5 8.2 %collective-permute-start.5 = (f32[3,1,128]{2,1,0:T(1,128)S(1)}, f32[3,1,128]{2,1,0:T(1,128)S(1)}, u32[]{:S(2)}, u32[]{:S(2)}) collective-permute-start(f32[3,1,128]{2,1,0:T(1,128)S(1)} %get-tuple-element.81), channel_id=1, source_target_pairs={{16,0},{32,16},{48,32},{64,48},{80,64},{96,80},{112,96},{128,112},... | collective-permute-start | bytes 4616 | tf_op jit(solution)/shard_map/ppermute | solution.py:92
  47.4 6.3 %collective-permute-start.6 = (f32[3,1,128]{2,1,0:T(1,128)S(1)}, f32[3,1,128]{2,1,0:T(1,128)S(1)}, u32[]{:S(2)}, u32[]{:S(2)}) collective-permute-start(f32[3,1,128]{2,1,0:T(1,128)S(1)} %get-tuple-element.84), channel_id=1, source_target_pairs={{0,1},{1,2},{2,3},{3,4},{4,5},{5,6},{6,7},{7,8},{8,9},{9,10},{10,1... | collective-permute-start | bytes 4616 | tf_op jit(solution)/shard_map/ppermute | solution.py:91
  51.2 5.2 %collective-permute-start.7 = (f32[3,1,128]{2,1,0:T(1,128)S(1)}, f32[3,1,128]{2,1,0:T(1,128)S(1)}, u32[]{:S(2)}, u32[]{:S(2)}) collective-permute-start(f32[3,1,128]{2,1,0:T(1,128)S(1)} %get-tuple-element.85), channel_id=1, source_target_pairs={{1,0},{2,1},{3,2},{4,3},{5,4},{6,5},{7,6},{8,7},{9,8},{10,9},{11,1... | collective-permute-start | bytes 4616 | tf_op jit(solution)/shard_map/ppermute | solution.py:92
  61.9 18.1 %all-to-all-start.1 = ((f32[16,2,192]{2,1,0:T(2,128)}), f32[16,2,192]{2,1,0:T(2,128)S(1)}, u32[]{:S(2)}, u32[]{:S(2)}) async-start(f32[16,2,192]{2,1,0:T(2,128)} %reshape.1672), calls=%async_computation.1 | async-start | bytes 65536 | tf_op jit(solution)/shard_map/all_to_all | solution.py:202

commit v4 on v3

--- a/solution.py
+++ b/solution.py
@@ -18,16 +18,6 @@
 BETA = 0.5
 
 HI = lax.Precision.HIGHEST
-
-
-def shift_pairs(count, step):
-    return [(i, i + step) for i in range(count) if 0 <= i + step < count]
-
-
-def rotated(code, east_part, north_part):
-    along = (code == 0).astype(east_part.dtype) - (code == 2).astype(east_part.dtype)
-    across = (code == 3).astype(east_part.dtype) - (code == 1).astype(east_part.dtype)
-    return (along * east_part + across * north_part, along * north_part - across * east_part)
 
 
 def centre(field):
@@ -126,7 +116,7 @@
     return advance(padded[0], padded[1], padded[2], coriolis)
 
 
-def body(state, coriolis, edge_rotation, nest_block_state, parent_tile_index, parent_spot_index):
+def step(state, coriolis, edge_rotation, nest_block_state, parent_tile_index, parent_spot_index):
     devices_y = lax.axis_size("gy")
     slots = nest_block_state.shape[2]
     capacity = 2
@@ -200,7 +190,8 @@
     picked_rows = jnp.einsum("kar,flrc->kflac", row_sel, tile, precision=HI)
     picked = jnp.einsum("kflac,kbc->kflab", picked_rows, col_sel, precision=HI)
     incoming = lax.all_to_all(
-        picked.reshape(devices_y, capacity, cells), "gy", split_axis=0, concat_axis=0, tiled=True
+        picked.reshape(devices_y, capacity, cells), "gy", split_axis=0, concat_axis=0,
+        tiled=True,
     ).reshape(width, cells)
 
     parent = jnp.take(incoming, slot_of, axis=0)
@@ -218,7 +209,7 @@
     turns = edge_turns(codes, flags)
     fields = (tile[0], tile[1], tile[2])
     cell_coriolis = coriolis[0][None]
-    for sub in range(NSUB):
+    for _ in range(NSUB):
         fields = substep(fields, cell_coriolis, turns, on_first_panel)
 
     block_mean = asked_means + ALPHA * (picked - asked_means)
@@ -242,4 +233,4 @@
         P("panel", "gx", "gy"),
     )
     out_specs = (P("panel", None, None, "gx", "gy"), P("panel", "gx", "gy", None, None, None))
-    return jax.shard_map(body, mesh=mesh, in_specs=in_specs, out_specs=out_specs, check_vma=False)
+    return jax.shard_map(step, mesh=mesh, in_specs=in_specs, out_specs=out_specs, check_vma=False)

time: 82.4 us -> 82.4 us (level)
  no operation moved by 1% of the time
where the time goes in v4:
time: 82.4 us; the launch traced here: 81.8 us
  starting transfers between devices  52 us (63%)
  local copies, waits for them, and re-layouts  11.4 us (14%)
  waiting for transfers between devices  9.25 us (11%)
  other arithmetic  4.12 us (5%)
  matrix products  3.82 us (5%)
  between operations  1.26 us (2%)
    ppermute x4, starting transfers between devices, ring_exchange(): got_forward = lax.ppermute(sent_forward, ('panel', axis), forward)  20.7 us
    all_to_all x1, starting transfers between devices, step(): lax.all_to_all(outgoing.reshape(devices_y, capacity, cells + 1), 'gy', sp...  12.9 us
    all_to_all x1, starting transfers between devices, step(): lax.all_to_all(picked.reshape(devices_y, capacity, cells), 'gy', split_ax...  10.7 us
    ppermute x4, starting transfers between devices, ring_exchange(): got_backward = lax.ppermute(sent_backward, ('panel', axis), backward)  7.68 us
    all_to_all x1, waiting for transfers between devices, step(): lax.all_to_all(picked.reshape(devices_y, capacity, cells), 'gy', split_ax...  5.99 us
    unnamed x14, local copies, waits for them, and re-layouts  3.94 us
    ppermute x4, waiting for transfers between devices, ring_exchange(): got_backward = lax.ppermute(sent_backward, ('panel', axis), backward)  3.25 us
  transfers between devices with their start and end apart: 10, of which 3 were waited for; matrix products, arithmetic and copies ran while one was open for 12% of the time, Pallas kernels for 0%

profile of v4, /device:TPU:31, one launch (start us, length us, event | category | flops | bytes accessed | tf_op | source)
XLA Modules:
  0.0 81.8 jit_solution(11353242119907558383)
XLA Ops:
  0.6 0.9 %slice_bitcast_fusion.2 = (f32[1,128,128]{2,1,0:T(8,128)S(1)}, f32[1,128,128]{2,1,0:T(8,128)S(1)}, f32[1,128,128]{2,1,0:T(8,128)S(1)}) fusion(f32[1,3,1,128,128]{4,3,2,1,0:T(8,128)} %param.6), kind=kLoop, calls=%fused_computation.166 | loop fusion | bytes 393216 | tf_op jit(solution)/shard_map/squeeze | solution.py:210
  1.6 4.8 %collective-permute-start = (f32[3,1,128]{2,1,0:T(1,128)S(1)}, f32[3,1,128]{2,1,0:T(1,128)S(1)}, u32[]{:S(2)}, u32[]{:S(2)}) collective-permute-start(f32[3,1,128]{2,1,0:T(1,128)S(1)} %get-tuple-element.88), channel_id=1, source_target_pairs={{0,16},{16,32},{32,48},{48,64},{64,80},{80,96},{96,112},{112,128},... | collective-permute-start | bytes 4616 | tf_op jit(solution)/shard_map/ppermute | solution.py:81
  6.4 1.9 %collective-permute-start.1 = (f32[3,1,128]{2,1,0:T(1,128)S(1)}, f32[3,1,128]{2,1,0:T(1,128)S(1)}, u32[]{:S(2)}, u32[]{:S(2)}) collective-permute-start(f32[3,1,128]{2,1,0:T(1,128)S(1)} %get-tuple-element.89), channel_id=1, source_target_pairs={{16,0},{32,16},{48,32},{64,48},{80,64},{96,80},{112,96},{128,112},... | collective-permute-start | bytes 4616 | tf_op jit(solution)/shard_map/ppermute | solution.py:82
  8.3 0.2 slice_reduce_fusion.9
  8.5 0.2 slice_reduce_fusion.11
  8.7 4.8 %collective-permute-start.2 = (f32[3,1,128]{2,1,0:T(1,128)S(1)}, f32[3,1,128]{2,1,0:T(1,128)S(1)}, u32[]{:S(2)}, u32[]{:S(2)}) collective-permute-start(f32[3,1,128]{2,1,0:T(1,128)S(1)} %get-tuple-element.92), channel_id=1, source_target_pairs={{0,1},{1,2},{2,3},{3,4},{4,5},{5,6},{6,7},{7,8},{8,9},{9,10},{10,1... | collective-permute-start | bytes 4616 | tf_op jit(solution)/shard_map/ppermute | solution.py:81
  13.6 1.9 %collective-permute-start.3 = (f32[3,1,128]{2,1,0:T(1,128)S(1)}, f32[3,1,128]{2,1,0:T(1,128)S(1)}, u32[]{:S(2)}, u32[]{:S(2)}) collective-permute-start(f32[3,1,128]{2,1,0:T(1,128)S(1)} %get-tuple-element.93), channel_id=1, source_target_pairs={{1,0},{2,1},{3,2},{4,3},{5,4},{6,5},{7,6},{8,7},{9,8},{10,9},{11,1... | collective-permute-start | bytes 4616 | tf_op jit(solution)/shard_map/ppermute | solution.py:82
  15.5 0.3 reduce.12
  16.3 0.2 fusion.22
  16.5 0.2 convolution_multiply_fusion
  16.8 0.7 copy-done.3
  17.4 0.2 convert_reduce_fusion.2
  17.6 0.6 copy-done.5
  18.4 0.2 fusion.87
  18.6 0.6 reshape.1667
  19.2 12.9 %all-to-all-start = ((f32[16,2,193]{2,1,0:T(2,128)}), f32[16,2,193]{2,1,0:T(2,128)S(1)}, u32[]{:S(2)}, u32[]{:S(2)}) async-start(f32[16,2,193]{2,1,0:T(2,128)} %reshape.1667), calls=%async_computation | async-start | bytes 65536 | tf_op jit(solution)/shard_map/all_to_all | solution.py:170
  32.1 0.6 copy-done.4
  33.3 0.7 copy-done.6
  34.0 0.2 fusion.96
  34.4 0.1 copy.293
  34.6 0.1 copy.294
  34.8 0.1 copy.295
  35.0 0.1 copy.296
  35.2 0.1 copy.297
  35.4 0.2 maximum_multiply_fusion
  35.6 0.6 copy-done.1
  36.2 0.1 fusion.71
  36.3 0.2 maximum_multiply_fusion.1
  36.5 0.2 fusion.59
  36.8 0.7 copy-done
  37.5 0.1 fusion.77
  37.6 0.2 slice_reduce_fusion.5
  37.8 0.2 slice_reduce_fusion.4
  38.0 0.2 slice_reduce_fusion.3
  38.2 7.3 %collective-permute-start.4 = (f32[3,1,128]{2,1,0:T(1,128)S(1)}, f32[3,1,128]{2,1,0:T(1,128)S(1)}, u32[]{:S(2)}, u32[]{:S(2)}) collective-permute-start(f32[3,1,128]{2,1,0:T(1,128)S(1)} %get-tuple-element.80), channel_id=1, source_target_pairs={{0,16},{16,32},{32,48},{48,64},{64,80},{80,96},{96,112},{112,128},... | collective-permute-start | bytes 4616 | tf_op jit(solution)/shard_map/ppermute | solution.py:81
  45.5 1.9 %collective-permute-start.5 = (f32[3,1,128]{2,1,0:T(1,128)S(1)}, f32[3,1,128]{2,1,0:T(1,128)S(1)}, u32[]{:S(2)}, u32[]{:S(2)}) collective-permute-start(f32[3,1,128]{2,1,0:T(1,128)S(1)} %get-tuple-element.81), channel_id=1, source_target_pairs={{16,0},{32,16},{48,32},{64,48},{80,64},{96,80},{112,96},{128,112},... | collective-permute-start | bytes 4616 | tf_op jit(solution)/shard_map/ppermute | solution.py:82
  47.4 3.8 %collective-permute-start.6 = (f32[3,1,128]{2,1,0:T(1,128)S(1)}, f32[3,1,128]{2,1,0:T(1,128)S(1)}, u32[]{:S(2)}, u32[]{:S(2)}) collective-permute-start(f32[3,1,128]{2,1,0:T(1,128)S(1)} %get-tuple-element.84), channel_id=1, source_target_pairs={{0,1},{1,2},{2,3},{3,4},{4,5},{5,6},{6,7},{7,8},{8,9},{9,10},{10,1... | collective-permute-start | bytes 4616 | tf_op jit(solution)/shard_map/ppermute | solution.py:81
  51.2 1.9 %collective-permute-start.7 = (f32[3,1,128]{2,1,0:T(1,128)S(1)}, f32[3,1,128]{2,1,0:T(1,128)S(1)}, u32[]{:S(2)}, u32[]{:S(2)}) collective-permute-start(f32[3,1,128]{2,1,0:T(1,128)S(1)} %get-tuple-element.85), channel_id=1, source_target_pairs={{1,0},{2,1},{3,2},{4,3},{5,4},{6,5},{7,6},{8,7},{9,8},{10,9},{11,1... | collective-permute-start | bytes 4616 | tf_op jit(solution)/shard_map/ppermute | solution.py:82
  53.2 0.5 collective-permute-done.5
  53.7 2.7 %collective-permute-done.7 = f32[3,1,128]{2,1,0:T(1,128)S(1)} collective-permute-done((f32[3,1,128]{2,1,0:T(1,128)S(1)}, f32[3,1,128]{2,1,0:T(1,128)S(1)}, u32[]{:S(2)}, u32[]{:S(2)}) %collective-permute-start.7) | collective-permute-done | bytes 1568 | tf_op jit(solution)/shard_map/ppermute | solution.py:82
  56.4 0.2 fusion.93
  56.9 0.1 copy.307
  57.1 0.1 copy.308
  57.3 0.1 copy.309
  57.8 0.2 maximum_multiply_fusion.2
  58.0 0.1 fusion.46
  58.1 0.2 maximum_multiply_fusion.3
  58.3 0.2 fusion.33
  58.6 0.1 fusion.53
  58.7 0.1 fusion.86
  59.0 0.4 convolution_bitcast_fusion
  59.4 0.1 convert_reduce_fusion.1
  59.6 0.1 convert_reduce_fusion
  59.8 0.5 fusion.14
  60.4 0.2 copy.321
  60.6 0.8 %reshape.1672 = f32[16,2,192]{2,1,0:T(2,128)} reshape(f32[32,3,8,8]{3,2,1,0:T(8,128)S(1)} %fusion.14) | data formatting | bytes 49152 | tf_op jit(solution)/shard_map/reshape | solution.py:193
  61.4 0.5 fusion.6
  61.9 10.7 %all-to-all-start.1 = ((f32[16,2,192]{2,1,0:T(2,128)}), f32[16,2,192]{2,1,0:T(2,128)S(1)}, u32[]{:S(2)}, u32[]{:S(2)}) async-start(f32[16,2,192]{2,1,0:T(2,128)} %reshape.1672), calls=%async_computation.1 | async-start | bytes 65536 | tf_op jit(solution)/shard_map/all_to_all | solution.py:192
  72.7 0.3 fusion.162
  73.0 1.1 %fusion.3 = f32[1,3,1,128,128]{4,3,2,1,0:T(8,128)} fusion(f32[32,3,8,128]{3,2,1,0:T(8,128)S(1)} %fusion.6, f32[1,1,128,128]{3,2,1,0:T(8,128)S(1)} %fusion.33, f32[1,1,128,128]{3,2,1,0:T(8,128)S(1)} %fusion.46, f32[1,1,128,128]{3,2,1,0:T(8,128)S(1)} %fusion.53, f32[128,128]{1,0:T(8,128)S(1)} %fusion.162, s32[32,8]{1,0:T(8,128)S(1)} %iota_add_fusion.1, ...), kind=kOutput, calls=%fused_computation.6 | convolution fusion | flops 151355392 | bytes 853024 | tf_op jit(solution)/shard_map/kar,kflac->flrc/dot_general | solution.py:217
  74.1 6.0 %all-to-all-done.1 = f32[16,2,192]{2,1,0:T(2,128)S(1)} async-done(((f32[16,2,192]{2,1,0:T(2,128)}), f32[16,2,192]{2,1,0:T(2,128)S(1)}, u32[]{:S(2)}, u32[]{:S(2)}) %all-to-all-start.1) | async-done | bytes 24608 | tf_op jit(solution)/shard_map/all_to_all | solution.py:192
  80.1 0.6 gather_fusion
  80.8 0.3 fusion.5
  81.0 0.8 reshape.1687
  (78 shorter events, 3.0 us)
Async XLA Ops:
  1.6 31.6 %collective-permute-start = (f32[3,1,128]{2,1,0:T(1,128)S(1)}, f32[3,1,128]{2,1,0:T(1,128)S(1)}, u32[]{:S(2)}, u32[]{:S(2)}) collective-permute-start(f32[3,1,128]{2,1,0:T(1,128)S(1)} %get-tuple-element.88), channel_id=1, source_target_pairs={{0,16},{16,32},{32,48},{48,64},{64,80},{80,96},{96,112},{112,128},... | collective-permute-start | bytes 4616 | tf_op jit(solution)/shard_map/ppermute | solution.py:81
  6.4 26.9 %collective-permute-start.1 = (f32[3,1,128]{2,1,0:T(1,128)S(1)}, f32[3,1,128]{2,1,0:T(1,128)S(1)}, u32[]{:S(2)}, u32[]{:S(2)}) collective-permute-start(f32[3,1,128]{2,1,0:T(1,128)S(1)} %get-tuple-element.89), channel_id=1, source_target_pairs={{16,0},{32,16},{48,32},{64,48},{80,64},{96,80},{112,96},{128,112},... | collective-permute-start | bytes 4616 | tf_op jit(solution)/shard_map/ppermute | solution.py:82
  8.5 7.0 %copy-start.2 = (f32[1,1,16,3,1,576]{5,4,3,2,1,0:T(1,128)S(1)}, f32[1,1,16,3,1,576]{5,4,3,2,1,0:T(1,128)}, u32[]{:S(2)}) copy-start(f32[1,1,16,3,1,576]{5,4,3,2,1,0:T(1,128)} %param.9) | copy-start | bytes 331780
  8.7 24.6 %collective-permute-start.2 = (f32[3,1,128]{2,1,0:T(1,128)S(1)}, f32[3,1,128]{2,1,0:T(1,128)S(1)}, u32[]{:S(2)}, u32[]{:S(2)}) collective-permute-start(f32[3,1,128]{2,1,0:T(1,128)S(1)} %get-tuple-element.92), channel_id=1, source_target_pairs={{0,1},{1,2},{2,3},{3,4},{4,5},{5,6},{6,7},{7,8},{8,9},{9,10},{10,1... | collective-permute-start | bytes 4616 | tf_op jit(solution)/shard_map/ppermute | solution.py:81
  13.6 19.7 %collective-permute-start.3 = (f32[3,1,128]{2,1,0:T(1,128)S(1)}, f32[3,1,128]{2,1,0:T(1,128)S(1)}, u32[]{:S(2)}, u32[]{:S(2)}) collective-permute-start(f32[3,1,128]{2,1,0:T(1,128)S(1)} %get-tuple-element.93), channel_id=1, source_target_pairs={{1,0},{2,1},{3,2},{4,3},{5,4},{6,5},{7,6},{8,7},{9,8},{10,9},{11,1... | collective-permute-start | bytes 4616 | tf_op jit(solution)/shard_map/ppermute | solution.py:82
  16.8 0.7 copy-start.3
  17.6 0.7 copy-start.5
  19.2 39.5 %all-to-all-start = ((f32[16,2,193]{2,1,0:T(2,128)}), f32[16,2,193]{2,1,0:T(2,128)S(1)}, u32[]{:S(2)}, u32[]{:S(2)}) async-start(f32[16,2,193]{2,1,0:T(2,128)} %reshape.1667), calls=%async_computation | async-start | bytes 65536 | tf_op jit(solution)/shard_map/all_to_all | solution.py:170
  32.1 0.7 copy-start.4
  33.3 0.7 copy-start.6
  35.3 0.8 %copy-start.1 = (f32[1,128,128]{2,1,0:T(8,128)S(1)}, f32[1,128,128]{2,1,0:T(8,128)}, u32[]{:S(2)}) copy-start(f32[1,128,128]{2,1,0:T(8,128)} %param.7) | copy-start | bytes 196612
  36.5 0.9 %copy-start = (f32[1,3,1,128,128]{4,3,2,1,0:T(8,128)S(1)}, f32[1,3,1,128,128]{4,3,2,1,0:T(8,128)}, u32[]{:S(2)}) copy-start(f32[1,3,1,128,128]{4,3,2,1,0:T(8,128)} %param.6) | copy-start | bytes 589828
  38.2 15.0 %collective-permute-start.4 = (f32[3,1,128]{2,1,0:T(1,128)S(1)}, f32[3,1,128]{2,1,0:T(1,128)S(1)}, u32[]{:S(2)}, u32[]{:S(2)}) collective-permute-start(f32[3,1,128]{2,1,0:T(1,128)S(1)} %get-tuple-element.80), channel_id=1, source_target_pairs={{0,16},{16,32},{32,48},{48,64},{64,80},{80,96},{96,112},{112,128},... | collective-permute-start | bytes 4616 | tf_op jit(solution)/shard_map/ppermute | solution.py:81
  45.5 8.2 %collective-permute-start.5 = (f32[3,1,128]{2,1,0:T(1,128)S(1)}, f32[3,1,128]{2,1,0:T(1,128)S(1)}, u32[]{:S(2)}, u32[]{:S(2)}) collective-permute-start(f32[3,1,128]{2,1,0:T(1,128)S(1)} %get-tuple-element.81), channel_id=1, source_target_pairs={{16,0},{32,16},{48,32},{64,48},{80,64},{96,80},{112,96},{128,112},... | collective-permute-start | bytes 4616 | tf_op jit(solution)/shard_map/ppermute | solution.py:82
  47.4 6.3 %collective-permute-start.6 = (f32[3,1,128]{2,1,0:T(1,128)S(1)}, f32[3,1,128]{2,1,0:T(1,128)S(1)}, u32[]{:S(2)}, u32[]{:S(2)}) collective-permute-start(f32[3,1,128]{2,1,0:T(1,128)S(1)} %get-tuple-element.84), channel_id=1, source_target_pairs={{0,1},{1,2},{2,3},{3,4},{4,5},{5,6},{6,7},{7,8},{8,9},{9,10},{10,1... | collective-permute-start | bytes 4616 | tf_op jit(solution)/shard_map/ppermute | solution.py:81
  51.2 5.2 %collective-permute-start.7 = (f32[3,1,128]{2,1,0:T(1,128)S(1)}, f32[3,1,128]{2,1,0:T(1,128)S(1)}, u32[]{:S(2)}, u32[]{:S(2)}) collective-permute-start(f32[3,1,128]{2,1,0:T(1,128)S(1)} %get-tuple-element.85), channel_id=1, source_target_pairs={{1,0},{2,1},{3,2},{4,3},{5,4},{6,5},{7,6},{8,7},{9,8},{10,9},{11,1... | collective-permute-start | bytes 4616 | tf_op jit(solution)/shard_map/ppermute | solution.py:82
  61.9 18.1 %all-to-all-start.1 = ((f32[16,2,192]{2,1,0:T(2,128)}), f32[16,2,192]{2,1,0:T(2,128)S(1)}, u32[]{:S(2)}, u32[]{:S(2)}) async-start(f32[16,2,192]{2,1,0:T(2,128)} %reshape.1672), calls=%async_computation.1 | async-start | bytes 65536 | tf_op jit(solution)/shard_map/all_to_all | solution.py:192

commit v5 on v4

--- a/solution.py
+++ b/solution.py
@@ -20,6 +20,10 @@
 HI = lax.Precision.HIGHEST
 
 
+def shift_pairs(count, step):
+    return [(i, i + step) for i in range(count) if 0 <= i + step < count]
+
+
 def centre(field):
     return field[..., 1:-1, 1:-1]
 
@@ -64,33 +68,9 @@
     return jnp.concatenate([low, rows, high], axis=2)
 
 
-def ring_pairs(count):
-    pairs = [(g, g + 1) for g in range(count - 1)]
-    pairs.append((count - 1, 2 * count - 1))
-    pairs += [(count + g, count + g - 1) for g in range(1, count)]
-    pairs.append((count, 0))
-    return pairs
-
-
-def ring_exchange(first, last, axis, on_first_panel):
-    count = lax.axis_size(axis)
-    forward = ring_pairs(count)
-    backward = [(target, source) for source, target in forward]
-    sent_forward = jnp.where(on_first_panel, last, first)
-    sent_backward = jnp.where(on_first_panel, first, last)
-    got_forward = lax.ppermute(sent_forward, ("panel", axis), forward)
-    got_backward = lax.ppermute(sent_backward, ("panel", axis), backward)
-    low = jnp.where(on_first_panel, got_forward, got_backward)
-    high = jnp.where(on_first_panel, got_backward, got_forward)
-    return low, high
-
-
-def edge_turns(codes, flags):
+def edge_turns(codes):
     along = (codes == 0).astype(jnp.float32) - (codes == 2).astype(jnp.float32)
     across = (codes == 3).astype(jnp.float32) - (codes == 1).astype(jnp.float32)
-    crossing = jnp.stack(flags)
-    along = jnp.where(crossing, along, 1.0)
-    across = jnp.where(crossing, across, 0.0)
     one = jnp.ones_like(along)
     zero = jnp.zeros_like(along)
     return jnp.stack(
@@ -103,15 +83,24 @@
     )
 
 
-def substep(fields, coriolis, turns, on_first_panel):
+def substep(fields, coriolis, turns, flags):
+    nx = lax.axis_size("gx")
+    ny = lax.axis_size("gy")
     first_rows = jnp.stack([f[:, 0, :] for f in fields], axis=0)
     last_rows = jnp.stack([f[:, -1, :] for f in fields], axis=0)
     first_cols = jnp.stack([f[:, :, 0] for f in fields], axis=0)
     last_cols = jnp.stack([f[:, :, -1] for f in fields], axis=0)
-    west, east = ring_exchange(first_rows, last_rows, "gx", on_first_panel)
-    south, north = ring_exchange(first_cols, last_cols, "gy", on_first_panel)
-    strips = jnp.stack([west, east, south, north], axis=0)
-    halos = jnp.einsum("sij,sjlc->silc", turns, strips, precision=HI)
+    strips = jnp.stack([first_rows, last_rows, first_cols, last_cols], axis=0)
+    partner = lax.ppermute(strips, "panel", [(0, 1), (1, 0)])
+    from_west = lax.ppermute(last_rows, "gx", shift_pairs(nx, 1))
+    from_east = lax.ppermute(first_rows, "gx", shift_pairs(nx, -1))
+    from_south = lax.ppermute(last_cols, "gy", shift_pairs(ny, 1))
+    from_north = lax.ppermute(first_cols, "gy", shift_pairs(ny, -1))
+    turned = jnp.einsum("sij,sjlc->silc", turns, partner, precision=HI)
+    halos = [
+        jnp.where(flags[side], turned[side], neighbour)
+        for side, neighbour in enumerate((from_west, from_east, from_south, from_north))
+    ]
     padded = [padded_field(fields[c], *(h[c] for h in halos)) for c in range(3)]
     return advance(padded[0], padded[1], padded[2], coriolis)
 
@@ -123,7 +112,6 @@
     width = devices_y * capacity
     my_row = lax.axis_index("gy")
     my_column = lax.axis_index("gx")
-    on_first_panel = lax.axis_index("panel") == 0
     tile = state[0]
     level_stack = tile.shape[1]
     side_x = tile.shape[2]
@@ -206,11 +194,11 @@
         my_row == 0,
         my_row == devices_y - 1,
     ]
-    turns = edge_turns(codes, flags)
+    turns = edge_turns(codes)
     fields = (tile[0], tile[1], tile[2])
     cell_coriolis = coriolis[0][None]
     for _ in range(NSUB):
-        fields = substep(fields, cell_coriolis, turns, on_first_panel)
+        fields = substep(fields, cell_coriolis, turns, flags)
 
     block_mean = asked_means + ALPHA * (picked - asked_means)
     spread_cols = jnp.einsum("kflab,kbc->kflac", block_mean, col_sel, precision=HI)

time: 82.4 us -> 84.4 us (1.024)
  the two profiles are of different devices: /device:TPU:31 before, /device:TPU:5 now
where the time goes in v5:
time: 84.4 us; the launch traced here: 83.8 us
  starting transfers between devices  57.7 us (68%)
  local copies, waits for them, and re-layouts  10.5 us (12%)
  waiting for transfers between devices  6.06 us (7%)
  other arithmetic  4.18 us (5%)
  matrix products  3.82 us (5%)
  between operations  1.48 us (2%)
    ppermute x2, starting transfers between devices, substep(): from_east = lax.ppermute(first_rows, 'gx', shift_pairs(nx, -1))  11.7 us
    all_to_all x1, starting transfers between devices, step(): lax.all_to_all(outgoing.reshape(devices_y, capacity, cells + 1), 'gy', sp...  9.66 us
    ppermute x2, starting transfers between devices, substep(): partner = lax.ppermute(strips, 'panel', [(0, 1), (1, 0)])  9.37 us
    all_to_all x1, starting transfers between devices, step(): lax.all_to_all(picked.reshape(devices_y, capacity, cells), 'gy', split_ax...  9.27 us
    ppermute x2, starting transfers between devices, substep(): from_south = lax.ppermute(last_cols, 'gy', shift_pairs(ny, 1))  7.91 us
    all_to_all x1, waiting for transfers between devices, step(): lax.all_to_all(picked.reshape(devices_y, capacity, cells), 'gy', split_ax...  5.99 us
    ppermute x2, starting transfers between devices, substep(): from_north = lax.ppermute(first_cols, 'gy', shift_pairs(ny, -1))  5.53 us
    ppermute x2, starting transfers between devices, substep(): from_west = lax.ppermute(last_rows, 'gx', shift_pairs(nx, 1))  4.23 us
  transfers between devices with their start and end apart: 12, of which 1 were waited for; matrix products, arithmetic and copies ran while one was open for 11% of the time, Pallas kernels for 0%

profile of v5, /device:TPU:5, one launch (start us, length us, event | category | flops | bytes accessed | tf_op | source)
XLA Modules:
  0.0 83.8 jit_solution(3534484435076926619)
XLA Ops:
  0.6 0.9 %slice_bitcast_fusion.2 = (f32[1,128,128]{2,1,0:T(8,128)S(1)}, f32[1,128,128]{2,1,0:T(8,128)S(1)}, f32[1,128,128]{2,1,0:T(8,128)S(1)}) fusion(f32[1,3,1,128,128]{4,3,2,1,0:T(8,128)} %param.6), kind=kLoop, calls=%fused_computation.166 | loop fusion | bytes 393216 | tf_op jit(solution)/shard_map/squeeze | solution.py:198
  1.6 0.2 slice_reduce_fusion.9
  1.8 0.2 slice_reduce_fusion.11
  2.1 7.5 %collective-permute-start = (f32[4,3,1,128]{3,2,1,0:T(1,128)S(1)}, f32[4,3,1,128]{3,2,1,0:T(1,128)S(1)}, u32[]{:S(2)}, u32[]{:S(2)}) collective-permute-start(f32[4,3,1,128]{3,2,1,0:T(1,128)S(1)} %pad_maximum_fusion.50), channel_id=1, source_target_pairs={{0,256},{256,0},{1,257},{257,1},{2,258},{258,2},{3,259},{259,3},{4... | collective-permute-start | bytes 18440 | tf_op jit(solution)/shard_map/ppermute | solution.py:94
  9.5 2.3 %collective-permute-start.2 = (f32[3,1,128]{2,1,0:T(1,128)S(1)}, f32[3,1,128]{2,1,0:T(1,128)S(1)}, u32[]{:S(2)}, u32[]{:S(2)}) collective-permute-start(f32[3,1,128]{2,1,0:T(1,128)S(1)} %pad_maximum_fusion.55), channel_id=1, source_target_pairs={{0,16},{16,32},{32,48},{48,64},{64,80},{80,96},{96,112},{112,128},... | collective-permute-start | bytes 4616 | tf_op jit(solution)/shard_map/ppermute | solution.py:95
  11.9 5.7 %collective-permute-start.3 = (f32[3,1,128]{2,1,0:T(1,128)S(1)}, f32[3,1,128]{2,1,0:T(1,128)S(1)}, u32[]{:S(2)}, u32[]{:S(2)}) collective-permute-start(f32[3,1,128]{2,1,0:T(1,128)S(1)} %pad_maximum_fusion.54), channel_id=1, source_target_pairs={{16,0},{32,16},{48,32},{64,48},{80,64},{96,80},{112,96},{128,112},... | collective-permute-start | bytes 4616 | tf_op jit(solution)/shard_map/ppermute | solution.py:96
  17.6 3.4 %collective-permute-start.4 = (f32[3,1,128]{2,1,0:T(1,128)S(1)}, f32[3,1,128]{2,1,0:T(1,128)S(1)}, u32[]{:S(2)}, u32[]{:S(2)}) collective-permute-start(f32[3,1,128]{2,1,0:T(1,128)S(1)} %pad_maximum_fusion.56), channel_id=1, source_target_pairs={{1,0},{2,1},{3,2},{4,3},{5,4},{6,5},{7,6},{8,7},{9,8},{10,9},{11,1... | collective-permute-start | bytes 4616 | tf_op jit(solution)/shard_map/ppermute | solution.py:98
  21.0 3.9 %collective-permute-start.1 = (f32[3,1,128]{2,1,0:T(1,128)S(1)}, f32[3,1,128]{2,1,0:T(1,128)S(1)}, u32[]{:S(2)}, u32[]{:S(2)}) collective-permute-start(f32[3,1,128]{2,1,0:T(1,128)S(1)} %pad_maximum_fusion.57), channel_id=1, source_target_pairs={{0,1},{1,2},{2,3},{3,4},{4,5},{5,6},{6,7},{7,8},{8,9},{9,10},{10,1... | collective-permute-start | bytes 4616 | tf_op jit(solution)/shard_map/ppermute | solution.py:97
  24.9 0.3 reduce.12
  25.7 0.2 fusion.22
  25.9 0.2 convolution_multiply_fusion
  26.2 0.7 copy-done.3
  26.8 0.2 convert_reduce_fusion.2
  27.0 0.6 copy-done.4
  27.8 0.2 fusion.87
  28.0 0.6 reshape.777
  28.6 9.7 %all-to-all-start = ((f32[16,2,193]{2,1,0:T(2,128)}), f32[16,2,193]{2,1,0:T(2,128)S(1)}, u32[]{:S(2)}, u32[]{:S(2)}) async-start(f32[16,2,193]{2,1,0:T(2,128)} %reshape.777), calls=%async_computation | async-start | bytes 65536 | tf_op jit(solution)/shard_map/all_to_all | solution.py:158
  38.8 0.5 copy-done.6
  39.3 0.2 fusion.96
  39.8 0.1 copy.375
  40.1 0.1 copy.372
  40.3 0.1 copy.374
  40.5 0.1 copy.377
  40.6 0.1 copy.376
  40.8 0.2 maximum_multiply_fusion
  41.0 0.6 copy-done.1
  41.6 0.1 fusion.71
  41.7 0.2 maximum_multiply_fusion.1
  42.0 0.2 fusion.59
  42.2 0.7 copy-done
  42.9 0.1 fusion.77
  43.0 0.2 slice_reduce_fusion.5
  43.2 0.2 slice_reduce_fusion.4
  43.4 0.2 slice_reduce_fusion.3
  43.7 1.9 %collective-permute-start.5 = (f32[4,3,1,128]{3,2,1,0:T(1,128)S(1)}, f32[4,3,1,128]{3,2,1,0:T(1,128)S(1)}, u32[]{:S(2)}, u32[]{:S(2)}) collective-permute-start(f32[4,3,1,128]{3,2,1,0:T(1,128)S(1)} %pad_maximum_fusion.51), channel_id=1, source_target_pairs={{0,256},{256,0},{1,257},{257,1},{2,258},{258,2},{3,259},{259,3},{4... | collective-permute-start | bytes 18440 | tf_op jit(solution)/shard_map/ppermute | solution.py:94
  45.6 2.1 %collective-permute-start.9 = (f32[3,1,128]{2,1,0:T(1,128)S(1)}, f32[3,1,128]{2,1,0:T(1,128)S(1)}, u32[]{:S(2)}, u32[]{:S(2)}) collective-permute-start(f32[3,1,128]{2,1,0:T(1,128)S(1)} %pad_maximum_fusion.60), channel_id=1, source_target_pairs={{1,0},{2,1},{3,2},{4,3},{5,4},{6,5},{7,6},{8,7},{9,8},{10,9},{11,1... | collective-permute-start | bytes 4616 | tf_op jit(solution)/shard_map/ppermute | solution.py:98
  47.8 1.9 %collective-permute-start.7 = (f32[3,1,128]{2,1,0:T(1,128)S(1)}, f32[3,1,128]{2,1,0:T(1,128)S(1)}, u32[]{:S(2)}, u32[]{:S(2)}) collective-permute-start(f32[3,1,128]{2,1,0:T(1,128)S(1)} %pad_maximum_fusion.59), channel_id=1, source_target_pairs={{0,16},{16,32},{32,48},{48,64},{64,80},{80,96},{96,112},{112,128},... | collective-permute-start | bytes 4616 | tf_op jit(solution)/shard_map/ppermute | solution.py:95
  49.7 6.1 %collective-permute-start.8 = (f32[3,1,128]{2,1,0:T(1,128)S(1)}, f32[3,1,128]{2,1,0:T(1,128)S(1)}, u32[]{:S(2)}, u32[]{:S(2)}) collective-permute-start(f32[3,1,128]{2,1,0:T(1,128)S(1)} %pad_maximum_fusion.58), channel_id=1, source_target_pairs={{16,0},{32,16},{48,32},{64,48},{80,64},{96,80},{112,96},{128,112},... | collective-permute-start | bytes 4616 | tf_op jit(solution)/shard_map/ppermute | solution.py:96
  55.7 4.0 %collective-permute-start.6 = (f32[3,1,128]{2,1,0:T(1,128)S(1)}, f32[3,1,128]{2,1,0:T(1,128)S(1)}, u32[]{:S(2)}, u32[]{:S(2)}) collective-permute-start(f32[3,1,128]{2,1,0:T(1,128)S(1)} %pad_maximum_fusion.61), channel_id=1, source_target_pairs={{0,1},{1,2},{2,3},{3,4},{4,5},{5,6},{6,7},{7,8},{8,9},{9,10},{10,1... | collective-permute-start | bytes 4616 | tf_op jit(solution)/shard_map/ppermute | solution.py:97
  59.8 0.2 fusion.93
  60.3 0.1 copy.393
  60.8 0.1 copy.392
  60.9 0.1 copy.395
  61.1 0.1 copy.394
  61.3 0.2 maximum_multiply_fusion.2
  61.5 0.1 fusion.46
  61.6 0.2 maximum_multiply_fusion.3
  61.8 0.2 fusion.33
  62.0 0.1 fusion.53
  62.2 0.1 fusion.86
  62.5 0.4 convolution_bitcast_fusion
  62.9 0.1 convert_reduce_fusion.1
  63.1 0.1 convert_reduce_fusion
  63.2 0.5 fusion.14
  63.9 0.2 copy.405
  64.1 0.8 reshape.782
  64.9 0.5 fusion.6
  65.4 9.3 %all-to-all-start.1 = ((f32[16,2,192]{2,1,0:T(2,128)}), f32[16,2,192]{2,1,0:T(2,128)S(1)}, u32[]{:S(2)}, u32[]{:S(2)}) async-start(f32[16,2,192]{2,1,0:T(2,128)} %reshape.782), calls=%async_computation.1 | async-start | bytes 65536 | tf_op jit(solution)/shard_map/all_to_all | solution.py:180
  74.7 0.3 fusion.153
  75.0 1.1 %fusion.3 = f32[1,3,1,128,128]{4,3,2,1,0:T(8,128)} fusion(f32[32,3,8,128]{3,2,1,0:T(8,128)S(1)} %fusion.6, f32[1,1,128,128]{3,2,1,0:T(8,128)S(1)} %fusion.33, f32[1,1,128,128]{3,2,1,0:T(8,128)S(1)} %fusion.46, f32[1,1,128,128]{3,2,1,0:T(8,128)S(1)} %fusion.53, f32[128,128]{1,0:T(8,128)S(1)} %fusion.153, s32[32,8]{1,0:T(8,128)S(1)} %iota_add_fusion.1, ...), kind=kOutput, calls=%fused_computation.6 | convolution fusion | flops 151355392 | bytes 853024 | tf_op jit(solution)/shard_map/kar,kflac->flrc/dot_general | solution.py:205
  76.1 6.0 %all-to-all-done.1 = f32[16,2,192]{2,1,0:T(2,128)S(1)} async-done(((f32[16,2,192]{2,1,0:T(2,128)}), f32[16,2,192]{2,1,0:T(2,128)S(1)}, u32[]{:S(2)}, u32[]{:S(2)}) %all-to-all-start.1) | async-done | bytes 24608 | tf_op jit(solution)/shard_map/all_to_all | solution.py:180
  82.1 0.6 gather_fusion
  82.8 0.3 fusion.5
  83.0 0.8 reshape.797
  (106 shorter events, 3.0 us)
Async XLA Ops:
  1.8 23.1 %copy-start.2 = (f32[1,1,16,3,1,576]{5,4,3,2,1,0:T(1,128)S(1)}, f32[1,1,16,3,1,576]{5,4,3,2,1,0:T(1,128)}, u32[]{:S(2)}) copy-start(f32[1,1,16,3,1,576]{5,4,3,2,1,0:T(1,128)} %param.9) | copy-start | bytes 331780
  2.1 36.7 %collective-permute-start = (f32[4,3,1,128]{3,2,1,0:T(1,128)S(1)}, f32[4,3,1,128]{3,2,1,0:T(1,128)S(1)}, u32[]{:S(2)}, u32[]{:S(2)}) collective-permute-start(f32[4,3,1,128]{3,2,1,0:T(1,128)S(1)} %pad_maximum_fusion.50), channel_id=1, source_target_pairs={{0,256},{256,0},{1,257},{257,1},{2,258},{258,2},{3,259},{259,3},{4... | collective-permute-start | bytes 18440 | tf_op jit(solution)/shard_map/ppermute | solution.py:94
  9.5 29.9 %collective-permute-start.2 = (f32[3,1,128]{2,1,0:T(1,128)S(1)}, f32[3,1,128]{2,1,0:T(1,128)S(1)}, u32[]{:S(2)}, u32[]{:S(2)}) collective-permute-start(f32[3,1,128]{2,1,0:T(1,128)S(1)} %pad_maximum_fusion.55), channel_id=1, source_target_pairs={{0,16},{16,32},{32,48},{48,64},{64,80},{80,96},{96,112},{112,128},... | collective-permute-start | bytes 4616 | tf_op jit(solution)/shard_map/ppermute | solution.py:95
  11.9 27.7 %collective-permute-start.3 = (f32[3,1,128]{2,1,0:T(1,128)S(1)}, f32[3,1,128]{2,1,0:T(1,128)S(1)}, u32[]{:S(2)}, u32[]{:S(2)}) collective-permute-start(f32[3,1,128]{2,1,0:T(1,128)S(1)} %pad_maximum_fusion.54), channel_id=1, source_target_pairs={{16,0},{32,16},{48,32},{64,48},{80,64},{96,80},{112,96},{128,112},... | collective-permute-start | bytes 4616 | tf_op jit(solution)/shard_map/ppermute | solution.py:96
  17.6 22.0 %collective-permute-start.4 = (f32[3,1,128]{2,1,0:T(1,128)S(1)}, f32[3,1,128]{2,1,0:T(1,128)S(1)}, u32[]{:S(2)}, u32[]{:S(2)}) collective-permute-start(f32[3,1,128]{2,1,0:T(1,128)S(1)} %pad_maximum_fusion.56), channel_id=1, source_target_pairs={{1,0},{2,1},{3,2},{4,3},{5,4},{6,5},{7,6},{8,7},{9,8},{10,9},{11,1... | collective-permute-start | bytes 4616 | tf_op jit(solution)/shard_map/ppermute | solution.py:98
  21.0 19.0 %collective-permute-start.1 = (f32[3,1,128]{2,1,0:T(1,128)S(1)}, f32[3,1,128]{2,1,0:T(1,128)S(1)}, u32[]{:S(2)}, u32[]{:S(2)}) collective-permute-start(f32[3,1,128]{2,1,0:T(1,128)S(1)} %pad_maximum_fusion.57), channel_id=1, source_target_pairs={{0,1},{1,2},{2,3},{3,4},{4,5},{5,6},{6,7},{7,8},{8,9},{9,10},{10,1... | collective-permute-start | bytes 4616 | tf_op jit(solution)/shard_map/ppermute | solution.py:97
  26.2 0.7 copy-start.3
  27.0 0.7 copy-start.4
  28.6 9.7 %copy-start.5 = (s32[1,4]{1,0:T(1,128)S(1)}, s32[1,4]{1,0:T(1,128)}, u32[]{:S(2)}) copy-start(s32[1,4]{1,0:T(1,128)} %param.8) | copy-start | bytes 52
  28.6 33.5 %all-to-all-start = ((f32[16,2,193]{2,1,0:T(2,128)}), f32[16,2,193]{2,1,0:T(2,128)S(1)}, u32[]{:S(2)}, u32[]{:S(2)}) async-start(f32[16,2,193]{2,1,0:T(2,128)} %reshape.777), calls=%async_computation | async-start | bytes 65536 | tf_op jit(solution)/shard_map/all_to_all | solution.py:158
  38.6 0.7 copy-start.6
  40.8 0.8 %copy-start.1 = (f32[1,128,128]{2,1,0:T(8,128)S(1)}, f32[1,128,128]{2,1,0:T(8,128)}, u32[]{:S(2)}) copy-start(f32[1,128,128]{2,1,0:T(8,128)} %param.7) | copy-start | bytes 196612
  41.9 0.9 %copy-start = (f32[1,3,1,128,128]{4,3,2,1,0:T(8,128)S(1)}, f32[1,3,1,128,128]{4,3,2,1,0:T(8,128)}, u32[]{:S(2)}) copy-start(f32[1,3,1,128,128]{4,3,2,1,0:T(8,128)} %param.6) | copy-start | bytes 589828
  43.7 16.1 %collective-permute-start.5 = (f32[4,3,1,128]{3,2,1,0:T(1,128)S(1)}, f32[4,3,1,128]{3,2,1,0:T(1,128)S(1)}, u32[]{:S(2)}, u32[]{:S(2)}) collective-permute-start(f32[4,3,1,128]{3,2,1,0:T(1,128)S(1)} %pad_maximum_fusion.51), channel_id=1, source_target_pairs={{0,256},{256,0},{1,257},{257,1},{2,258},{258,2},{3,259},{259,3},{4... | collective-permute-start | bytes 18440 | tf_op jit(solution)/shard_map/ppermute | solution.py:94
  45.6 14.3 %collective-permute-start.9 = (f32[3,1,128]{2,1,0:T(1,128)S(1)}, f32[3,1,128]{2,1,0:T(1,128)S(1)}, u32[]{:S(2)}, u32[]{:S(2)}) collective-permute-start(f32[3,1,128]{2,1,0:T(1,128)S(1)} %pad_maximum_fusion.60), channel_id=1, source_target_pairs={{1,0},{2,1},{3,2},{4,3},{5,4},{6,5},{7,6},{8,7},{9,8},{10,9},{11,1... | collective-permute-start | bytes 4616 | tf_op jit(solution)/shard_map/ppermute | solution.py:98
  47.8 12.2 %collective-permute-start.7 = (f32[3,1,128]{2,1,0:T(1,128)S(1)}, f32[3,1,128]{2,1,0:T(1,128)S(1)}, u32[]{:S(2)}, u32[]{:S(2)}) collective-permute-start(f32[3,1,128]{2,1,0:T(1,128)S(1)} %pad_maximum_fusion.59), channel_id=1, source_target_pairs={{0,16},{16,32},{32,48},{48,64},{64,80},{80,96},{96,112},{112,128},... | collective-permute-start | bytes 4616 | tf_op jit(solution)/shard_map/ppermute | solution.py:95
  49.7 10.4 %collective-permute-start.8 = (f32[3,1,128]{2,1,0:T(1,128)S(1)}, f32[3,1,128]{2,1,0:T(1,128)S(1)}, u32[]{:S(2)}, u32[]{:S(2)}) collective-permute-start(f32[3,1,128]{2,1,0:T(1,128)S(1)} %pad_maximum_fusion.58), channel_id=1, source_target_pairs={{16,0},{32,16},{48,32},{64,48},{80,64},{96,80},{112,96},{128,112},... | collective-permute-start | bytes 4616 | tf_op jit(solution)/shard_map/ppermute | solution.py:96
  55.7 4.7 %collective-permute-start.6 = (f32[3,1,128]{2,1,0:T(1,128)S(1)}, f32[3,1,128]{2,1,0:T(1,128)S(1)}, u32[]{:S(2)}, u32[]{:S(2)}) collective-permute-start(f32[3,1,128]{2,1,0:T(1,128)S(1)} %pad_maximum_fusion.61), channel_id=1, source_target_pairs={{0,1},{1,2},{2,3},{3,4},{4,5},{5,6},{6,7},{7,8},{8,9},{9,10},{10,1... | collective-permute-start | bytes 4616 | tf_op jit(solution)/shard_map/ppermute | solution.py:97
  65.4 16.7 %all-to-all-start.1 = ((f32[16,2,192]{2,1,0:T(2,128)}), f32[16,2,192]{2,1,0:T(2,128)S(1)}, u32[]{:S(2)}, u32[]{:S(2)}) async-start(f32[16,2,192]{2,1,0:T(2,128)} %reshape.782), calls=%async_computation.1 | async-start | bytes 65536 | tf_op jit(solution)/shard_map/all_to_all | solution.py:180

commit v6 on v5

--- a/solution.py
+++ b/solution.py
@@ -3,7 +3,6 @@
 from jax import lax
 from jax.sharding import PartitionSpec as P
 
-NSUB = 2
 PATCH = 8
 RATIO = 3
 FINE = 24
@@ -83,19 +82,38 @@
     )
 
 
-def substep(fields, coriolis, turns, flags):
-    nx = lax.axis_size("gx")
-    ny = lax.axis_size("gy")
+def edge_strips(fields):
     first_rows = jnp.stack([f[:, 0, :] for f in fields], axis=0)
     last_rows = jnp.stack([f[:, -1, :] for f in fields], axis=0)
     first_cols = jnp.stack([f[:, :, 0] for f in fields], axis=0)
     last_cols = jnp.stack([f[:, :, -1] for f in fields], axis=0)
-    strips = jnp.stack([first_rows, last_rows, first_cols, last_cols], axis=0)
-    partner = lax.ppermute(strips, "panel", [(0, 1), (1, 0)])
+    return first_rows, last_rows, first_cols, last_cols
+
+
+def column_halos(first_cols, last_cols):
+    count = lax.axis_size("gy")
+    here = lax.axis_index("gy")
+    target = jnp.arange(count, dtype=jnp.int32)
+    to_next = (target == here + 1)[:, None, None, None]
+    to_prev = (target == here - 1)[:, None, None, None]
+    return jnp.where(to_next, last_cols[None], jnp.where(to_prev, first_cols[None], 0.0))
+
+
+def received_columns(got):
+    count = lax.axis_size("gy")
+    here = lax.axis_index("gy")
+    south = lax.dynamic_index_in_dim(got, jnp.maximum(here - 1, 0), axis=0, keepdims=False)
+    north = lax.dynamic_index_in_dim(got, jnp.minimum(here + 1, count - 1), axis=0, keepdims=False)
+    return south, north
+
+
+def substep(fields, strips, from_south, from_north, coriolis, turns, flags):
+    nx = lax.axis_size("gx")
+    first_rows, last_rows, first_cols, last_cols = strips
+    edges = jnp.stack([first_rows, last_rows, first_cols, last_cols], axis=0)
+    partner = lax.ppermute(edges, "panel", [(0, 1), (1, 0)])
     from_west = lax.ppermute(last_rows, "gx", shift_pairs(nx, 1))
     from_east = lax.ppermute(first_rows, "gx", shift_pairs(nx, -1))
-    from_south = lax.ppermute(last_cols, "gy", shift_pairs(ny, 1))
-    from_north = lax.ppermute(first_cols, "gy", shift_pairs(ny, -1))
     turned = jnp.einsum("sij,sjlc->silc", turns, partner, precision=HI)
     halos = [
         jnp.where(flags[side], turned[side], neighbour)
@@ -155,10 +173,15 @@
         [(spots + 1).astype(jnp.float32)[:, None], smooth_means], axis=1
     )
     outgoing = jnp.dot(slot_hit, payload, precision=HI)
-    asked_payload = lax.all_to_all(
-        outgoing.reshape(devices_y, capacity, cells + 1), "gy", split_axis=0, concat_axis=0,
-        tiled=True,
-    ).reshape(width, cells + 1)
+    strips0 = edge_strips((tile[0], tile[1], tile[2]))
+    columns0 = column_halos(strips0[2], strips0[3])
+    ask_out = jnp.concatenate(
+        [outgoing.reshape(devices_y, capacity * (cells + 1)), columns0.reshape(devices_y, -1)],
+        axis=1,
+    )
+    ask_in = lax.all_to_all(ask_out, "gy", split_axis=0, concat_axis=0, tiled=True)
+    asked_payload = ask_in[:, : capacity * (cells + 1)].reshape(width, cells + 1)
+    got0 = ask_in[:, capacity * (cells + 1) :].reshape(columns0.shape)
     asked = asked_payload[:, 0].astype(jnp.int32) - 1
     asked_means = asked_payload[:, 1:].reshape(width, 3, level_stack, PATCH, PATCH)
 
@@ -177,16 +200,6 @@
     )
     picked_rows = jnp.einsum("kar,flrc->kflac", row_sel, tile, precision=HI)
     picked = jnp.einsum("kflac,kbc->kflab", picked_rows, col_sel, precision=HI)
-    incoming = lax.all_to_all(
-        picked.reshape(devices_y, capacity, cells), "gy", split_axis=0, concat_axis=0,
-        tiled=True,
-    ).reshape(width, cells)
-
-    parent = jnp.take(incoming, slot_of, axis=0)
-    coarse = parent.reshape(slots * 3 * level_stack, coarse_cells)
-    upsampled = jnp.dot(coarse, spread, precision=HI)
-    blended = smoothed + ALPHA * (upsampled - smoothed)
-
     codes = edge_rotation[0]
     flags = [
         my_column == 0,
@@ -195,10 +208,26 @@
         my_row == devices_y - 1,
     ]
     turns = edge_turns(codes)
-    fields = (tile[0], tile[1], tile[2])
     cell_coriolis = coriolis[0][None]
-    for _ in range(NSUB):
-        fields = substep(fields, cell_coriolis, turns, flags)
+    south0, north0 = received_columns(got0)
+    fields = substep(
+        (tile[0], tile[1], tile[2]), strips0, south0, north0, cell_coriolis, turns, flags
+    )
+    strips1 = edge_strips(fields)
+    columns1 = column_halos(strips1[2], strips1[3])
+    answer_out = jnp.concatenate(
+        [picked.reshape(devices_y, capacity * cells), columns1.reshape(devices_y, -1)], axis=1
+    )
+    answer_in = lax.all_to_all(answer_out, "gy", split_axis=0, concat_axis=0, tiled=True)
+    incoming = answer_in[:, : capacity * cells].reshape(width, cells)
+    got1 = answer_in[:, capacity * cells :].reshape(columns1.shape)
+    south1, north1 = received_columns(got1)
+    fields = substep(fields, strips1, south1, north1, cell_coriolis, turns, flags)
+
+    parent = jnp.take(incoming, slot_of, axis=0)
+    coarse = parent.reshape(slots * 3 * level_stack, coarse_cells)
+    upsampled = jnp.dot(coarse, spread, precision=HI)
+    blended = smoothed + ALPHA * (upsampled - smoothed)
 
     block_mean = asked_means + ALPHA * (picked - asked_means)
     spread_cols = jnp.einsum("kflab,kbc->kflac", block_mean, col_sel, precision=HI)

time: 84.4 us -> 70.1 us (0.83)
  the two profiles are of different devices: /device:TPU:5 before, /device:TPU:58 now
where the time goes in v6:
time: 70.1 us; the launch traced here: 69.6 us
  starting transfers between devices  41.8 us (60%)
  local copies, waits for them, and re-layouts  10.3 us (15%)
  waiting for transfers between devices  6.99 us (10%)
  other arithmetic  5.3 us (8%)
  matrix products  3.82 us (5%)
  between operations  1.4 us (2%)
    ppermute x2, starting transfers between devices, substep(): partner = lax.ppermute(edges, 'panel', [(0, 1), (1, 0)])  12.4 us
    all_to_all x1, starting transfers between devices, step(): lax.all_to_all(ask_out, 'gy', split_axis=0, concat_axis=0, tiled=True)  10.4 us
    all_to_all x1, starting transfers between devices, step(): lax.all_to_all(answer_out, 'gy', split_axis=0, concat_axis=0, tiled=True)  7.21 us
    ppermute x2, waiting for transfers between devices, substep(): from_east = lax.ppermute(first_rows, 'gx', shift_pairs(nx, -1))  6.97 us
    ppermute x2, starting transfers between devices, substep(): from_east = lax.ppermute(first_rows, 'gx', shift_pairs(nx, -1))  6.71 us
    ppermute x2, starting transfers between devices, substep(): from_west = lax.ppermute(last_rows, 'gx', shift_pairs(nx, 1))  4.98 us
    unnamed x14, local copies, waits for them, and re-layouts  3.25 us
  transfers between devices with their start and end apart: 8, of which 2 were waited for; matrix products, arithmetic and copies ran while one was open for 3% of the time, Pallas kernels for 0%

profile of v6, /device:TPU:58, one launch (start us, length us, event | category | flops | bytes accessed | tf_op | source)
XLA Modules:
  0.0 69.6 jit_solution(11391117732265250342)
XLA Ops:
  0.6 1.2 %reduce.6 = f32[16,3,576]{2,1,0:T(4,128)S(1)} reduce(f32[1,1,16,3,1,576]{5,4,3,2,1,0:T(1,128)} %param.9, f32[]{:T(128)} %constant.140), dimensions={0,1,4}, to_apply=%param.9.reduce_sub_computation | reduce | bytes 221188 | tf_op args[3]
  2.4 0.7 %copy-done = f32[1,3,1,128,128]{4,3,2,1,0:T(8,128)S(1)} copy-done((f32[1,3,1,128,128]{4,3,2,1,0:T(8,128)S(1)}, f32[1,3,1,128,128]{4,3,2,1,0:T(8,128)}, u32[]{:S(2)}) %copy-start) | copy-done | bytes 196632
  3.1 0.2 slice_reduce_fusion.8
  3.3 0.2 slice_reduce_fusion.7
  3.5 0.2 slice_reduce_fusion.6
  3.7 0.2 fusion.22
  3.8 0.2 convolution_multiply_fusion
  4.1 0.7 copy-done.2
  4.8 0.2 convert_reduce_fusion.2
  5.0 0.6 copy-done.3
  5.7 0.2 fusion.87
  6.2 0.7 all_to_all.16
  6.9 10.4 %all-to-all-start = ((f32[16,1,770]{2,1,0:T(1,128)}), f32[16,1,770]{2,1,0:T(1,128)S(1)}, u32[]{:S(2)}, u32[]{:S(2)}) async-start(f32[16,1,770]{2,1,0:T(1,128)} %all_to_all.16), calls=%async_computation | async-start | bytes 114688 | tf_op jit(solution)/shard_map/all_to_all | solution.py:182
  17.4 4.7 %collective-permute-start = (f32[4,3,1,128]{3,2,1,0:T(1,128)S(1)}, f32[4,3,1,128]{3,2,1,0:T(1,128)S(1)}, u32[]{:S(2)}, u32[]{:S(2)}) collective-permute-start(f32[4,3,1,128]{3,2,1,0:T(1,128)S(1)} %pad_maximum_fusion.51), channel_id=1, source_target_pairs={{0,256},{256,0},{1,257},{257,1},{2,258},{258,2},{3,259},{259,3},{4... | collective-permute-start | bytes 18440 | tf_op jit(solution)/shard_map/ppermute | solution.py:114
  22.1 3.1 %collective-permute-start.1 = (f32[3,1,128]{2,1,0:T(1,128)S(1)}, f32[3,1,128]{2,1,0:T(1,128)S(1)}, u32[]{:S(2)}, u32[]{:S(2)}) collective-permute-start(f32[3,1,128]{2,1,0:T(1,128)S(1)} %pad_maximum_fusion.56), channel_id=1, source_target_pairs={{0,16},{16,32},{32,48},{48,64},{64,80},{80,96},{96,112},{112,128},... | collective-permute-start | bytes 4616 | tf_op jit(solution)/shard_map/ppermute | solution.py:115
  25.2 2.8 %collective-permute-start.2 = (f32[3,1,128]{2,1,0:T(1,128)S(1)}, f32[3,1,128]{2,1,0:T(1,128)S(1)}, u32[]{:S(2)}, u32[]{:S(2)}) collective-permute-start(f32[3,1,128]{2,1,0:T(1,128)S(1)} %pad_maximum_fusion.55), channel_id=1, source_target_pairs={{16,0},{32,16},{48,32},{64,48},{80,64},{96,80},{112,96},{128,112},... | collective-permute-start | bytes 4616 | tf_op jit(solution)/shard_map/ppermute | solution.py:116
  28.5 0.6 copy-done.5
  29.1 0.2 fusion.96
  29.3 4.1 %collective-permute-done.2 = f32[3,1,128]{2,1,0:T(1,128)S(1)} collective-permute-done((f32[3,1,128]{2,1,0:T(1,128)S(1)}, f32[3,1,128]{2,1,0:T(1,128)S(1)}, u32[]{:S(2)}, u32[]{:S(2)}) %collective-permute-start.2) | collective-permute-done | bytes 1568 | tf_op jit(solution)/shard_map/ppermute | solution.py:116
  33.6 0.1 copy.497
  33.8 0.1 copy.498
  34.0 0.1 copy.499
  34.2 0.1 copy.500
  34.4 0.1 copy.501
  34.6 0.1 copy.502
  34.7 0.2 maximum_multiply_fusion
  34.9 0.6 copy-done.1
  35.6 0.1 fusion.71
  35.7 0.2 maximum_multiply_fusion.1
  35.9 0.2 fusion.59
  36.2 0.1 fusion.86
  36.5 0.4 convolution_bitcast_fusion
  36.8 0.1 convert_reduce_fusion.1
  37.0 0.1 fusion.77
  37.1 0.2 slice_reduce_fusion.5
  37.3 0.2 slice_reduce_fusion.4
  37.5 0.2 slice_reduce_fusion.3
  37.8 0.1 convert_reduce_fusion
  37.9 0.5 fusion.14
  38.5 0.2 reshape.914
  38.8 0.7 copy.511
  39.5 7.2 %all-to-all-start.1 = ((f32[16,1,768]{2,1,0:T(1,128)}), f32[16,1,768]{2,1,0:T(1,128)S(1)}, u32[]{:S(2)}, u32[]{:S(2)}) async-start(f32[16,1,768]{2,1,0:T(1,128)} %copy.511), calls=%async_computation.1 | async-start | bytes 98304 | tf_op jit(solution)/shard_map/all_to_all | solution.py:221
  46.7 1.9 %collective-permute-start.4 = (f32[3,1,128]{2,1,0:T(1,128)S(1)}, f32[3,1,128]{2,1,0:T(1,128)S(1)}, u32[]{:S(2)}, u32[]{:S(2)}) collective-permute-start(f32[3,1,128]{2,1,0:T(1,128)S(1)} %pad_maximum_fusion.60), channel_id=1, source_target_pairs={{0,16},{16,32},{32,48},{48,64},{64,80},{80,96},{96,112},{112,128},... | collective-permute-start | bytes 4616 | tf_op jit(solution)/shard_map/ppermute | solution.py:115
  48.6 7.7 %collective-permute-start.3 = (f32[4,3,1,128]{3,2,1,0:T(1,128)S(1)}, f32[4,3,1,128]{3,2,1,0:T(1,128)S(1)}, u32[]{:S(2)}, u32[]{:S(2)}) collective-permute-start(f32[4,3,1,128]{3,2,1,0:T(1,128)S(1)} %pad_maximum_fusion.52), channel_id=1, source_target_pairs={{0,256},{256,0},{1,257},{257,1},{2,258},{258,2},{3,259},{259,3},{4... | collective-permute-start | bytes 18440 | tf_op jit(solution)/shard_map/ppermute | solution.py:114
  56.4 3.9 %collective-permute-start.5 = (f32[3,1,128]{2,1,0:T(1,128)S(1)}, f32[3,1,128]{2,1,0:T(1,128)S(1)}, u32[]{:S(2)}, u32[]{:S(2)}) collective-permute-start(f32[3,1,128]{2,1,0:T(1,128)S(1)} %pad_maximum_fusion.59), channel_id=1, source_target_pairs={{16,0},{32,16},{48,32},{64,48},{80,64},{96,80},{112,96},{128,112},... | collective-permute-start | bytes 4616 | tf_op jit(solution)/shard_map/ppermute | solution.py:116
  60.4 0.2 copy.528
  60.6 0.5 fusion.6
  61.1 0.3 fusion.162
  61.4 0.2 fusion.93
  61.6 2.9 %collective-permute-done.5 = f32[3,1,128]{2,1,0:T(1,128)S(1)} collective-permute-done((f32[3,1,128]{2,1,0:T(1,128)S(1)}, f32[3,1,128]{2,1,0:T(1,128)S(1)}, u32[]{:S(2)}, u32[]{:S(2)}) %collective-permute-start.5) | collective-permute-done | bytes 1568 | tf_op jit(solution)/shard_map/ppermute | solution.py:116
  64.9 0.1 copy.515
  65.1 0.1 copy.516
  65.3 0.1 copy.517
  65.5 0.1 copy.518
  65.7 0.1 copy.519
  65.8 0.2 maximum_multiply_fusion.2
  66.0 0.1 fusion.46
  66.1 0.2 maximum_multiply_fusion.3
  66.3 0.2 fusion.33
  66.7 0.6 gather_fusion
  67.3 0.3 fusion.5
  67.6 0.8 %reshape.931 = f32[1,1,16,3,1,576]{5,4,3,2,1,0:T(1,128)} reshape(f32[48,576]{1,0:T(8,128)S(1)} %fusion.5) | data formatting | bytes 221184 | tf_op jit(solution)/shard_map/reshape | solution.py:240
  68.3 0.1 fusion.53
  68.5 1.1 %fusion.3 = f32[1,3,1,128,128]{4,3,2,1,0:T(8,128)} fusion(f32[32,3,8,128]{3,2,1,0:T(8,128)S(1)} %fusion.6, f32[1,1,128,128]{3,2,1,0:T(8,128)S(1)} %fusion.33, f32[1,1,128,128]{3,2,1,0:T(8,128)S(1)} %fusion.46, f32[1,1,128,128]{3,2,1,0:T(8,128)S(1)} %fusion.53, f32[128,128]{1,0:T(8,128)S(1)} %fusion.162, s32[32,8]{1,0:T(8,128)S(1)} %get-tuple-element.104, ...), kind=kOutput, calls=%fused_computation.6 | convolution fusion | flops 151355392 | bytes 853024 | tf_op jit(solution)/shard_map/kar,kflac->flrc/dot_general | solution.py:234
  (105 shorter events, 3.3 us)
Async XLA Ops:
  2.1 0.9 %copy-start = (f32[1,3,1,128,128]{4,3,2,1,0:T(8,128)S(1)}, f32[1,3,1,128,128]{4,3,2,1,0:T(8,128)}, u32[]{:S(2)}) copy-start(f32[1,3,1,128,128]{4,3,2,1,0:T(8,128)} %param.6) | copy-start | bytes 589828
  4.1 0.7 copy-start.2
  5.0 0.7 copy-start.3
  6.9 26.5 %all-to-all-start = ((f32[16,1,770]{2,1,0:T(1,128)}), f32[16,1,770]{2,1,0:T(1,128)S(1)}, u32[]{:S(2)}, u32[]{:S(2)}) async-start(f32[16,1,770]{2,1,0:T(1,128)} %all_to_all.16), calls=%async_computation | async-start | bytes 114688 | tf_op jit(solution)/shard_map/all_to_all | solution.py:182
  17.4 11.1 %collective-permute-start = (f32[4,3,1,128]{3,2,1,0:T(1,128)S(1)}, f32[4,3,1,128]{3,2,1,0:T(1,128)S(1)}, u32[]{:S(2)}, u32[]{:S(2)}) collective-permute-start(f32[4,3,1,128]{3,2,1,0:T(1,128)S(1)} %pad_maximum_fusion.51), channel_id=1, source_target_pairs={{0,256},{256,0},{1,257},{257,1},{2,258},{258,2},{3,259},{259,3},{4... | collective-permute-start | bytes 18440 | tf_op jit(solution)/shard_map/ppermute | solution.py:114
  22.1 5.9 %copy-start.4 = (s32[1,4]{1,0:T(1,128)S(1)}, s32[1,4]{1,0:T(1,128)}, u32[]{:S(2)}) copy-start(s32[1,4]{1,0:T(1,128)} %param.8) | copy-start | bytes 52
  22.1 7.1 %collective-permute-start.1 = (f32[3,1,128]{2,1,0:T(1,128)S(1)}, f32[3,1,128]{2,1,0:T(1,128)S(1)}, u32[]{:S(2)}, u32[]{:S(2)}) collective-permute-start(f32[3,1,128]{2,1,0:T(1,128)S(1)} %pad_maximum_fusion.56), channel_id=1, source_target_pairs={{0,16},{16,32},{32,48},{48,64},{64,80},{80,96},{96,112},{112,128},... | collective-permute-start | bytes 4616 | tf_op jit(solution)/shard_map/ppermute | solution.py:115
  25.2 8.2 %collective-permute-start.2 = (f32[3,1,128]{2,1,0:T(1,128)S(1)}, f32[3,1,128]{2,1,0:T(1,128)S(1)}, u32[]{:S(2)}, u32[]{:S(2)}) collective-permute-start(f32[3,1,128]{2,1,0:T(1,128)S(1)} %pad_maximum_fusion.55), channel_id=1, source_target_pairs={{16,0},{32,16},{48,32},{64,48},{80,64},{96,80},{112,96},{128,112},... | collective-permute-start | bytes 4616 | tf_op jit(solution)/shard_map/ppermute | solution.py:116
  28.4 0.7 copy-start.5
  34.7 0.8 %copy-start.1 = (f32[1,128,128]{2,1,0:T(8,128)S(1)}, f32[1,128,128]{2,1,0:T(8,128)}, u32[]{:S(2)}) copy-start(f32[1,128,128]{2,1,0:T(8,128)} %param.7) | copy-start | bytes 196612
  39.5 25.1 %all-to-all-start.1 = ((f32[16,1,768]{2,1,0:T(1,128)}), f32[16,1,768]{2,1,0:T(1,128)S(1)}, u32[]{:S(2)}, u32[]{:S(2)}) async-start(f32[16,1,768]{2,1,0:T(1,128)} %copy.511), calls=%async_computation.1 | async-start | bytes 98304 | tf_op jit(solution)/shard_map/all_to_all | solution.py:221
  46.7 14.9 %collective-permute-start.4 = (f32[3,1,128]{2,1,0:T(1,128)S(1)}, f32[3,1,128]{2,1,0:T(1,128)S(1)}, u32[]{:S(2)}, u32[]{:S(2)}) collective-permute-start(f32[3,1,128]{2,1,0:T(1,128)S(1)} %pad_maximum_fusion.60), channel_id=1, source_target_pairs={{0,16},{16,32},{32,48},{48,64},{64,80},{80,96},{96,112},{112,128},... | collective-permute-start | bytes 4616 | tf_op jit(solution)/shard_map/ppermute | solution.py:115
  48.6 12.8 %collective-permute-start.3 = (f32[4,3,1,128]{3,2,1,0:T(1,128)S(1)}, f32[4,3,1,128]{3,2,1,0:T(1,128)S(1)}, u32[]{:S(2)}, u32[]{:S(2)}) collective-permute-start(f32[4,3,1,128]{3,2,1,0:T(1,128)S(1)} %pad_maximum_fusion.52), channel_id=1, source_target_pairs={{0,256},{256,0},{1,257},{257,1},{2,258},{258,2},{3,259},{259,3},{4... | collective-permute-start | bytes 18440 | tf_op jit(solution)/shard_map/ppermute | solution.py:114
  56.4 8.2 %collective-permute-start.5 = (f32[3,1,128]{2,1,0:T(1,128)S(1)}, f32[3,1,128]{2,1,0:T(1,128)S(1)}, u32[]{:S(2)}, u32[]{:S(2)}) collective-permute-start(f32[3,1,128]{2,1,0:T(1,128)S(1)} %pad_maximum_fusion.59), channel_id=1, source_target_pairs={{16,0},{32,16},{48,32},{64,48},{80,64},{96,80},{112,96},{128,112},... | collective-permute-start | bytes 4616 | tf_op jit(solution)/shard_map/ppermute | solution.py:116

commit v7 on v6

--- a/solution.py
+++ b/solution.py
@@ -90,30 +90,49 @@
     return first_rows, last_rows, first_cols, last_cols
 
 
-def column_halos(first_cols, last_cols):
+def exchange(nest_part, first_rows, last_rows, first_cols, last_cols):
     count = lax.axis_size("gy")
     here = lax.axis_index("gy")
+    on_first_panel = lax.axis_index("panel") == 0
     target = jnp.arange(count, dtype=jnp.int32)
     to_next = (target == here + 1)[:, None, None, None]
     to_prev = (target == here - 1)[:, None, None, None]
-    return jnp.where(to_next, last_cols[None], jnp.where(to_prev, first_cols[None], 0.0))
-
-
-def received_columns(got):
-    count = lax.axis_size("gy")
-    here = lax.axis_index("gy")
-    south = lax.dynamic_index_in_dim(got, jnp.maximum(here - 1, 0), axis=0, keepdims=False)
-    north = lax.dynamic_index_in_dim(got, jnp.minimum(here + 1, count - 1), axis=0, keepdims=False)
-    return south, north
-
-
-def substep(fields, strips, from_south, from_north, coriolis, turns, flags):
+    columns = jnp.where(to_next, last_cols[None], jnp.where(to_prev, first_cols[None], 0.0))
+    mine = jnp.concatenate([nest_part, columns.reshape(count, -1)], axis=1)
+    row_edge = jnp.where(lax.axis_index("gx") == 0, first_rows, last_rows)
+    col_edge = jnp.where(here == 0, first_cols, last_cols)
+    edge = jnp.concatenate([row_edge.reshape(-1), col_edge.reshape(-1)])
+    edge = jnp.pad(edge, (0, mine.shape[1] - edge.shape[0]))
+    other = jnp.where((target == here)[:, None], edge[None], 0.0)
+    sent = jnp.where(
+        on_first_panel,
+        jnp.concatenate([mine, other], axis=0),
+        jnp.concatenate([other, mine], axis=0),
+    )
+    got = lax.all_to_all(sent, ("panel", "gy"), split_axis=0, concat_axis=0, tiled=True)
+    own_start = jnp.where(on_first_panel, 0, count)
+    partner_at = jnp.where(on_first_panel, count, 0) + here
+    from_panel = lax.dynamic_slice_in_dim(got, own_start, count, axis=0)
+    from_partner = lax.dynamic_index_in_dim(got, partner_at, axis=0, keepdims=False)
+    nest_in = from_panel[:, : nest_part.shape[1]]
+    got_columns = from_panel[:, nest_part.shape[1] :].reshape(columns.shape)
+    south = lax.dynamic_index_in_dim(got_columns, jnp.maximum(here - 1, 0), axis=0, keepdims=False)
+    north = lax.dynamic_index_in_dim(
+        got_columns, jnp.minimum(here + 1, count - 1), axis=0, keepdims=False
+    )
+    strip = first_rows.size
+    partner_row = from_partner[:strip].reshape(first_rows.shape)
+    partner_col = from_partner[strip : 2 * strip].reshape(first_cols.shape)
+    return nest_in, south, north, partner_row, partner_col
+
+
+def substep(fields, strips, halos_y, coriolis, turns, flags):
     nx = lax.axis_size("gx")
-    first_rows, last_rows, first_cols, last_cols = strips
-    edges = jnp.stack([first_rows, last_rows, first_cols, last_cols], axis=0)
-    partner = lax.ppermute(edges, "panel", [(0, 1), (1, 0)])
+    first_rows, last_rows, _, _ = strips
+    from_south, from_north, partner_row, partner_col = halos_y
     from_west = lax.ppermute(last_rows, "gx", shift_pairs(nx, 1))
     from_east = lax.ppermute(first_rows, "gx", shift_pairs(nx, -1))
+    partner = jnp.stack([partner_row, partner_row, partner_col, partner_col], axis=0)
     turned = jnp.einsum("sij,sjlc->silc", turns, partner, precision=HI)
     halos = [
         jnp.where(flags[side], turned[side], neighbour)
@@ -174,14 +193,10 @@
     )
     outgoing = jnp.dot(slot_hit, payload, precision=HI)
     strips0 = edge_strips((tile[0], tile[1], tile[2]))
-    columns0 = column_halos(strips0[2], strips0[3])
-    ask_out = jnp.concatenate(
-        [outgoing.reshape(devices_y, capacity * (cells + 1)), columns0.reshape(devices_y, -1)],
-        axis=1,
-    )
-    ask_in = lax.all_to_all(ask_out, "gy", split_axis=0, concat_axis=0, tiled=True)
-    asked_payload = ask_in[:, : capacity * (cells + 1)].reshape(width, cells + 1)
-    got0 = ask_in[:, capacity * (cells + 1) :].reshape(columns0.shape)
+    ask_in, south0, north0, partner_row0, partner_col0 = exchange(
+        outgoing.reshape(devices_y, capacity * (cells + 1)), *strips0
+    )
+    asked_payload = ask_in.reshape(width, cells + 1)
     asked = asked_payload[:, 0].astype(jnp.int32) - 1
     asked_means = asked_payload[:, 1:].reshape(width, 3, level_stack, PATCH, PATCH)
 
@@ -209,20 +224,23 @@
     ]
     turns = edge_turns(codes)
     cell_coriolis = coriolis[0][None]
-    south0, north0 = received_columns(got0)
     fields = substep(
-        (tile[0], tile[1], tile[2]), strips0, south0, north0, cell_coriolis, turns, flags
+        (tile[0], tile[1], tile[2]),
+        strips0,
+        (south0, north0, partner_row0, partner_col0),
+        cell_coriolis,
+        turns,
+        flags,
     )
     strips1 = edge_strips(fields)
-    columns1 = column_halos(strips1[2], strips1[3])
-    answer_out = jnp.concatenate(
-        [picked.reshape(devices_y, capacity * cells), columns1.reshape(devices_y, -1)], axis=1
-    )
-    answer_in = lax.all_to_all(answer_out, "gy", split_axis=0, concat_axis=0, tiled=True)
-    incoming = answer_in[:, : capacity * cells].reshape(width, cells)
-    got1 = answer_in[:, capacity * cells :].reshape(columns1.shape)
-    south1, north1 = received_columns(got1)
-    fields = substep(fields, strips1, south1, north1, cell_coriolis, turns, flags)
+    answer_in, south1, north1, partner_row1, partner_col1 = exchange(
+        picked.reshape(devices_y, capacity * cells), *strips1
+    )
+    incoming = answer_in.reshape(width, cells)
+    fields = substep(
+        fields, strips1, (south1, north1, partner_row1, partner_col1), cell_coriolis, turns,
+        flags,
+    )
 
     parent = jnp.take(incoming, slot_of, axis=0)
     coarse = parent.reshape(slots * 3 * level_stack, coarse_cells)

time: 70.1 us -> 71.3 us (1.017)
  local copies, waits for them, and re-layouts: 10.3 us -> 11.1 us
    ppermute x2 -> x0, starting transfers between devices: 12.4 us -> none  [substep(): partner = lax.ppermute(edges, 'panel', [(0, 1), (1, 0)])]
    all_to_all x2, starting transfers between devices: 17.6 us -> 28.1 us  [exchange(): lax.all_to_all(sent, ('panel', 'gy'), split_axis=0, concat_axis=0, tiled=...]
    ppermute x2, starting transfers between devices: 4.98 us -> 8.54 us  [substep(): from_west = lax.ppermute(last_rows, 'gx', shift_pairs(nx, 1))]
    ppermute x2, starting transfers between devices: 6.71 us -> 4.98 us  [substep(): from_east = lax.ppermute(first_rows, 'gx', shift_pairs(nx, -1))]
    all_to_all x2 -> x0, local copies, waits for them, and re-layouts: 1.34 us -> none  [the longest x1 0.67 us: step(): lax.all_to_all(answer_out, 'gy', split_axis=0, concat_axis=0, tiled=True)]
    all_to_all x2, waiting for transfers between devices: 0.01 us -> 1.11 us  [exchange(): lax.all_to_all(sent, ('panel', 'gy'), split_axis=0, concat_axis=0, tiled=...]
    squeeze x1, local copies, waits for them, and re-layouts: 0.01 us -> 0.92 us  [step(): tile[0]]
    select_n x2 -> x9, other arithmetic: 0.15 us -> 1.06 us  [the longest x2 0.77 us: exchange(): jnp.where(on_first_panel, jnp.concatenate([mine, other], axis=0), jnp.con...]
  transfers between devices with their start and end apart: 8 -> 6, of which waited for: 2 -> 4; matrix products, arithmetic and copies ran while one was open for 3% -> 4% of each run, Pallas kernels for 0% -> 0%
where the time goes in v7:
time: 71.3 us; the launch traced here: 70.8 us
  starting transfers between devices  41.6 us (58%)
  local copies, waits for them, and re-layouts  11.1 us (16%)
  waiting for transfers between devices  7.57 us (11%)
  other arithmetic  5.4 us (8%)
  matrix products  3.82 us (5%)
  between operations  1.36 us (2%)
    all_to_all x2, starting transfers between devices, exchange(): lax.all_to_all(sent, ('panel', 'gy'), split_axis=0, concat_axis=0, tiled=...  28.1 us
    ppermute x2, starting transfers between devices, substep(): from_west = lax.ppermute(last_rows, 'gx', shift_pairs(nx, 1))  8.54 us
    ppermute x2, waiting for transfers between devices, substep(): from_east = lax.ppermute(first_rows, 'gx', shift_pairs(nx, -1))  6.46 us
    ppermute x2, starting transfers between devices, substep(): from_east = lax.ppermute(first_rows, 'gx', shift_pairs(nx, -1))  4.98 us
    unnamed x16, local copies, waits for them, and re-layouts  3.74 us
  transfers between devices with their start and end apart: 6, of which 4 were waited for; matrix products, arithmetic and copies ran while one was open for 4% of the time, Pallas kernels for 0%

profile of v7, /device:TPU:58, one launch (start us, length us, event | category | flops | bytes accessed | tf_op | source)
XLA Modules:
  0.0 70.8 jit_solution(6976423054859651499)
XLA Ops:
  0.6 0.9 %slice_bitcast_fusion.2 = (f32[1,128,128]{2,1,0:T(8,128)S(1)}, f32[1,128,128]{2,1,0:T(8,128)S(1)}, f32[1,128,128]{2,1,0:T(8,128)S(1)}) fusion(f32[1,3,1,128,128]{4,3,2,1,0:T(8,128)} %param.6), kind=kLoop, calls=%fused_computation.168 | loop fusion | bytes 393216 | tf_op jit(solution)/shard_map/squeeze | solution.py:228
  1.6 0.2 slice_reduce_fusion.11
  1.8 0.2 slice_reduce_fusion.9
  2.0 0.7 copy-done.2
  2.7 0.3 reduce
  3.7 0.2 fusion.22
  3.9 0.2 convolution_multiply_fusion
  4.2 0.7 copy-done.3
  4.8 0.2 convert_reduce_fusion.2
  5.0 0.6 copy-done.4
  5.8 0.2 fusion.87
  6.3 0.8 %broadcast_select_fusion = f32[32,1,770]{2,1,0:T(1,128)} fusion(pred[]{:T(512)S(6)} %eq.206, f32[16,1,770]{2,1,0:T(1,128)S(1)} %concatenate.331, f32[16,1,770]{2,1,0:T(1,128)S(1)} %concatenate.329), kind=kLoop, calls=%fused_computation.15 | loop fusion | flops 73920 | bytes 197121 | tf_op jit(solution)/shard_map/jit(_where)/select_n | solution.py:107
  7.0 15.8 %all-to-all-start = ((f32[32,1,770]{2,1,0:T(1,128)}), f32[32,1,770]{2,1,0:T(1,128)S(1)}, u32[]{:S(2)}, u32[]{:S(2)}) async-start(f32[32,1,770]{2,1,0:T(1,128)} %broadcast_select_fusion), calls=%async_computation | async-start | bytes 229376 | tf_op jit(solution)/shard_map/all_to_all | solution.py:112
  22.9 5.8 %collective-permute-start = (f32[3,1,128]{2,1,0:T(1,128)S(1)}, f32[3,1,128]{2,1,0:T(1,128)S(1)}, u32[]{:S(2)}, u32[]{:S(2)}) collective-permute-start(f32[3,1,128]{2,1,0:T(1,128)S(1)} %get-tuple-element.36), channel_id=1, source_target_pairs={{0,16},{16,32},{32,48},{48,64},{64,80},{80,96},{96,112},{112,128},... | collective-permute-start | bytes 4616 | tf_op jit(solution)/shard_map/ppermute | solution.py:133
  28.6 1.9 %collective-permute-start.1 = (f32[3,1,128]{2,1,0:T(1,128)S(1)}, f32[3,1,128]{2,1,0:T(1,128)S(1)}, u32[]{:S(2)}, u32[]{:S(2)}) collective-permute-start(f32[3,1,128]{2,1,0:T(1,128)S(1)} %get-tuple-element.37), channel_id=1, source_target_pairs={{16,0},{32,16},{48,32},{64,48},{80,64},{96,80},{112,96},{128,112},... | collective-permute-start | bytes 4616 | tf_op jit(solution)/shard_map/ppermute | solution.py:134
  31.3 0.7 copy-done.6
  32.0 0.2 fusion.93
  32.7 0.1 copy.417
  32.8 0.1 copy.418
  32.9 0.1 copy.419
  33.0 3.8 %collective-permute-done.1 = f32[3,1,128]{2,1,0:T(1,128)S(1)} collective-permute-done((f32[3,1,128]{2,1,0:T(1,128)S(1)}, f32[3,1,128]{2,1,0:T(1,128)S(1)}, u32[]{:S(2)}, u32[]{:S(2)}) %collective-permute-start.1) | collective-permute-done | bytes 1568 | tf_op jit(solution)/shard_map/ppermute | solution.py:134
  36.9 0.1 copy.420
  37.1 0.1 copy.421
  37.2 0.2 maximum_multiply_fusion
  37.4 0.6 copy-done.1
  38.1 0.1 fusion.71
  38.2 0.2 maximum_multiply_fusion.1
  38.4 0.2 fusion.59
  38.7 0.1 fusion.86
  38.9 0.4 copy-done
  39.3 0.1 fusion.77
  39.5 0.2 slice_reduce_fusion.5
  39.6 0.2 slice_reduce_fusion.4
  39.8 0.2 slice_reduce_fusion.3
  40.1 0.4 convolution_bitcast_fusion
  40.5 0.1 convert_reduce_fusion.1
  40.8 0.1 convert_reduce_fusion
  40.9 0.5 fusion.14
  41.4 0.2 reshape.1217
  41.9 0.7 %copy.428 = f32[32,1,768]{2,1,0:T(1,128)} copy(f32[32,1,768]{2,0,1:T(8,128)S(1)} %maximum_select_fusion.2) | data formatting | bytes 196608 | tf_op jit(solution)/shard_map/jit(_where)/select_n | solution.py:107
  42.6 12.2 %all-to-all-start.1 = ((f32[32,1,768]{2,1,0:T(1,128)}), f32[32,1,768]{2,1,0:T(1,128)S(1)}, u32[]{:S(2)}, u32[]{:S(2)}) async-start(f32[32,1,768]{2,1,0:T(1,128)} %copy.428), calls=%async_computation.1 | async-start | bytes 196608 | tf_op jit(solution)/shard_map/all_to_all | solution.py:112
  54.9 2.8 %collective-permute-start.2 = (f32[3,1,128]{2,1,0:T(1,128)S(1)}, f32[3,1,128]{2,1,0:T(1,128)S(1)}, u32[]{:S(2)}, u32[]{:S(2)}) collective-permute-start(f32[3,1,128]{2,1,0:T(1,128)S(1)} %get-tuple-element.33), channel_id=1, source_target_pairs={{0,16},{16,32},{32,48},{48,64},{64,80},{80,96},{96,112},{112,128},... | collective-permute-start | bytes 4616 | tf_op jit(solution)/shard_map/ppermute | solution.py:133
  57.7 3.1 %collective-permute-start.3 = (f32[3,1,128]{2,1,0:T(1,128)S(1)}, f32[3,1,128]{2,1,0:T(1,128)S(1)}, u32[]{:S(2)}, u32[]{:S(2)}) collective-permute-start(f32[3,1,128]{2,1,0:T(1,128)S(1)} %get-tuple-element.34), channel_id=1, source_target_pairs={{16,0},{32,16},{48,32},{64,48},{80,64},{96,80},{112,96},{128,112},... | collective-permute-start | bytes 4616 | tf_op jit(solution)/shard_map/ppermute | solution.py:134
  60.8 0.2 copy.449
  61.0 0.5 fusion.6
  61.6 0.3 fusion.168
  61.9 1.0 %all-to-all-done.1 = f32[32,1,768]{2,1,0:T(1,128)S(1)} async-done(((f32[32,1,768]{2,1,0:T(1,128)}), f32[32,1,768]{2,1,0:T(1,128)S(1)}, u32[]{:S(2)}, u32[]{:S(2)}) %all-to-all-start.1) | async-done | bytes 98336 | tf_op jit(solution)/shard_map/all_to_all | solution.py:112
  63.0 0.2 fusion.100
  63.2 2.7 %collective-permute-done.3 = f32[3,1,128]{2,1,0:T(1,128)S(1)} collective-permute-done((f32[3,1,128]{2,1,0:T(1,128)S(1)}, f32[3,1,128]{2,1,0:T(1,128)S(1)}, u32[]{:S(2)}, u32[]{:S(2)}) %collective-permute-start.3) | collective-permute-done | bytes 1568 | tf_op jit(solution)/shard_map/ppermute | solution.py:134
  66.0 0.1 copy.435
  66.2 0.1 copy.436
  66.4 0.1 copy.437
  66.5 0.1 copy.438
  66.7 0.1 copy.439
  66.9 0.1 copy.440
  67.1 0.2 maximum_multiply_fusion.2
  67.3 0.1 fusion.46
  67.4 0.2 maximum_multiply_fusion.3
  67.6 0.2 fusion.33
  67.9 0.6 gather_fusion
  68.6 0.3 fusion.5
  68.8 0.8 %reshape.1235 = f32[1,1,16,3,1,576]{5,4,3,2,1,0:T(1,128)} reshape(f32[48,576]{1,0:T(8,128)S(1)} %fusion.5) | data formatting | bytes 221184 | tf_op jit(solution)/shard_map/reshape | solution.py:258
  69.6 0.1 fusion.53
  69.7 1.1 %fusion.3 = f32[1,3,1,128,128]{4,3,2,1,0:T(8,128)} fusion(f32[32,3,8,128]{3,2,1,0:T(8,128)S(1)} %fusion.6, f32[1,1,128,128]{3,2,1,0:T(8,128)S(1)} %fusion.33, f32[1,1,128,128]{3,2,1,0:T(8,128)S(1)} %fusion.46, f32[1,1,128,128]{3,2,1,0:T(8,128)S(1)} %fusion.53, f32[128,128]{1,0:T(8,128)S(1)} %fusion.168, s32[32,8]{1,0:T(8,128)S(1)} %iota_add_fusion.1, ...), kind=kOutput, calls=%fused_computation.6 | convolution fusion | flops 151355392 | bytes 853024 | tf_op jit(solution)/shard_map/kar,kflac->flrc/dot_general | solution.py:252
  (110 shorter events, 3.8 us)
Async XLA Ops:
  1.7 0.9 %copy-start.2 = (f32[1,1,16,3,1,576]{5,4,3,2,1,0:T(1,128)S(1)}, f32[1,1,16,3,1,576]{5,4,3,2,1,0:T(1,128)}, u32[]{:S(2)}) copy-start(f32[1,1,16,3,1,576]{5,4,3,2,1,0:T(1,128)} %param.9) | copy-start | bytes 331780
  4.2 0.7 copy-start.3
  5.0 0.7 copy-start.4
  7.0 24.1 %all-to-all-start = ((f32[32,1,770]{2,1,0:T(1,128)}), f32[32,1,770]{2,1,0:T(1,128)S(1)}, u32[]{:S(2)}, u32[]{:S(2)}) async-start(f32[32,1,770]{2,1,0:T(1,128)} %broadcast_select_fusion), calls=%async_computation | async-start | bytes 229376 | tf_op jit(solution)/shard_map/all_to_all | solution.py:112
  22.9 7.7 %copy-start.5 = (s32[1,4]{1,0:T(1,128)S(1)}, s32[1,4]{1,0:T(1,128)}, u32[]{:S(2)}) copy-start(s32[1,4]{1,0:T(1,128)} %param.8) | copy-start | bytes 52
  22.9 9.6 %collective-permute-start = (f32[3,1,128]{2,1,0:T(1,128)S(1)}, f32[3,1,128]{2,1,0:T(1,128)S(1)}, u32[]{:S(2)}, u32[]{:S(2)}) collective-permute-start(f32[3,1,128]{2,1,0:T(1,128)S(1)} %get-tuple-element.36), channel_id=1, source_target_pairs={{0,16},{16,32},{32,48},{48,64},{64,80},{80,96},{96,112},{112,128},... | collective-permute-start | bytes 4616 | tf_op jit(solution)/shard_map/ppermute | solution.py:133
  28.6 8.2 %collective-permute-start.1 = (f32[3,1,128]{2,1,0:T(1,128)S(1)}, f32[3,1,128]{2,1,0:T(1,128)S(1)}, u32[]{:S(2)}, u32[]{:S(2)}) collective-permute-start(f32[3,1,128]{2,1,0:T(1,128)S(1)} %get-tuple-element.37), channel_id=1, source_target_pairs={{16,0},{32,16},{48,32},{64,48},{80,64},{96,80},{112,96},{128,112},... | collective-permute-start | bytes 4616 | tf_op jit(solution)/shard_map/ppermute | solution.py:134
  31.3 0.7 copy-start.6
  37.2 0.8 %copy-start.1 = (f32[1,128,128]{2,1,0:T(8,128)S(1)}, f32[1,128,128]{2,1,0:T(8,128)}, u32[]{:S(2)}) copy-start(f32[1,128,128]{2,1,0:T(8,128)} %param.7) | copy-start | bytes 196612
  38.4 0.9 %copy-start = (f32[1,3,1,128,128]{4,3,2,1,0:T(8,128)S(1)}, f32[1,3,1,128,128]{4,3,2,1,0:T(8,128)}, u32[]{:S(2)}) copy-start(f32[1,3,1,128,128]{4,3,2,1,0:T(8,128)} %param.6) | copy-start | bytes 589828
  42.6 20.2 %all-to-all-start.1 = ((f32[32,1,768]{2,1,0:T(1,128)}), f32[32,1,768]{2,1,0:T(1,128)S(1)}, u32[]{:S(2)}, u32[]{:S(2)}) async-start(f32[32,1,768]{2,1,0:T(1,128)} %copy.428), calls=%async_computation.1 | async-start | bytes 196608 | tf_op jit(solution)/shard_map/all_to_all | solution.py:112
  54.9 8.3 %collective-permute-start.2 = (f32[3,1,128]{2,1,0:T(1,128)S(1)}, f32[3,1,128]{2,1,0:T(1,128)S(1)}, u32[]{:S(2)}, u32[]{:S(2)}) collective-permute-start(f32[3,1,128]{2,1,0:T(1,128)S(1)} %get-tuple-element.33), channel_id=1, source_target_pairs={{0,16},{16,32},{32,48},{48,64},{64,80},{80,96},{96,112},{112,128},... | collective-permute-start | bytes 4616 | tf_op jit(solution)/shard_map/ppermute | solution.py:133
  57.7 8.2 %collective-permute-start.3 = (f32[3,1,128]{2,1,0:T(1,128)S(1)}, f32[3,1,128]{2,1,0:T(1,128)S(1)}, u32[]{:S(2)}, u32[]{:S(2)}) collective-permute-start(f32[3,1,128]{2,1,0:T(1,128)S(1)} %get-tuple-element.34), channel_id=1, source_target_pairs={{16,0},{32,16},{48,32},{64,48},{80,64},{96,80},{112,96},{128,112},... | collective-permute-start | bytes 4616 | tf_op jit(solution)/shard_map/ppermute | solution.py:134

commit v8 on v6

--- a/solution.py
+++ b/solution.py
@@ -169,21 +169,15 @@
     slot_hit = (jnp.arange(width, dtype=jnp.int32)[:, None] == slot_of[None, :]).astype(
         jnp.float32
     )
-    payload = jnp.concatenate(
-        [(spots + 1).astype(jnp.float32)[:, None], smooth_means], axis=1
-    )
-    outgoing = jnp.dot(slot_hit, payload, precision=HI)
+    outgoing = jnp.dot(slot_hit, (spots + 1).astype(jnp.float32)[:, None], precision=HI)
     strips0 = edge_strips((tile[0], tile[1], tile[2]))
     columns0 = column_halos(strips0[2], strips0[3])
     ask_out = jnp.concatenate(
-        [outgoing.reshape(devices_y, capacity * (cells + 1)), columns0.reshape(devices_y, -1)],
-        axis=1,
+        [outgoing.reshape(devices_y, capacity), columns0.reshape(devices_y, -1)], axis=1
     )
     ask_in = lax.all_to_all(ask_out, "gy", split_axis=0, concat_axis=0, tiled=True)
-    asked_payload = ask_in[:, : capacity * (cells + 1)].reshape(width, cells + 1)
-    got0 = ask_in[:, capacity * (cells + 1) :].reshape(columns0.shape)
-    asked = asked_payload[:, 0].astype(jnp.int32) - 1
-    asked_means = asked_payload[:, 1:].reshape(width, 3, level_stack, PATCH, PATCH)
+    got0 = ask_in[:, capacity:].reshape(columns0.shape)
+    asked = ask_in[:, :capacity].reshape(width).astype(jnp.int32) - 1
 
     valid = asked >= 0
     row0 = (asked // qy) * PATCH
@@ -215,12 +209,21 @@
     )
     strips1 = edge_strips(fields)
     columns1 = column_halos(strips1[2], strips1[3])
+    held_means = jnp.dot(slot_hit, smooth_means, precision=HI)
     answer_out = jnp.concatenate(
-        [picked.reshape(devices_y, capacity * cells), columns1.reshape(devices_y, -1)], axis=1
+        [
+            picked.reshape(devices_y, capacity * cells),
+            held_means.reshape(devices_y, capacity * cells),
+            columns1.reshape(devices_y, -1),
+        ],
+        axis=1,
     )
     answer_in = lax.all_to_all(answer_out, "gy", split_axis=0, concat_axis=0, tiled=True)
     incoming = answer_in[:, : capacity * cells].reshape(width, cells)
-    got1 = answer_in[:, capacity * cells :].reshape(columns1.shape)
+    asked_means = answer_in[:, capacity * cells : 2 * capacity * cells].reshape(
+        width, 3, level_stack, PATCH, PATCH
+    )
+    got1 = answer_in[:, 2 * capacity * cells :].reshape(columns1.shape)
     south1, north1 = received_columns(got1)
     fields = substep(fields, strips1, south1, north1, cell_coriolis, turns, flags)
 

time: 70.1 us -> 70.6 us (level)
  the two profiles are of different devices: /device:TPU:58 before, /device:TPU:56 now
where the time goes in v8:
time: 70.6 us; the launch traced here: 70.1 us
  starting transfers between devices  41.8 us (59%)
  local copies, waits for them, and re-layouts  11 us (16%)
  waiting for transfers between devices  7.6 us (11%)
  other arithmetic  4.42 us (6%)
  matrix products  3.88 us (5%)
  between operations  1.43 us (2%)
    ppermute x2, starting transfers between devices, substep(): partner = lax.ppermute(edges, 'panel', [(0, 1), (1, 0)])  12.4 us
    all_to_all x1, starting transfers between devices, step(): lax.all_to_all(ask_out, 'gy', split_axis=0, concat_axis=0, tiled=True)  10.4 us
    ppermute x2, waiting for transfers between devices, substep(): from_east = lax.ppermute(first_rows, 'gx', shift_pairs(nx, -1))  7.59 us
    all_to_all x1, starting transfers between devices, step(): lax.all_to_all(answer_out, 'gy', split_axis=0, concat_axis=0, tiled=True)  7.21 us
    ppermute x2, starting transfers between devices, substep(): from_west = lax.ppermute(last_rows, 'gx', shift_pairs(nx, 1))  6.26 us
    ppermute x2, starting transfers between devices, substep(): from_east = lax.ppermute(first_rows, 'gx', shift_pairs(nx, -1))  5.43 us
    unnamed x16, local copies, waits for them, and re-layouts  3.13 us
  transfers between devices with their start and end apart: 8, of which 2 were waited for; matrix products, arithmetic and copies ran while one was open for 4% of the time, Pallas kernels for 0%

profile of v8, /device:TPU:56, one launch (start us, length us, event | category | flops | bytes accessed | tf_op | source)
XLA Modules:
  0.0 70.1 jit_solution(15724996171921448077)
XLA Ops:
  0.6 0.9 %slice_bitcast_fusion.2 = (f32[1,128,128]{2,1,0:T(8,128)S(1)}, f32[1,128,128]{2,1,0:T(8,128)S(1)}, f32[1,128,128]{2,1,0:T(8,128)S(1)}) fusion(f32[1,3,1,128,128]{4,3,2,1,0:T(8,128)} %param.6), kind=kLoop, calls=%fused_computation.168 | loop fusion | bytes 393216 | tf_op jit(solution)/shard_map/squeeze | solution.py:208
  1.6 0.2 slice_reduce_fusion.11
  1.7 0.2 slice_reduce_fusion.10
  1.9 0.2 slice_reduce_fusion.9
  2.2 0.6 copy-done.3
  2.8 0.2 convert_reduce_fusion.2
  3.1 0.6 copy-done.4
  3.7 0.1 fusion.86
  4.1 0.7 copy.391
  4.8 10.4 %all-to-all-start = ((f32[16,1,386]{2,1,0:T(1,128)}), f32[16,1,386]{2,1,0:T(1,128)S(1)}, u32[]{:S(2)}, u32[]{:S(2)}) async-start(f32[16,1,386]{2,1,0:T(1,128)} %copy.391), calls=%async_computation | async-start | bytes 65536 | tf_op jit(solution)/shard_map/all_to_all | solution.py:178
  15.3 4.7 %collective-permute-start = (f32[4,3,1,128]{3,2,1,0:T(1,128)S(1)}, f32[4,3,1,128]{3,2,1,0:T(1,128)S(1)}, u32[]{:S(2)}, u32[]{:S(2)}) collective-permute-start(f32[4,3,1,128]{3,2,1,0:T(1,128)S(1)} %pad_maximum_fusion.50), channel_id=1, source_target_pairs={{0,256},{256,0},{1,257},{257,1},{2,258},{258,2},{3,259},{259,3},{4... | collective-permute-start | bytes 18440 | tf_op jit(solution)/shard_map/ppermute | solution.py:114
  20.1 3.1 %collective-permute-start.1 = (f32[3,1,128]{2,1,0:T(1,128)S(1)}, f32[3,1,128]{2,1,0:T(1,128)S(1)}, u32[]{:S(2)}, u32[]{:S(2)}) collective-permute-start(f32[3,1,128]{2,1,0:T(1,128)S(1)} %pad_maximum_fusion.55), channel_id=1, source_target_pairs={{0,16},{16,32},{32,48},{48,64},{64,80},{80,96},{96,112},{112,128},... | collective-permute-start | bytes 4616 | tf_op jit(solution)/shard_map/ppermute | solution.py:115
  23.1 2.8 %collective-permute-start.2 = (f32[3,1,128]{2,1,0:T(1,128)S(1)}, f32[3,1,128]{2,1,0:T(1,128)S(1)}, u32[]{:S(2)}, u32[]{:S(2)}) collective-permute-start(f32[3,1,128]{2,1,0:T(1,128)S(1)} %pad_maximum_fusion.54), channel_id=1, source_target_pairs={{16,0},{32,16},{48,32},{64,48},{80,64},{96,80},{112,96},{128,112},... | collective-permute-start | bytes 4616 | tf_op jit(solution)/shard_map/ppermute | solution.py:116
  26.0 0.3 reduce.14
  26.8 0.2 fusion.22
  26.9 0.2 convolution_multiply_fusion
  27.2 0.1 fusion.85
  27.9 0.6 copy-done.6
  28.5 0.2 fusion.94
  28.7 2.6 %collective-permute-done.2 = f32[3,1,128]{2,1,0:T(1,128)S(1)} collective-permute-done((f32[3,1,128]{2,1,0:T(1,128)S(1)}, f32[3,1,128]{2,1,0:T(1,128)S(1)}, u32[]{:S(2)}, u32[]{:S(2)}) %collective-permute-start.2) | collective-permute-done | bytes 1568 | tf_op jit(solution)/shard_map/ppermute | solution.py:116
  31.7 0.1 copy.394
  31.9 0.1 copy.395
  32.1 0.1 copy.396
  32.3 0.1 copy.397
  32.4 0.1 copy.398
  32.6 0.1 copy.399
  32.8 0.2 maximum_multiply_fusion
  33.0 0.6 copy-done.1
  33.6 0.1 fusion.71
  33.7 0.2 maximum_multiply_fusion.1
  34.0 0.2 fusion.59
  34.2 0.7 copy-done
  34.9 0.1 fusion.77
  35.0 0.2 slice_reduce_fusion.2
  35.2 0.2 slice_reduce_fusion.1
  35.4 0.2 slice_reduce_fusion
  35.7 0.4 convolution_bitcast_fusion
  36.1 0.1 convert_reduce_fusion.1
  36.2 0.1 convert_reduce_fusion
  36.4 0.5 fusion.14
  36.9 0.2 reshape.918
  37.2 0.7 %copy.408 = f32[16,1,1152]{2,1,0:T(1,128)} copy(f32[16,1,1152]{2,0,1:T(8,128)S(1)} %maximum_bitcast_fusion) | data formatting | bytes 147456 | tf_op jit(solution)/shard_map/all_to_all | solution.py:221
  37.9 7.2 %all-to-all-start.1 = ((f32[16,1,1152]{2,1,0:T(1,128)}), f32[16,1,1152]{2,1,0:T(1,128)S(1)}, u32[]{:S(2)}, u32[]{:S(2)}) async-start(f32[16,1,1152]{2,1,0:T(1,128)} %copy.408), calls=%async_computation.1 | async-start | bytes 147456 | tf_op jit(solution)/shard_map/all_to_all | solution.py:221
  45.1 3.2 %collective-permute-start.4 = (f32[3,1,128]{2,1,0:T(1,128)S(1)}, f32[3,1,128]{2,1,0:T(1,128)S(1)}, u32[]{:S(2)}, u32[]{:S(2)}) collective-permute-start(f32[3,1,128]{2,1,0:T(1,128)S(1)} %pad_maximum_fusion.59), channel_id=1, source_target_pairs={{0,16},{16,32},{32,48},{48,64},{64,80},{80,96},{96,112},{112,128},... | collective-permute-start | bytes 4616 | tf_op jit(solution)/shard_map/ppermute | solution.py:115
  48.3 7.7 %collective-permute-start.3 = (f32[4,3,1,128]{3,2,1,0:T(1,128)S(1)}, f32[4,3,1,128]{3,2,1,0:T(1,128)S(1)}, u32[]{:S(2)}, u32[]{:S(2)}) collective-permute-start(f32[4,3,1,128]{3,2,1,0:T(1,128)S(1)} %pad_maximum_fusion.51), channel_id=1, source_target_pairs={{0,256},{256,0},{1,257},{257,1},{2,258},{258,2},{3,259},{259,3},{4... | collective-permute-start | bytes 18440 | tf_op jit(solution)/shard_map/ppermute | solution.py:114
  56.1 2.6 %collective-permute-start.5 = (f32[3,1,128]{2,1,0:T(1,128)S(1)}, f32[3,1,128]{2,1,0:T(1,128)S(1)}, u32[]{:S(2)}, u32[]{:S(2)}) collective-permute-start(f32[3,1,128]{2,1,0:T(1,128)S(1)} %pad_maximum_fusion.58), channel_id=1, source_target_pairs={{16,0},{32,16},{48,32},{64,48},{80,64},{96,80},{112,96},{128,112},... | collective-permute-start | bytes 4616 | tf_op jit(solution)/shard_map/ppermute | solution.py:116
  58.7 0.3 fusion.162
  59.0 0.2 fusion.91
  59.3 5.0 %collective-permute-done.5 = f32[3,1,128]{2,1,0:T(1,128)S(1)} collective-permute-done((f32[3,1,128]{2,1,0:T(1,128)S(1)}, f32[3,1,128]{2,1,0:T(1,128)S(1)}, u32[]{:S(2)}, u32[]{:S(2)}) %collective-permute-start.5) | collective-permute-done | bytes 1568 | tf_op jit(solution)/shard_map/ppermute | solution.py:116
  64.8 0.1 copy.413
  65.0 0.1 copy.414
  65.2 0.1 copy.415
  65.4 0.1 copy.416
  65.5 0.2 maximum_multiply_fusion.2
  65.7 0.1 fusion.46
  65.9 0.2 maximum_multiply_fusion.3
  66.1 0.2 fusion.33
  66.4 0.6 gather_fusion
  67.0 0.3 fusion.5
  67.3 0.8 %reshape.939 = f32[1,1,16,3,1,576]{5,4,3,2,1,0:T(1,128)} reshape(f32[48,576]{1,0:T(8,128)S(1)} %fusion.5) | data formatting | bytes 221184 | tf_op jit(solution)/shard_map/reshape | solution.py:243
  68.1 0.2 reshape.922
  68.3 0.5 fusion.6
  68.8 0.1 fusion.53
  69.0 1.1 %fusion.3 = f32[1,3,1,128,128]{4,3,2,1,0:T(8,128)} fusion(f32[32,3,8,128]{3,2,1,0:T(8,128)S(1)} %fusion.6, f32[1,1,128,128]{3,2,1,0:T(8,128)S(1)} %fusion.33, f32[1,1,128,128]{3,2,1,0:T(8,128)S(1)} %fusion.46, f32[1,1,128,128]{3,2,1,0:T(8,128)S(1)} %fusion.53, f32[128,128]{1,0:T(8,128)S(1)} %fusion.162, s32[32,8]{1,0:T(8,128)S(1)} %get-tuple-element.105, ...), kind=kOutput, calls=%fused_computation.6 | convolution fusion | flops 151355392 | bytes 853024 | tf_op jit(solution)/shard_map/kar,kflac->flrc/dot_general | solution.py:237
  (105 shorter events, 3.4 us)
Async XLA Ops:
  2.2 0.7 copy-start.3
  3.0 0.7 copy-start.4
  4.1 21.9 %copy-start.2 = (f32[1,1,16,3,1,576]{5,4,3,2,1,0:T(1,128)S(1)}, f32[1,1,16,3,1,576]{5,4,3,2,1,0:T(1,128)}, u32[]{:S(2)}) copy-start(f32[1,1,16,3,1,576]{5,4,3,2,1,0:T(1,128)} %param.9) | copy-start | bytes 331780
  4.8 26.5 %all-to-all-start = ((f32[16,1,386]{2,1,0:T(1,128)}), f32[16,1,386]{2,1,0:T(1,128)S(1)}, u32[]{:S(2)}, u32[]{:S(2)}) async-start(f32[16,1,386]{2,1,0:T(1,128)} %copy.391), calls=%async_computation | async-start | bytes 65536 | tf_op jit(solution)/shard_map/all_to_all | solution.py:178
  15.3 12.6 %collective-permute-start = (f32[4,3,1,128]{3,2,1,0:T(1,128)S(1)}, f32[4,3,1,128]{3,2,1,0:T(1,128)S(1)}, u32[]{:S(2)}, u32[]{:S(2)}) collective-permute-start(f32[4,3,1,128]{3,2,1,0:T(1,128)S(1)} %pad_maximum_fusion.50), channel_id=1, source_target_pairs={{0,256},{256,0},{1,257},{257,1},{2,258},{258,2},{3,259},{259,3},{4... | collective-permute-start | bytes 18440 | tf_op jit(solution)/shard_map/ppermute | solution.py:114
  20.0 5.9 %copy-start.5 = (s32[1,4]{1,0:T(1,128)S(1)}, s32[1,4]{1,0:T(1,128)}, u32[]{:S(2)}) copy-start(s32[1,4]{1,0:T(1,128)} %param.8) | copy-start | bytes 52
  20.1 8.6 %collective-permute-start.1 = (f32[3,1,128]{2,1,0:T(1,128)S(1)}, f32[3,1,128]{2,1,0:T(1,128)S(1)}, u32[]{:S(2)}, u32[]{:S(2)}) collective-permute-start(f32[3,1,128]{2,1,0:T(1,128)S(1)} %pad_maximum_fusion.55), channel_id=1, source_target_pairs={{0,16},{16,32},{32,48},{48,64},{64,80},{80,96},{96,112},{112,128},... | collective-permute-start | bytes 4616 | tf_op jit(solution)/shard_map/ppermute | solution.py:115
  23.1 8.2 %collective-permute-start.2 = (f32[3,1,128]{2,1,0:T(1,128)S(1)}, f32[3,1,128]{2,1,0:T(1,128)S(1)}, u32[]{:S(2)}, u32[]{:S(2)}) collective-permute-start(f32[3,1,128]{2,1,0:T(1,128)S(1)} %pad_maximum_fusion.54), channel_id=1, source_target_pairs={{16,0},{32,16},{48,32},{64,48},{80,64},{96,80},{112,96},{128,112},... | collective-permute-start | bytes 4616 | tf_op jit(solution)/shard_map/ppermute | solution.py:116
  27.8 0.7 copy-start.6
  32.8 0.8 %copy-start.1 = (f32[1,128,128]{2,1,0:T(8,128)S(1)}, f32[1,128,128]{2,1,0:T(8,128)}, u32[]{:S(2)}) copy-start(f32[1,128,128]{2,1,0:T(8,128)} %param.7) | copy-start | bytes 196612
  33.9 0.9 %copy-start = (f32[1,3,1,128,128]{4,3,2,1,0:T(8,128)S(1)}, f32[1,3,1,128,128]{4,3,2,1,0:T(8,128)}, u32[]{:S(2)}) copy-start(f32[1,3,1,128,128]{4,3,2,1,0:T(8,128)} %param.6) | copy-start | bytes 589828
  37.9 26.4 %all-to-all-start.1 = ((f32[16,1,1152]{2,1,0:T(1,128)}), f32[16,1,1152]{2,1,0:T(1,128)S(1)}, u32[]{:S(2)}, u32[]{:S(2)}) async-start(f32[16,1,1152]{2,1,0:T(1,128)} %copy.408), calls=%async_computation.1 | async-start | bytes 147456 | tf_op jit(solution)/shard_map/all_to_all | solution.py:221
  45.1 14.1 %collective-permute-start.4 = (f32[3,1,128]{2,1,0:T(1,128)S(1)}, f32[3,1,128]{2,1,0:T(1,128)S(1)}, u32[]{:S(2)}, u32[]{:S(2)}) collective-permute-start(f32[3,1,128]{2,1,0:T(1,128)S(1)} %pad_maximum_fusion.59), channel_id=1, source_target_pairs={{0,16},{16,32},{32,48},{48,64},{64,80},{80,96},{96,112},{112,128},... | collective-permute-start | bytes 4616 | tf_op jit(solution)/shard_map/ppermute | solution.py:115
  48.3 10.7 %collective-permute-start.3 = (f32[4,3,1,128]{3,2,1,0:T(1,128)S(1)}, f32[4,3,1,128]{3,2,1,0:T(1,128)S(1)}, u32[]{:S(2)}, u32[]{:S(2)}) collective-permute-start(f32[4,3,1,128]{3,2,1,0:T(1,128)S(1)} %pad_maximum_fusion.51), channel_id=1, source_target_pairs={{0,256},{256,0},{1,257},{257,1},{2,258},{258,2},{3,259},{259,3},{4... | collective-permute-start | bytes 18440 | tf_op jit(solution)/shard_map/ppermute | solution.py:114
  56.1 8.2 %collective-permute-start.5 = (f32[3,1,128]{2,1,0:T(1,128)S(1)}, f32[3,1,128]{2,1,0:T(1,128)S(1)}, u32[]{:S(2)}, u32[]{:S(2)}) collective-permute-start(f32[3,1,128]{2,1,0:T(1,128)S(1)} %pad_maximum_fusion.58), channel_id=1, source_target_pairs={{16,0},{32,16},{48,32},{64,48},{80,64},{96,80},{112,96},{128,112},... | collective-permute-start | bytes 4616 | tf_op jit(solution)/shard_map/ppermute | solution.py:116

commit v9 on v8

--- a/solution.py
+++ b/solution.py
@@ -173,11 +173,11 @@
     strips0 = edge_strips((tile[0], tile[1], tile[2]))
     columns0 = column_halos(strips0[2], strips0[3])
     ask_out = jnp.concatenate(
-        [outgoing.reshape(devices_y, capacity), columns0.reshape(devices_y, -1)], axis=1
+        [outgoing.reshape(devices_y, 1, capacity), columns0.reshape(devices_y, 1, -1)], axis=2
     )
     ask_in = lax.all_to_all(ask_out, "gy", split_axis=0, concat_axis=0, tiled=True)
-    got0 = ask_in[:, capacity:].reshape(columns0.shape)
-    asked = ask_in[:, :capacity].reshape(width).astype(jnp.int32) - 1
+    got0 = ask_in[:, 0, capacity:].reshape(columns0.shape)
+    asked = ask_in[:, 0, :capacity].reshape(width).astype(jnp.int32) - 1
 
     valid = asked >= 0
     row0 = (asked // qy) * PATCH
@@ -212,18 +212,18 @@
     held_means = jnp.dot(slot_hit, smooth_means, precision=HI)
     answer_out = jnp.concatenate(
         [
-            picked.reshape(devices_y, capacity * cells),
-            held_means.reshape(devices_y, capacity * cells),
-            columns1.reshape(devices_y, -1),
+            picked.reshape(devices_y, 1, capacity * cells),
+            held_means.reshape(devices_y, 1, capacity * cells),
+            columns1.reshape(devices_y, 1, -1),
         ],
-        axis=1,
+        axis=2,
     )
     answer_in = lax.all_to_all(answer_out, "gy", split_axis=0, concat_axis=0, tiled=True)
-    incoming = answer_in[:, : capacity * cells].reshape(width, cells)
-    asked_means = answer_in[:, capacity * cells : 2 * capacity * cells].reshape(
+    incoming = answer_in[:, 0, : capacity * cells].reshape(width, cells)
+    asked_means = answer_in[:, 0, capacity * cells : 2 * capacity * cells].reshape(
         width, 3, level_stack, PATCH, PATCH
     )
-    got1 = answer_in[:, 2 * capacity * cells :].reshape(columns1.shape)
+    got1 = answer_in[:, 0, 2 * capacity * cells :].reshape(columns1.shape)
     south1, north1 = received_columns(got1)
     fields = substep(fields, strips1, south1, north1, cell_coriolis, turns, flags)
 
@@ -238,6 +238,7 @@
     row_mask = jnp.sum(row_sel, axis=1)
     col_mask = jnp.sum(col_sel, axis=1)
     count = jnp.dot(row_mask.T, col_mask, precision=HI)
+    dense, count = lax.optimization_barrier((dense, count))
     after = jnp.stack(fields, axis=0)
     final_result = after + BETA * (dense - count[None, None] * after)
     return (final_result[None], blended.reshape(1, 1, slots, 3, level_stack, fine_cells))

time: 70.6 us -> 70.9 us (level)
  other arithmetic: 4.42 us -> 5.17 us
    all_to_all x2 -> x0, local copies, waits for them, and re-layouts: 1.37 us -> none  [the longest x1 0.71 us: step(): lax.all_to_all(answer_out, 'gy', split_axis=0, concat_axis=0, tiled=True)]
    concatenate x0 -> x2, local copies, waits for them, and re-layouts: none -> 1.37 us  [the longest x1 0.71 us: step(): jnp.concatenate([picked.reshape(devices_y, 1, capacity * cells), held_mea...]
    unnamed x1 -> x2, other arithmetic: 0.34 us -> 1.06 us
    unnamed x16 -> x14, local copies, waits for them, and re-layouts: 3.13 us -> 3.12 us
where the time goes in v9:
time: 70.9 us; the launch traced here: 70.3 us
  starting transfers between devices  41.8 us (59%)
  local copies, waits for them, and re-layouts  11.2 us (16%)
  waiting for transfers between devices  7.6 us (11%)
  other arithmetic  5.17 us (7%)
  matrix products  3.2 us (5%)
  between operations  1.43 us (2%)
    ppermute x2, starting transfers between devices, substep(): partner = lax.ppermute(edges, 'panel', [(0, 1), (1, 0)])  12.4 us
    all_to_all x1, starting transfers between devices, step(): lax.all_to_all(ask_out, 'gy', split_axis=0, concat_axis=0, tiled=True)  10.4 us
    ppermute x2, waiting for transfers between devices, substep(): from_east = lax.ppermute(first_rows, 'gx', shift_pairs(nx, -1))  7.59 us
    all_to_all x1, starting transfers between devices, step(): lax.all_to_all(answer_out, 'gy', split_axis=0, concat_axis=0, tiled=True)  7.21 us
    ppermute x2, starting transfers between devices, substep(): from_west = lax.ppermute(last_rows, 'gx', shift_pairs(nx, 1))  6.26 us
    ppermute x2, starting transfers between devices, substep(): from_east = lax.ppermute(first_rows, 'gx', shift_pairs(nx, -1))  5.43 us
    unnamed x14, local copies, waits for them, and re-layouts  3.12 us
  transfers between devices with their start and end apart: 8, of which 2 were waited for; matrix products, arithmetic and copies ran while one was open for 4% of the time, Pallas kernels for 0%

profile of v9, /device:TPU:56, one launch (start us, length us, event | category | flops | bytes accessed | tf_op | source)
XLA Modules:
  0.0 70.3 jit_solution(8389129272261958585)
XLA Ops:
  0.6 0.9 %slice_bitcast_fusion.2 = (f32[1,128,128]{2,1,0:T(8,128)S(1)}, f32[1,128,128]{2,1,0:T(8,128)S(1)}, f32[1,128,128]{2,1,0:T(8,128)S(1)}) fusion(f32[1,3,1,128,128]{4,3,2,1,0:T(8,128)} %param.6), kind=kLoop, calls=%fused_computation.164 | loop fusion | bytes 393216 | tf_op jit(solution)/shard_map/squeeze | solution.py:208
  1.6 0.2 slice_reduce_fusion.11
  1.7 0.2 slice_reduce_fusion.10
  1.9 0.2 slice_reduce_fusion.9
  2.2 0.6 copy-done.3
  2.8 0.2 convert_reduce_fusion.2
  3.1 0.6 copy-done.4
  3.7 0.1 fusion.82
  4.1 0.7 copy.397
  4.8 10.4 %all-to-all-start = ((f32[16,1,386]{2,1,0:T(1,128)}), f32[16,1,386]{2,1,0:T(1,128)S(1)}, u32[]{:S(2)}, u32[]{:S(2)}) async-start(f32[16,1,386]{2,1,0:T(1,128)} %copy.397), calls=%async_computation | async-start | bytes 65536 | tf_op jit(solution)/shard_map/all_to_all | solution.py:178
  15.3 4.7 %collective-permute-start = (f32[4,3,1,128]{3,2,1,0:T(1,128)S(1)}, f32[4,3,1,128]{3,2,1,0:T(1,128)S(1)}, u32[]{:S(2)}, u32[]{:S(2)}) collective-permute-start(f32[4,3,1,128]{3,2,1,0:T(1,128)S(1)} %pad_maximum_fusion.52), channel_id=1, source_target_pairs={{0,256},{256,0},{1,257},{257,1},{2,258},{258,2},{3,259},{259,3},{4... | collective-permute-start | bytes 18440 | tf_op jit(solution)/shard_map/ppermute | solution.py:114
  20.1 3.1 %collective-permute-start.1 = (f32[3,1,128]{2,1,0:T(1,128)S(1)}, f32[3,1,128]{2,1,0:T(1,128)S(1)}, u32[]{:S(2)}, u32[]{:S(2)}) collective-permute-start(f32[3,1,128]{2,1,0:T(1,128)S(1)} %pad_maximum_fusion.57), channel_id=1, source_target_pairs={{0,16},{16,32},{32,48},{48,64},{64,80},{80,96},{96,112},{112,128},... | collective-permute-start | bytes 4616 | tf_op jit(solution)/shard_map/ppermute | solution.py:115
  23.1 2.8 %collective-permute-start.2 = (f32[3,1,128]{2,1,0:T(1,128)S(1)}, f32[3,1,128]{2,1,0:T(1,128)S(1)}, u32[]{:S(2)}, u32[]{:S(2)}) collective-permute-start(f32[3,1,128]{2,1,0:T(1,128)S(1)} %pad_maximum_fusion.56), channel_id=1, source_target_pairs={{16,0},{32,16},{48,32},{64,48},{80,64},{96,80},{112,96},{128,112},... | collective-permute-start | bytes 4616 | tf_op jit(solution)/shard_map/ppermute | solution.py:116
  26.0 0.3 reduce.16
  26.8 0.2 fusion.18
  26.9 0.2 convolution_multiply_fusion
  27.2 0.1 fusion.81
  27.9 0.6 copy-done.6
  28.5 0.2 fusion.91
  28.7 2.6 %collective-permute-done.2 = f32[3,1,128]{2,1,0:T(1,128)S(1)} collective-permute-done((f32[3,1,128]{2,1,0:T(1,128)S(1)}, f32[3,1,128]{2,1,0:T(1,128)S(1)}, u32[]{:S(2)}, u32[]{:S(2)}) %collective-permute-start.2) | collective-permute-done | bytes 1568 | tf_op jit(solution)/shard_map/ppermute | solution.py:116
  31.5 0.1 slice_reduce_fusion.15
  32.1 0.1 copy.402
  32.3 0.1 copy.403
  32.5 0.1 copy.404
  32.7 0.1 copy.405
  32.8 0.2 maximum_multiply_fusion
  33.0 0.6 copy-done.1
  33.7 0.1 fusion.67
  33.8 0.2 maximum_multiply_fusion.1
  34.0 0.2 fusion.55
  34.3 0.7 copy-done
  34.9 0.1 fusion.73
  35.1 0.2 slice_reduce_fusion.2
  35.2 0.2 slice_reduce_fusion.1
  35.4 0.2 slice_reduce_fusion
  35.8 0.4 convolution_bitcast_fusion
  36.1 0.1 convert_reduce_fusion.1
  36.3 0.1 convert_reduce_fusion
  36.4 0.5 fusion.10
  36.9 0.2 reshape.1047
  37.3 0.7 %copy.414 = f32[16,1,1152]{2,1,0:T(1,128)} copy(f32[16,1,1152]{2,0,1:T(8,128)S(1)} %pad_maximum_fusion.1) | data formatting | bytes 147456 | tf_op jit(solution)/shard_map/concatenate | solution.py:213
  38.0 7.2 %all-to-all-start.1 = ((f32[16,1,1152]{2,1,0:T(1,128)}), f32[16,1,1152]{2,1,0:T(1,128)S(1)}, u32[]{:S(2)}, u32[]{:S(2)}) async-start(f32[16,1,1152]{2,1,0:T(1,128)} %copy.414), calls=%async_computation.1 | async-start | bytes 147456 | tf_op jit(solution)/shard_map/all_to_all | solution.py:221
  45.2 3.2 %collective-permute-start.4 = (f32[3,1,128]{2,1,0:T(1,128)S(1)}, f32[3,1,128]{2,1,0:T(1,128)S(1)}, u32[]{:S(2)}, u32[]{:S(2)}) collective-permute-start(f32[3,1,128]{2,1,0:T(1,128)S(1)} %pad_maximum_fusion.61), channel_id=1, source_target_pairs={{0,16},{16,32},{32,48},{48,64},{64,80},{80,96},{96,112},{112,128},... | collective-permute-start | bytes 4616 | tf_op jit(solution)/shard_map/ppermute | solution.py:115
  48.4 7.7 %collective-permute-start.3 = (f32[4,3,1,128]{3,2,1,0:T(1,128)S(1)}, f32[4,3,1,128]{3,2,1,0:T(1,128)S(1)}, u32[]{:S(2)}, u32[]{:S(2)}) collective-permute-start(f32[4,3,1,128]{3,2,1,0:T(1,128)S(1)} %pad_maximum_fusion.53), channel_id=1, source_target_pairs={{0,256},{256,0},{1,257},{257,1},{2,258},{258,2},{3,259},{259,3},{4... | collective-permute-start | bytes 18440 | tf_op jit(solution)/shard_map/ppermute | solution.py:114
  56.2 2.6 %collective-permute-start.5 = (f32[3,1,128]{2,1,0:T(1,128)S(1)}, f32[3,1,128]{2,1,0:T(1,128)S(1)}, u32[]{:S(2)}, u32[]{:S(2)}) collective-permute-start(f32[3,1,128]{2,1,0:T(1,128)S(1)} %pad_maximum_fusion.60), channel_id=1, source_target_pairs={{16,0},{32,16},{48,32},{64,48},{80,64},{96,80},{112,96},{128,112},... | collective-permute-start | bytes 4616 | tf_op jit(solution)/shard_map/ppermute | solution.py:116
  58.8 0.3 fusion.158
  59.1 0.2 fusion.88
  59.3 5.0 %collective-permute-done.5 = f32[3,1,128]{2,1,0:T(1,128)S(1)} collective-permute-done((f32[3,1,128]{2,1,0:T(1,128)S(1)}, f32[3,1,128]{2,1,0:T(1,128)S(1)}, u32[]{:S(2)}, u32[]{:S(2)}) %collective-permute-start.5) | collective-permute-done | bytes 1568 | tf_op jit(solution)/shard_map/ppermute | solution.py:116
  64.3 0.2 slice_reduce_fusion.12
  65.0 0.1 copy.419
  65.2 0.1 copy.420
  65.4 0.1 copy.421
  65.7 0.2 maximum_multiply_fusion.2
  66.0 0.1 fusion.42
  66.1 0.2 maximum_multiply_fusion.3
  66.3 0.2 fusion.29
  66.6 0.6 gather_fusion
  67.3 0.3 fusion.1
  67.5 0.8 %reshape.1065 = f32[1,1,16,3,1,576]{5,4,3,2,1,0:T(1,128)} reshape(f32[48,576]{1,0:T(8,128)S(1)} %fusion.1) | data formatting | bytes 221184 | tf_op jit(solution)/shard_map/reshape | solution.py:244
  68.3 0.2 reshape_squeeze.19
  68.5 0.5 fusion.2
  69.1 0.4 convolution_bitcast_fusion.1
  69.5 0.1 fusion.49
  69.6 0.7 %add_bitcast_fusion = f32[1,3,1,128,128]{4,3,2,1,0:T(8,128)} fusion(f32[3,1,128,128]{3,2,1,0:T(8,128)S(1)} %convolution_bitcast_fusion.1, f32[1,1,128,128]{3,2,1,0:T(8,128)S(1)} %fusion.29, f32[1,1,128,128]{3,2,1,0:T(8,128)S(1)} %fusion.42, f32[1,1,128,128]{3,2,1,0:T(8,128)S(1)} %fusion.49, f32[128,128]{1,0:T(8,128)S(1)} %fusion.158), kind=kLoop, calls=%fused_computation.13 | loop fusion | flops 294912 | bytes 655360
  (104 shorter events, 3.6 us)
Async XLA Ops:
  2.2 0.7 copy-start.3
  3.0 0.7 copy-start.4
  4.1 21.9 %copy-start.2 = (f32[1,1,16,3,1,576]{5,4,3,2,1,0:T(1,128)S(1)}, f32[1,1,16,3,1,576]{5,4,3,2,1,0:T(1,128)}, u32[]{:S(2)}) copy-start(f32[1,1,16,3,1,576]{5,4,3,2,1,0:T(1,128)} %param.9) | copy-start | bytes 331780
  4.8 26.5 %all-to-all-start = ((f32[16,1,386]{2,1,0:T(1,128)}), f32[16,1,386]{2,1,0:T(1,128)S(1)}, u32[]{:S(2)}, u32[]{:S(2)}) async-start(f32[16,1,386]{2,1,0:T(1,128)} %copy.397), calls=%async_computation | async-start | bytes 65536 | tf_op jit(solution)/shard_map/all_to_all | solution.py:178
  15.3 12.6 %collective-permute-start = (f32[4,3,1,128]{3,2,1,0:T(1,128)S(1)}, f32[4,3,1,128]{3,2,1,0:T(1,128)S(1)}, u32[]{:S(2)}, u32[]{:S(2)}) collective-permute-start(f32[4,3,1,128]{3,2,1,0:T(1,128)S(1)} %pad_maximum_fusion.52), channel_id=1, source_target_pairs={{0,256},{256,0},{1,257},{257,1},{2,258},{258,2},{3,259},{259,3},{4... | collective-permute-start | bytes 18440 | tf_op jit(solution)/shard_map/ppermute | solution.py:114
  20.0 5.9 %copy-start.5 = (s32[1,4]{1,0:T(1,128)S(1)}, s32[1,4]{1,0:T(1,128)}, u32[]{:S(2)}) copy-start(s32[1,4]{1,0:T(1,128)} %param.8) | copy-start | bytes 52
  20.1 8.6 %collective-permute-start.1 = (f32[3,1,128]{2,1,0:T(1,128)S(1)}, f32[3,1,128]{2,1,0:T(1,128)S(1)}, u32[]{:S(2)}, u32[]{:S(2)}) collective-permute-start(f32[3,1,128]{2,1,0:T(1,128)S(1)} %pad_maximum_fusion.57), channel_id=1, source_target_pairs={{0,16},{16,32},{32,48},{48,64},{64,80},{80,96},{96,112},{112,128},... | collective-permute-start | bytes 4616 | tf_op jit(solution)/shard_map/ppermute | solution.py:115
  23.1 8.2 %collective-permute-start.2 = (f32[3,1,128]{2,1,0:T(1,128)S(1)}, f32[3,1,128]{2,1,0:T(1,128)S(1)}, u32[]{:S(2)}, u32[]{:S(2)}) collective-permute-start(f32[3,1,128]{2,1,0:T(1,128)S(1)} %pad_maximum_fusion.56), channel_id=1, source_target_pairs={{16,0},{32,16},{48,32},{64,48},{80,64},{96,80},{112,96},{128,112},... | collective-permute-start | bytes 4616 | tf_op jit(solution)/shard_map/ppermute | solution.py:116
  27.8 0.7 copy-start.6
  32.8 0.8 %copy-start.1 = (f32[1,128,128]{2,1,0:T(8,128)S(1)}, f32[1,128,128]{2,1,0:T(8,128)}, u32[]{:S(2)}) copy-start(f32[1,128,128]{2,1,0:T(8,128)} %param.7) | copy-start | bytes 196612
  34.0 0.9 %copy-start = (f32[1,3,1,128,128]{4,3,2,1,0:T(8,128)S(1)}, f32[1,3,1,128,128]{4,3,2,1,0:T(8,128)}, u32[]{:S(2)}) copy-start(f32[1,3,1,128,128]{4,3,2,1,0:T(8,128)} %param.6) | copy-start | bytes 589828
  38.0 26.4 %all-to-all-start.1 = ((f32[16,1,1152]{2,1,0:T(1,128)}), f32[16,1,1152]{2,1,0:T(1,128)S(1)}, u32[]{:S(2)}, u32[]{:S(2)}) async-start(f32[16,1,1152]{2,1,0:T(1,128)} %copy.414), calls=%async_computation.1 | async-start | bytes 147456 | tf_op jit(solution)/shard_map/all_to_all | solution.py:221
  45.2 14.1 %collective-permute-start.4 = (f32[3,1,128]{2,1,0:T(1,128)S(1)}, f32[3,1,128]{2,1,0:T(1,128)S(1)}, u32[]{:S(2)}, u32[]{:S(2)}) collective-permute-start(f32[3,1,128]{2,1,0:T(1,128)S(1)} %pad_maximum_fusion.61), channel_id=1, source_target_pairs={{0,16},{16,32},{32,48},{48,64},{64,80},{80,96},{96,112},{112,128},... | collective-permute-start | bytes 4616 | tf_op jit(solution)/shard_map/ppermute | solution.py:115
  48.4 10.7 %collective-permute-start.3 = (f32[4,3,1,128]{3,2,1,0:T(1,128)S(1)}, f32[4,3,1,128]{3,2,1,0:T(1,128)S(1)}, u32[]{:S(2)}, u32[]{:S(2)}) collective-permute-start(f32[4,3,1,128]{3,2,1,0:T(1,128)S(1)} %pad_maximum_fusion.53), channel_id=1, source_target_pairs={{0,256},{256,0},{1,257},{257,1},{2,258},{258,2},{3,259},{259,3},{4... | collective-permute-start | bytes 18440 | tf_op jit(solution)/shard_map/ppermute | solution.py:114
  56.2 8.2 %collective-permute-start.5 = (f32[3,1,128]{2,1,0:T(1,128)S(1)}, f32[3,1,128]{2,1,0:T(1,128)S(1)}, u32[]{:S(2)}, u32[]{:S(2)}) collective-permute-start(f32[3,1,128]{2,1,0:T(1,128)S(1)} %pad_maximum_fusion.60), channel_id=1, source_target_pairs={{16,0},{32,16},{48,32},{64,48},{80,64},{96,80},{112,96},{128,112},... | collective-permute-start | bytes 4616 | tf_op jit(solution)/shard_map/ppermute | solution.py:116

commit v10 on v6

--- a/solution.py
+++ b/solution.py
@@ -23,48 +23,35 @@
     return [(i, i + step) for i in range(count) if 0 <= i + step < count]
 
 
-def centre(field):
-    return field[..., 1:-1, 1:-1]
-
-
-def along_x(field):
-    return 0.5 * (field[..., 2:, 1:-1] - field[..., :-2, 1:-1])
-
-
-def along_y(field):
-    return 0.5 * (field[..., 1:-1, 2:] - field[..., 1:-1, :-2])
-
-
-def laplacian(field):
-    return (
-        field[..., 2:, 1:-1]
-        + field[..., :-2, 1:-1]
-        + field[..., 1:-1, 2:]
-        + field[..., 1:-1, :-2]
-        - 4.0 * centre(field)
-    )
-
-
-def advance(height, east, north, coriolis):
-    absolute = coriolis + along_x(north) - along_y(east)
-    depth = DEPTH + height
-    divergence = along_x(depth * east) + along_y(depth * north)
-    new_height = centre(height) - DT_STEP * divergence
-    new_east = centre(east) + DT_STEP * (
-        absolute * centre(north) - GRAVITY * along_x(height) + DAMPING * laplacian(east)
-    )
-    new_north = centre(north) + DT_STEP * (
-        -absolute * centre(east) - GRAVITY * along_y(height) + DAMPING * laplacian(north)
+def shifted(field, west, east, south, north):
+    x_plus = jnp.concatenate([field[:, 1:, :], east[:, None, :]], axis=1)
+    x_minus = jnp.concatenate([west[:, None, :], field[:, :-1, :]], axis=1)
+    y_plus = jnp.concatenate([field[:, :, 1:], north[:, :, None]], axis=2)
+    y_minus = jnp.concatenate([south[:, :, None], field[:, :, :-1]], axis=2)
+    return x_plus, x_minus, y_plus, y_minus
+
+
+def advance_shifted(fields, halos, coriolis):
+    height, east, north = fields
+    hxp, hxm, hyp, hym = shifted(height, *(h[0] for h in halos))
+    uxp, uxm, uyp, uym = shifted(east, *(h[1] for h in halos))
+    vxp, vxm, vyp, vym = shifted(north, *(h[2] for h in halos))
+    absolute = coriolis + 0.5 * (vxp - vxm) - 0.5 * (uyp - uym)
+    divergence = 0.5 * ((DEPTH + hxp) * uxp - (DEPTH + hxm) * uxm) + 0.5 * (
+        (DEPTH + hyp) * vyp - (DEPTH + hym) * vym
+    )
+    new_height = height - DT_STEP * divergence
+    new_east = east + DT_STEP * (
+        absolute * north
+        - GRAVITY * (0.5 * (hxp - hxm))
+        + DAMPING * (uxp + uxm + uyp + uym - 4.0 * east)
+    )
+    new_north = north + DT_STEP * (
+        -absolute * east
+        - GRAVITY * (0.5 * (hyp - hym))
+        + DAMPING * (vxp + vxm + vyp + vym - 4.0 * north)
     )
     return (new_height, new_east, new_north)
-
-
-def padded_field(field, west, east, south, north):
-    rows = jnp.concatenate([west[:, None, :], field, east[:, None, :]], axis=1)
-    zero = jnp.zeros_like(south[:, :1])
-    low = jnp.concatenate([zero, south, zero], axis=1)[:, :, None]
-    high = jnp.concatenate([zero, north, zero], axis=1)[:, :, None]
-    return jnp.concatenate([low, rows, high], axis=2)
 
 
 def edge_turns(codes):
@@ -119,8 +106,7 @@
         jnp.where(flags[side], turned[side], neighbour)
         for side, neighbour in enumerate((from_west, from_east, from_south, from_north))
     ]
-    padded = [padded_field(fields[c], *(h[c] for h in halos)) for c in range(3)]
-    return advance(padded[0], padded[1], padded[2], coriolis)
+    return advance_shifted(fields, halos, coriolis)
 
 
 def step(state, coriolis, edge_rotation, nest_block_state, parent_tile_index, parent_spot_index):
@@ -176,12 +162,15 @@
     strips0 = edge_strips((tile[0], tile[1], tile[2]))
     columns0 = column_halos(strips0[2], strips0[3])
     ask_out = jnp.concatenate(
-        [outgoing.reshape(devices_y, capacity * (cells + 1)), columns0.reshape(devices_y, -1)],
-        axis=1,
+        [
+            outgoing.reshape(devices_y, 1, capacity * (cells + 1)),
+            columns0.reshape(devices_y, 1, -1),
+        ],
+        axis=2,
     )
     ask_in = lax.all_to_all(ask_out, "gy", split_axis=0, concat_axis=0, tiled=True)
-    asked_payload = ask_in[:, : capacity * (cells + 1)].reshape(width, cells + 1)
-    got0 = ask_in[:, capacity * (cells + 1) :].reshape(columns0.shape)
+    asked_payload = ask_in[:, 0, : capacity * (cells + 1)].reshape(width, cells + 1)
+    got0 = ask_in[:, 0, capacity * (cells + 1) :].reshape(columns0.shape)
     asked = asked_payload[:, 0].astype(jnp.int32) - 1
     asked_means = asked_payload[:, 1:].reshape(width, 3, level_stack, PATCH, PATCH)
 
@@ -216,11 +205,12 @@
     strips1 = edge_strips(fields)
     columns1 = column_halos(strips1[2], strips1[3])
     answer_out = jnp.concatenate(
-        [picked.reshape(devices_y, capacity * cells), columns1.reshape(devices_y, -1)], axis=1
+        [picked.reshape(devices_y, 1, capacity * cells), columns1.reshape(devices_y, 1, -1)],
+        axis=2,
     )
     answer_in = lax.all_to_all(answer_out, "gy", split_axis=0, concat_axis=0, tiled=True)
-    incoming = answer_in[:, : capacity * cells].reshape(width, cells)
-    got1 = answer_in[:, capacity * cells :].reshape(columns1.shape)
+    incoming = answer_in[:, 0, : capacity * cells].reshape(width, cells)
+    got1 = answer_in[:, 0, capacity * cells :].reshape(columns1.shape)
     south1, north1 = received_columns(got1)
     fields = substep(fields, strips1, south1, north1, cell_coriolis, turns, flags)
 
@@ -235,6 +225,7 @@
     row_mask = jnp.sum(row_sel, axis=1)
     col_mask = jnp.sum(col_sel, axis=1)
     count = jnp.dot(row_mask.T, col_mask, precision=HI)
+    dense, count = lax.optimization_barrier((dense, count))
     after = jnp.stack(fields, axis=0)
     final_result = after + BETA * (dense - count[None, None] * after)
     return (final_result[None], blended.reshape(1, 1, slots, 3, level_stack, fine_cells))

time: 70.1 us -> 73.8 us (1.053)
  the two profiles are of different devices: /device:TPU:58 before, /device:TPU:6 now
where the time goes in v10:
time: 73.8 us; the launch traced here: 73.2 us
  starting transfers between devices  41.8 us (57%)
  local copies, waits for them, and re-layouts  15.9 us (22%)
  other arithmetic  7.06 us (10%)
  matrix products  3.83 us (5%)
  waiting for transfers between devices  3.32 us (4%)
  between operations  1.34 us (2%)
    ppermute x2, starting transfers between devices, substep(): partner = lax.ppermute(edges, 'panel', [(0, 1), (1, 0)])  12.4 us
    all_to_all x1, starting transfers between devices, step(): lax.all_to_all(ask_out, 'gy', split_axis=0, concat_axis=0, tiled=True)  10.4 us
    all_to_all x1, starting transfers between devices, step(): lax.all_to_all(answer_out, 'gy', split_axis=0, concat_axis=0, tiled=True)  7.21 us
    ppermute x2, starting transfers between devices, substep(): from_west = lax.ppermute(last_rows, 'gx', shift_pairs(nx, 1))  6.12 us
    ppermute x2, starting transfers between devices, substep(): from_east = lax.ppermute(first_rows, 'gx', shift_pairs(nx, -1))  5.56 us
    unnamed x38, local copies, waits for them, and re-layouts  5.16 us
    ppermute x2, waiting for transfers between devices, substep(): from_west = lax.ppermute(last_rows, 'gx', shift_pairs(nx, 1))  3.3 us
    unnamed x2, other arithmetic  1.95 us
  transfers between devices with their start and end apart: 8, of which 1 were waited for; matrix products, arithmetic and copies ran while one was open for 9% of the time, Pallas kernels for 0%

profile of v10, /device:TPU:6, one launch (start us, length us, event | category | flops | bytes accessed | tf_op | source)
XLA Modules:
  0.0 73.2 jit_solution(7027560799069658766)
XLA Ops:
  0.6 1.2 %reduce.6 = f32[16,3,576]{2,1,0:T(4,128)S(1)} reduce(f32[1,1,16,3,1,576]{5,4,3,2,1,0:T(1,128)} %param.9, f32[]{:T(128)} %constant.138), dimensions={0,1,4}, to_apply=%param.9.reduce_sub_computation | reduce | bytes 221188 | tf_op args[3]
  2.3 0.7 %copy-done = f32[1,3,1,128,128]{4,3,2,1,0:T(8,128)S(1)} copy-done((f32[1,3,1,128,128]{4,3,2,1,0:T(8,128)S(1)}, f32[1,3,1,128,128]{4,3,2,1,0:T(8,128)}, u32[]{:S(2)}) %copy-start) | copy-done | bytes 196632
  3.1 0.2 slice_reduce_fusion.11
  3.3 0.2 slice_reduce_fusion.9
  3.7 0.2 fusion.23
  3.8 0.2 convolution_multiply_fusion
  4.1 0.7 copy-done.14
  4.8 0.2 convert_reduce_fusion.2
  5.0 0.6 copy-done.15
  5.7 0.2 fusion.55
  6.0 0.8 %pad_maximum_fusion.28 = f32[16,1,770]{2,1,0:T(1,128)} fusion(f32[16,1,384]{2,1,0:T(1,128)S(1)} %copy.454, f32[16,1,386]{2,1,0:T(1,128)S(1)} %reshape.3319), kind=kLoop, calls=%fused_computation.120 | loop fusion | flops 12320 | bytes 98560 | tf_op jit(solution)/shard_map/concatenate | solution.py:164
  6.8 10.4 %all-to-all-start = ((f32[16,1,770]{2,1,0:T(1,128)}), f32[16,1,770]{2,1,0:T(1,128)S(1)}, u32[]{:S(2)}, u32[]{:S(2)}) async-start(f32[16,1,770]{2,1,0:T(1,128)} %pad_maximum_fusion.28), calls=%async_computation | async-start | bytes 114688 | tf_op jit(solution)/shard_map/all_to_all | solution.py:171
  17.3 7.7 %collective-permute-start = (f32[4,3,1,128]{3,2,1,0:T(1,128)S(1)}, f32[4,3,1,128]{3,2,1,0:T(1,128)S(1)}, u32[]{:S(2)}, u32[]{:S(2)}) collective-permute-start(f32[4,3,1,128]{3,2,1,0:T(1,128)S(1)} %pad_maximum_fusion.31), channel_id=1, source_target_pairs={{0,256},{256,0},{1,257},{257,1},{2,258},{258,2},{3,259},{259,3},{4... | collective-permute-start | bytes 18440 | tf_op jit(solution)/shard_map/ppermute | solution.py:101
  25.1 3.1 %collective-permute-start.1 = (f32[3,1,128]{2,1,0:T(1,128)S(1)}, f32[3,1,128]{2,1,0:T(1,128)S(1)}, u32[]{:S(2)}, u32[]{:S(2)}) collective-permute-start(f32[3,1,128]{2,1,0:T(1,128)S(1)} %pad_maximum_fusion.35), channel_id=1, source_target_pairs={{16,0},{32,16},{48,32},{64,48},{80,64},{96,80},{112,96},{128,112},... | collective-permute-start | bytes 4616 | tf_op jit(solution)/shard_map/ppermute | solution.py:103
  28.2 2.8 %collective-permute-start.2 = (f32[3,1,128]{2,1,0:T(1,128)S(1)}, f32[3,1,128]{2,1,0:T(1,128)S(1)}, u32[]{:S(2)}, u32[]{:S(2)}) collective-permute-start(f32[3,1,128]{2,1,0:T(1,128)S(1)} %pad_maximum_fusion.36), channel_id=1, source_target_pairs={{0,16},{16,32},{32,48},{48,64},{64,80},{80,96},{96,112},{112,128},... | collective-permute-start | bytes 4616 | tf_op jit(solution)/shard_map/ppermute | solution.py:102
  31.7 0.3 copy-done.10
  32.1 0.2 copy-done.17
  32.3 0.2 fusion.64
  32.5 0.6 slice_bitcast_fusion.33
  33.0 3.3 %collective-permute-done.2 = f32[3,1,128]{2,1,0:T(1,128)S(1)} collective-permute-done((f32[3,1,128]{2,1,0:T(1,128)S(1)}, f32[3,1,128]{2,1,0:T(1,128)S(1)}, u32[]{:S(2)}, u32[]{:S(2)}) %collective-permute-start.2) | collective-permute-done | bytes 1568 | tf_op jit(solution)/shard_map/ppermute | solution.py:102
  36.3 0.6 slice_bitcast_fusion.31
  37.1 0.1 fusion.54
  37.2 0.1 slice_reduce_fusion.15
  37.4 0.1 copy.459
  37.7 0.5 slice_bitcast_fusion.20
  38.6 0.1 multiply_subtract_fusion.2
  38.8 0.7 copy-done.1
  39.5 0.1 multiply_add_fusion.1
  39.6 0.2 multiply_add_fusion
  39.8 0.2 slice_reduce_fusion.5
  40.0 0.2 slice_reduce_fusion.4
  40.2 0.2 slice_reduce_fusion.3
  40.5 0.6 pad_maximum_fusion.39
  41.1 0.6 pad_maximum_fusion.40
  41.9 0.4 convolution_bitcast_fusion
  42.3 0.1 convert_reduce_fusion.1
  42.7 0.1 convert_reduce_fusion
  42.8 0.5 fusion.15
  43.3 0.2 reshape.3304
  43.6 0.7 copy.469
  44.3 7.2 %all-to-all-start.1 = ((f32[16,1,768]{2,1,0:T(1,128)}), f32[16,1,768]{2,1,0:T(1,128)S(1)}, u32[]{:S(2)}, u32[]{:S(2)}) async-start(f32[16,1,768]{2,1,0:T(1,128)} %copy.469), calls=%async_computation.1 | async-start | bytes 98304 | tf_op jit(solution)/shard_map/all_to_all | solution.py:211
  51.5 4.7 %collective-permute-start.3 = (f32[4,3,1,128]{3,2,1,0:T(1,128)S(1)}, f32[4,3,1,128]{3,2,1,0:T(1,128)}, u32[]{:S(2)}, u32[]{:S(2)}) collective-permute-start(f32[4,3,1,128]{3,2,1,0:T(1,128)S(1)} %pad_maximum_fusion.32), channel_id=1, source_target_pairs={{0,256},{256,0},{1,257},{257,1},{2,258},{258,2},{3,259},{259,3},{4... | collective-permute-start | bytes 18440 | tf_op jit(solution)/shard_map/ppermute | solution.py:101
  56.3 2.5 %collective-permute-start.4 = (f32[3,1,128]{2,1,0:T(1,128)}, f32[3,1,128]{2,1,0:T(1,128)}, u32[]{:S(2)}, u32[]{:S(2)}) collective-permute-start(f32[3,1,128]{2,1,0:T(1,128)} %pad_maximum_fusion.39), channel_id=1, source_target_pairs={{16,0},{32,16},{48,32},{64,48},{80,64},{96,80},{112,96},{128,112},... | collective-permute-start | bytes 4616 | tf_op jit(solution)/shard_map/ppermute | solution.py:103
  58.8 3.4 %collective-permute-start.5 = (f32[3,1,128]{2,1,0:T(1,128)}, f32[3,1,128]{2,1,0:T(1,128)S(1)}, u32[]{:S(2)}, u32[]{:S(2)}) collective-permute-start(f32[3,1,128]{2,1,0:T(1,128)} %pad_maximum_fusion.40), channel_id=1, source_target_pairs={{0,16},{16,32},{32,48},{48,64},{64,80},{80,96},{96,112},{112,128},... | collective-permute-start | bytes 4616 | tf_op jit(solution)/shard_map/ppermute | solution.py:102
  62.2 0.2 copy.482
  62.4 0.5 fusion.2
  63.0 0.4 convolution_bitcast_fusion.1
  63.4 0.3 fusion.117
  64.0 0.6 copy-done.5
  64.8 0.5 copy-done.11
  65.4 0.8 %fusion.61 = f32[4,3,128]{2,1,0:T(4,128)S(1)} fusion(f32[4,3,1,128]{3,2,1,0:T(1,128)} %collective-permute-done.3, f32[4,1,3]{2,1,0:T(1,128)S(1)} %copy-done.13, f32[4,1,3]{2,1,0:T(1,128)S(1)} %copy-done.11, f32[4,1,3]{2,1,0:T(1,128)S(1)} %copy-done.18), kind=kOutput, calls=%fused_computation.142 | convolution fusion | flops 55368 | bytes 12432 | tf_op jit(solution)/shard_map/sij,sjlc->silc/dot_general | solution.py:104
  66.2 0.7 broadcast_select_fusion.2
  66.9 0.6 slice_bitcast_fusion.29
  67.5 0.5 slice_bitcast_fusion.27
  68.0 0.1 slice_reduce_fusion.13
  68.9 0.1 subtract_bitcast_fusion
  69.1 0.1 add_bitcast_fusion.1
  69.2 0.2 add_bitcast_fusion
  69.9 0.6 gather_fusion
  70.6 0.3 fusion.1
  70.9 0.8 %reshape.3320 = f32[1,1,16,3,1,576]{5,4,3,2,1,0:T(1,128)} reshape(f32[48,576]{1,0:T(8,128)S(1)} %fusion.1) | data formatting | bytes 221184 | tf_op jit(solution)/shard_map/reshape | solution.py:231
  71.7 0.6 copy-done.2
  72.3 0.2 fusion.33
  72.5 0.7 fusion.7
  (132 shorter events, 5.1 us)
Async XLA Ops:
  2.1 0.9 %copy-start = (f32[1,3,1,128,128]{4,3,2,1,0:T(8,128)S(1)}, f32[1,3,1,128,128]{4,3,2,1,0:T(8,128)}, u32[]{:S(2)}) copy-start(f32[1,3,1,128,128]{4,3,2,1,0:T(8,128)} %param.6) | copy-start | bytes 589828
  4.1 0.7 copy-start.14
  5.0 0.7 copy-start.15
  6.8 30.1 %all-to-all-start = ((f32[16,1,770]{2,1,0:T(1,128)}), f32[16,1,770]{2,1,0:T(1,128)S(1)}, u32[]{:S(2)}, u32[]{:S(2)}) async-start(f32[16,1,770]{2,1,0:T(1,128)} %pad_maximum_fusion.28), calls=%async_computation | async-start | bytes 114688 | tf_op jit(solution)/shard_map/all_to_all | solution.py:171
  17.3 14.4 %collective-permute-start = (f32[4,3,1,128]{3,2,1,0:T(1,128)S(1)}, f32[4,3,1,128]{3,2,1,0:T(1,128)S(1)}, u32[]{:S(2)}, u32[]{:S(2)}) collective-permute-start(f32[4,3,1,128]{3,2,1,0:T(1,128)S(1)} %pad_maximum_fusion.31), channel_id=1, source_target_pairs={{0,256},{256,0},{1,257},{257,1},{2,258},{258,2},{3,259},{259,3},{4... | collective-permute-start | bytes 18440 | tf_op jit(solution)/shard_map/ppermute | solution.py:101
  25.1 5.9 %copy-start.16 = (s32[1,4]{1,0:T(1,128)S(1)}, s32[1,4]{1,0:T(1,128)}, u32[]{:S(2)}) copy-start(s32[1,4]{1,0:T(1,128)} %param.8) | copy-start | bytes 52
  25.1 7.4 %collective-permute-start.1 = (f32[3,1,128]{2,1,0:T(1,128)S(1)}, f32[3,1,128]{2,1,0:T(1,128)S(1)}, u32[]{:S(2)}, u32[]{:S(2)}) collective-permute-start(f32[3,1,128]{2,1,0:T(1,128)S(1)} %pad_maximum_fusion.35), channel_id=1, source_target_pairs={{16,0},{32,16},{48,32},{64,48},{80,64},{96,80},{112,96},{128,112},... | collective-permute-start | bytes 4616 | tf_op jit(solution)/shard_map/ppermute | solution.py:103
  28.2 8.2 %collective-permute-start.2 = (f32[3,1,128]{2,1,0:T(1,128)S(1)}, f32[3,1,128]{2,1,0:T(1,128)S(1)}, u32[]{:S(2)}, u32[]{:S(2)}) collective-permute-start(f32[3,1,128]{2,1,0:T(1,128)S(1)} %pad_maximum_fusion.36), channel_id=1, source_target_pairs={{0,16},{16,32},{32,48},{48,64},{64,80},{80,96},{96,112},{112,128},... | collective-permute-start | bytes 4616 | tf_op jit(solution)/shard_map/ppermute | solution.py:102
  31.4 0.6 copy-start.10
  31.5 0.6 copy-start.12
  31.6 0.7 copy-start.17
  38.6 0.8 %copy-start.1 = (f32[1,128,128]{2,1,0:T(8,128)S(1)}, f32[1,128,128]{2,1,0:T(8,128)}, u32[]{:S(2)}) copy-start(f32[1,128,128]{2,1,0:T(8,128)} %param.7) | copy-start | bytes 196612
  44.3 23.7 %all-to-all-start.1 = ((f32[16,1,768]{2,1,0:T(1,128)}), f32[16,1,768]{2,1,0:T(1,128)S(1)}, u32[]{:S(2)}, u32[]{:S(2)}) async-start(f32[16,1,768]{2,1,0:T(1,128)} %copy.469), calls=%async_computation.1 | async-start | bytes 98304 | tf_op jit(solution)/shard_map/all_to_all | solution.py:211
  51.5 13.2 %collective-permute-start.3 = (f32[4,3,1,128]{3,2,1,0:T(1,128)S(1)}, f32[4,3,1,128]{3,2,1,0:T(1,128)}, u32[]{:S(2)}, u32[]{:S(2)}) collective-permute-start(f32[4,3,1,128]{3,2,1,0:T(1,128)S(1)} %pad_maximum_fusion.32), channel_id=1, source_target_pairs={{0,256},{256,0},{1,257},{257,1},{2,258},{258,2},{3,259},{259,3},{4... | collective-permute-start | bytes 18440 | tf_op jit(solution)/shard_map/ppermute | solution.py:101
  56.3 10.0 %collective-permute-start.4 = (f32[3,1,128]{2,1,0:T(1,128)}, f32[3,1,128]{2,1,0:T(1,128)}, u32[]{:S(2)}, u32[]{:S(2)}) collective-permute-start(f32[3,1,128]{2,1,0:T(1,128)} %pad_maximum_fusion.39), channel_id=1, source_target_pairs={{16,0},{32,16},{48,32},{64,48},{80,64},{96,80},{112,96},{128,112},... | collective-permute-start | bytes 4616 | tf_op jit(solution)/shard_map/ppermute | solution.py:103
  58.8 8.8 %collective-permute-start.5 = (f32[3,1,128]{2,1,0:T(1,128)}, f32[3,1,128]{2,1,0:T(1,128)S(1)}, u32[]{:S(2)}, u32[]{:S(2)}) collective-permute-start(f32[3,1,128]{2,1,0:T(1,128)} %pad_maximum_fusion.40), channel_id=1, source_target_pairs={{0,16},{16,32},{32,48},{48,64},{64,80},{80,96},{96,112},{112,128},... | collective-permute-start | bytes 4616 | tf_op jit(solution)/shard_map/ppermute | solution.py:102
  64.0 0.6 copy-start.5
  64.7 0.7 copy-start.11
  64.7 0.7 copy-start.13
  64.7 0.7 copy-start.18
  70.8 0.8 %copy-start.6 = (f32[1,1,1,128]{3,2,1,0:T(1,128)S(1)}, f32[1,1,1,128]{3,2,1,0:T(1,128)}, u32[]{:S(2)}) copy-start(f32[1,1,1,128]{3,2,1,0:T(1,128)} %get-tuple-element.140) | copy-start | bytes 1540
  70.8 0.8 %copy-start.7 = (f32[1,1,1,128]{3,2,1,0:T(1,128)S(1)}, f32[1,1,1,128]{3,2,1,0:T(1,128)}, u32[]{:S(2)}) copy-start(f32[1,1,1,128]{3,2,1,0:T(1,128)} %get-tuple-element.141) | copy-start | bytes 1540
  70.8 0.8 %copy-start.8 = (f32[1,1,1,128]{3,2,1,0:T(1,128)S(1)}, f32[1,1,1,128]{3,2,1,0:T(1,128)}, u32[]{:S(2)}) copy-start(f32[1,1,1,128]{3,2,1,0:T(1,128)} %get-tuple-element.135) | copy-start | bytes 1540
  70.9 0.8 %copy-start.9 = (f32[1,1,1,128]{3,2,1,0:T(1,128)S(1)}, f32[1,1,1,128]{3,2,1,0:T(1,128)}, u32[]{:S(2)}) copy-start(f32[1,1,1,128]{3,2,1,0:T(1,128)} %get-tuple-element.136) | copy-start | bytes 1540
  71.6 0.7 copy-start.2
  71.6 0.7 copy-start.3
  71.6 0.7 copy-start.4

commit v11 on v6

--- a/solution.py
+++ b/solution.py
@@ -145,18 +145,18 @@
     coarse_of = (fi // RATIO) * PATCH + (fj // RATIO)
     m_idx = jnp.arange(coarse_cells, dtype=jnp.int32)
     spread = (m_idx[:, None] == coarse_of[None, :]).astype(jnp.float32)
-    blocks = nest_block_state[0, 0].reshape(slots * 3 * level_stack, fine_cells)
-    pad_lo = jnp.concatenate([blocks[:, :FINE], blocks[:, :-FINE]], axis=1)
-    pad_hi = jnp.concatenate([blocks[:, FINE:], blocks[:, -FINE:]], axis=1)
-    left = jnp.concatenate([blocks[:, :1], blocks[:, :-1]], axis=1)
-    right = jnp.concatenate([blocks[:, 1:], blocks[:, -1:]], axis=1)
-    left = jnp.where((fj == 0)[None, :], blocks, left)
-    right = jnp.where((fj == FINE - 1)[None, :], blocks, right)
+    blocks = nest_block_state[0, 0]
+    pad_lo = jnp.concatenate([blocks[..., :FINE], blocks[..., :-FINE]], axis=-1)
+    pad_hi = jnp.concatenate([blocks[..., FINE:], blocks[..., -FINE:]], axis=-1)
+    left = jnp.concatenate([blocks[..., :1], blocks[..., :-1]], axis=-1)
+    right = jnp.concatenate([blocks[..., 1:], blocks[..., -1:]], axis=-1)
+    left = jnp.where(fj == 0, blocks, left)
+    right = jnp.where(fj == FINE - 1, blocks, right)
     lap = pad_hi + pad_lo + right + left - 4.0 * blocks
     smoothed = blocks + KAPPA * lap
-    smooth_means = (jnp.dot(smoothed, spread.T, precision=HI) / float(RATIO * RATIO)).reshape(
-        slots, cells
-    )
+    smooth_means = (
+        jnp.einsum("bfln,mn->bflm", smoothed, spread, precision=HI) / float(RATIO * RATIO)
+    ).reshape(slots, cells)
 
     mine = parent_tile_index.reshape(slots)
     spots = parent_spot_index.reshape(slots)
@@ -176,12 +176,15 @@
     strips0 = edge_strips((tile[0], tile[1], tile[2]))
     columns0 = column_halos(strips0[2], strips0[3])
     ask_out = jnp.concatenate(
-        [outgoing.reshape(devices_y, capacity * (cells + 1)), columns0.reshape(devices_y, -1)],
-        axis=1,
+        [
+            outgoing.reshape(devices_y, 1, capacity * (cells + 1)),
+            columns0.reshape(devices_y, 1, -1),
+        ],
+        axis=2,
     )
     ask_in = lax.all_to_all(ask_out, "gy", split_axis=0, concat_axis=0, tiled=True)
-    asked_payload = ask_in[:, : capacity * (cells + 1)].reshape(width, cells + 1)
-    got0 = ask_in[:, capacity * (cells + 1) :].reshape(columns0.shape)
+    asked_payload = ask_in[:, 0, : capacity * (cells + 1)].reshape(width, cells + 1)
+    got0 = ask_in[:, 0, capacity * (cells + 1) :].reshape(columns0.shape)
     asked = asked_payload[:, 0].astype(jnp.int32) - 1
     asked_means = asked_payload[:, 1:].reshape(width, 3, level_stack, PATCH, PATCH)
 
@@ -216,17 +219,18 @@
     strips1 = edge_strips(fields)
     columns1 = column_halos(strips1[2], strips1[3])
     answer_out = jnp.concatenate(
-        [picked.reshape(devices_y, capacity * cells), columns1.reshape(devices_y, -1)], axis=1
+        [picked.reshape(devices_y, 1, capacity * cells), columns1.reshape(devices_y, 1, -1)],
+        axis=2,
     )
     answer_in = lax.all_to_all(answer_out, "gy", split_axis=0, concat_axis=0, tiled=True)
-    incoming = answer_in[:, : capacity * cells].reshape(width, cells)
-    got1 = answer_in[:, capacity * cells :].reshape(columns1.shape)
+    incoming = answer_in[:, 0, : capacity * cells].reshape(width, cells)
+    got1 = answer_in[:, 0, capacity * cells :].reshape(columns1.shape)
     south1, north1 = received_columns(got1)
     fields = substep(fields, strips1, south1, north1, cell_coriolis, turns, flags)
 
     parent = jnp.take(incoming, slot_of, axis=0)
-    coarse = parent.reshape(slots * 3 * level_stack, coarse_cells)
-    upsampled = jnp.dot(coarse, spread, precision=HI)
+    coarse = parent.reshape(slots, 3, level_stack, coarse_cells)
+    upsampled = jnp.einsum("bflm,mn->bfln", coarse, spread, precision=HI)
     blended = smoothed + ALPHA * (upsampled - smoothed)
 
     block_mean = asked_means + ALPHA * (picked - asked_means)
@@ -235,6 +239,7 @@
     row_mask = jnp.sum(row_sel, axis=1)
     col_mask = jnp.sum(col_sel, axis=1)
     count = jnp.dot(row_mask.T, col_mask, precision=HI)
+    dense, count = lax.optimization_barrier((dense, count))
     after = jnp.stack(fields, axis=0)
     final_result = after + BETA * (dense - count[None, None] * after)
     return (final_result[None], blended.reshape(1, 1, slots, 3, level_stack, fine_cells))

time: 70.1 us -> 69.4 us (0.990)
  the two profiles are of different devices: /device:TPU:58 before, /device:TPU:56 now
where the time goes in v11:
time: 69.4 us; the launch traced here: 68.8 us
  starting transfers between devices  41.8 us (60%)
  local copies, waits for them, and re-layouts  10.4 us (15%)
  waiting for transfers between devices  6.62 us (10%)
  other arithmetic  5.54 us (8%)
  matrix products  3.1 us (4%)
  between operations  1.43 us (2%)
    ppermute x2, starting transfers between devices, substep(): partner = lax.ppermute(edges, 'panel', [(0, 1), (1, 0)])  12.4 us
    all_to_all x1, starting transfers between devices, step(): lax.all_to_all(ask_out, 'gy', split_axis=0, concat_axis=0, tiled=True)  10.4 us
    all_to_all x1, starting transfers between devices, step(): lax.all_to_all(answer_out, 'gy', split_axis=0, concat_axis=0, tiled=True)  7.22 us
    ppermute x2, starting transfers between devices, substep(): from_east = lax.ppermute(first_rows, 'gx', shift_pairs(nx, -1))  6.71 us
    ppermute x2, waiting for transfers between devices, substep(): from_east = lax.ppermute(first_rows, 'gx', shift_pairs(nx, -1))  6.61 us
    ppermute x2, starting transfers between devices, substep(): from_west = lax.ppermute(last_rows, 'gx', shift_pairs(nx, 1))  4.98 us
    unnamed x16, local copies, waits for them, and re-layouts  3.78 us
  transfers between devices with their start and end apart: 8, of which 2 were waited for; matrix products, arithmetic and copies ran while one was open for 7% of the time, Pallas kernels for 0%

profile of v11, /device:TPU:56, one launch (start us, length us, event | category | flops | bytes accessed | tf_op | source)
XLA Modules:
  0.0 68.8 jit_solution(12103418737615359243)
XLA Ops:
  0.6 0.9 %slice_bitcast_fusion.6 = (f32[1,128,128]{2,1,0:T(8,128)S(1)}, f32[1,128,128]{2,1,0:T(8,128)S(1)}, f32[1,128,128]{2,1,0:T(8,128)S(1)}) fusion(f32[1,3,1,128,128]{4,3,2,1,0:T(8,128)} %param.6), kind=kLoop, calls=%fused_computation.171 | loop fusion | bytes 393216 | tf_op jit(solution)/shard_map/squeeze | solution.py:217
  1.6 0.2 slice_reduce_fusion.8
  1.8 0.2 slice_reduce_fusion.7
  2.0 0.2 slice_reduce_fusion.6
  2.2 4.7 %collective-permute-start = (f32[4,3,1,128]{3,2,1,0:T(1,128)S(1)}, f32[4,3,1,128]{3,2,1,0:T(1,128)S(1)}, u32[]{:S(2)}, u32[]{:S(2)}) collective-permute-start(f32[4,3,1,128]{3,2,1,0:T(1,128)S(1)} %pad_maximum_fusion.52), channel_id=1, source_target_pairs={{0,256},{256,0},{1,257},{257,1},{2,258},{258,2},{3,259},{259,3},{4... | collective-permute-start | bytes 18440 | tf_op jit(solution)/shard_map/ppermute | solution.py:114
  7.5 0.2 fusion.22
  7.7 0.2 convolution_multiply_fusion
  8.0 0.7 copy-done.3
  8.7 0.2 convert_reduce_fusion.2
  8.9 0.6 copy-done.4
  9.6 0.2 fusion.87
  9.9 0.8 %pad_maximum_fusion.49 = f32[16,1,770]{2,1,0:T(1,128)} fusion(f32[16,1,384]{2,1,0:T(1,128)S(1)} %copy.542, f32[16,1,386]{2,1,0:T(1,128)S(1)} %reshape.1124), kind=kLoop, calls=%fused_computation.174 | loop fusion | flops 12320 | bytes 98560 | tf_op jit(solution)/shard_map/concatenate | solution.py:178
  10.7 10.4 %all-to-all-start = ((f32[16,1,770]{2,1,0:T(1,128)}), f32[16,1,770]{2,1,0:T(1,128)S(1)}, u32[]{:S(2)}, u32[]{:S(2)}) async-start(f32[16,1,770]{2,1,0:T(1,128)} %pad_maximum_fusion.49), calls=%async_computation | async-start | bytes 114688 | tf_op jit(solution)/shard_map/all_to_all | solution.py:185
  21.2 3.1 %collective-permute-start.1 = (f32[3,1,128]{2,1,0:T(1,128)S(1)}, f32[3,1,128]{2,1,0:T(1,128)S(1)}, u32[]{:S(2)}, u32[]{:S(2)}) collective-permute-start(f32[3,1,128]{2,1,0:T(1,128)S(1)} %pad_maximum_fusion.57), channel_id=1, source_target_pairs={{0,16},{16,32},{32,48},{48,64},{64,80},{80,96},{96,112},{112,128},... | collective-permute-start | bytes 4616 | tf_op jit(solution)/shard_map/ppermute | solution.py:115
  24.2 2.8 %collective-permute-start.2 = (f32[3,1,128]{2,1,0:T(1,128)S(1)}, f32[3,1,128]{2,1,0:T(1,128)S(1)}, u32[]{:S(2)}, u32[]{:S(2)}) collective-permute-start(f32[3,1,128]{2,1,0:T(1,128)S(1)} %pad_maximum_fusion.56), channel_id=1, source_target_pairs={{16,0},{32,16},{48,32},{64,48},{80,64},{96,80},{112,96},{128,112},... | collective-permute-start | bytes 4616 | tf_op jit(solution)/shard_map/ppermute | solution.py:116
  27.4 0.7 copy-done.6
  28.0 0.2 fusion.94
  28.2 4.2 %collective-permute-done.2 = f32[3,1,128]{2,1,0:T(1,128)S(1)} collective-permute-done((f32[3,1,128]{2,1,0:T(1,128)S(1)}, f32[3,1,128]{2,1,0:T(1,128)S(1)}, u32[]{:S(2)}, u32[]{:S(2)}) %collective-permute-start.2) | collective-permute-done | bytes 1568 | tf_op jit(solution)/shard_map/ppermute | solution.py:116
  32.4 0.1 slice_reduce_fusion.15
  33.1 0.1 copy.547
  33.3 0.1 copy.548
  33.5 0.1 copy.549
  33.6 0.1 copy.550
  33.8 0.2 maximum_multiply_fusion
  34.0 0.6 copy-done.1
  34.6 0.1 fusion.71
  34.7 0.2 maximum_multiply_fusion.1
  35.0 0.2 fusion.59
  35.4 0.1 fusion.86
  35.5 0.4 copy-done
  35.9 0.1 fusion.77
  36.0 0.2 slice_reduce_fusion.5
  36.2 0.2 slice_reduce_fusion.4
  36.4 0.2 slice_reduce_fusion.3
  36.7 0.4 convolution_bitcast_fusion
  37.1 0.1 convert_reduce_fusion.1
  37.3 0.1 convert_reduce_fusion
  37.4 0.5 fusion.14
  38.0 0.2 reshape.1108
  38.3 0.7 copy.559
  38.9 7.2 %all-to-all-start.1 = ((f32[16,1,768]{2,1,0:T(1,128)}), f32[16,1,768]{2,1,0:T(1,128)S(1)}, u32[]{:S(2)}, u32[]{:S(2)}) async-start(f32[16,1,768]{2,1,0:T(1,128)} %copy.559), calls=%async_computation.1 | async-start | bytes 98304 | tf_op jit(solution)/shard_map/all_to_all | solution.py:225
  46.2 1.9 %collective-permute-start.4 = (f32[3,1,128]{2,1,0:T(1,128)S(1)}, f32[3,1,128]{2,1,0:T(1,128)S(1)}, u32[]{:S(2)}, u32[]{:S(2)}) collective-permute-start(f32[3,1,128]{2,1,0:T(1,128)S(1)} %pad_maximum_fusion.61), channel_id=1, source_target_pairs={{0,16},{16,32},{32,48},{48,64},{64,80},{80,96},{96,112},{112,128},... | collective-permute-start | bytes 4616 | tf_op jit(solution)/shard_map/ppermute | solution.py:115
  48.1 7.7 %collective-permute-start.3 = (f32[4,3,1,128]{3,2,1,0:T(1,128)S(1)}, f32[4,3,1,128]{3,2,1,0:T(1,128)S(1)}, u32[]{:S(2)}, u32[]{:S(2)}) collective-permute-start(f32[4,3,1,128]{3,2,1,0:T(1,128)S(1)} %pad_maximum_fusion.53), channel_id=1, source_target_pairs={{0,256},{256,0},{1,257},{257,1},{2,258},{258,2},{3,259},{259,3},{4... | collective-permute-start | bytes 18440 | tf_op jit(solution)/shard_map/ppermute | solution.py:114
  55.9 3.9 %collective-permute-start.5 = (f32[3,1,128]{2,1,0:T(1,128)S(1)}, f32[3,1,128]{2,1,0:T(1,128)S(1)}, u32[]{:S(2)}, u32[]{:S(2)}) collective-permute-start(f32[3,1,128]{2,1,0:T(1,128)S(1)} %pad_maximum_fusion.60), channel_id=1, source_target_pairs={{16,0},{32,16},{48,32},{64,48},{80,64},{96,80},{112,96},{128,112},... | collective-permute-start | bytes 4616 | tf_op jit(solution)/shard_map/ppermute | solution.py:116
  59.9 0.2 copy.576
  60.1 0.5 fusion.3
  60.6 0.4 convolution_bitcast_fusion.1
  61.1 0.3 fusion.154
  61.4 0.2 fusion.91
  61.6 2.4 %collective-permute-done.5 = f32[3,1,128]{2,1,0:T(1,128)S(1)} collective-permute-done((f32[3,1,128]{2,1,0:T(1,128)S(1)}, f32[3,1,128]{2,1,0:T(1,128)S(1)}, u32[]{:S(2)}, u32[]{:S(2)}) %collective-permute-start.5) | collective-permute-done | bytes 1568 | tf_op jit(solution)/shard_map/ppermute | solution.py:116
  64.0 0.1 slice_reduce_fusion.13
  64.7 0.1 copy.564
  64.9 0.1 copy.565
  65.1 0.1 copy.566
  65.3 0.1 copy.567
  65.4 0.2 maximum_multiply_fusion.2
  65.6 0.1 fusion.46
  65.7 0.2 maximum_multiply_fusion.3
  65.9 0.2 fusion.33
  66.3 0.6 gather_fusion
  67.0 0.2 fusion.2
  67.2 0.8 %copy.580 = f32[1,1,16,3,1,576]{5,4,3,2,1,0:T(1,128)} copy(f32[1,1,16,3,1,576]{5,2,3,4,1,0:T(8,128)S(1)} %fusion.2) | data formatting | bytes 221184
  68.0 0.1 fusion.53
  68.1 0.7 %add_bitcast_fusion = f32[1,3,1,128,128]{4,3,2,1,0:T(8,128)} fusion(f32[3,1,128,128]{3,2,1,0:T(8,128)S(1)} %convolution_bitcast_fusion.1, f32[1,1,128,128]{3,2,1,0:T(8,128)S(1)} %fusion.33, f32[1,1,128,128]{3,2,1,0:T(8,128)S(1)} %fusion.46, f32[1,1,128,128]{3,2,1,0:T(8,128)S(1)} %fusion.53, f32[128,128]{1,0:T(8,128)S(1)} %fusion.154), kind=kLoop, calls=%fused_computation.14 | loop fusion | flops 294912 | bytes 655360
  (105 shorter events, 3.5 us)
Async XLA Ops:
  1.9 5.0 %copy-start.2 = (f32[1,1,16,3,1,576]{5,4,3,2,1,0:T(1,128)S(1)}, f32[1,1,16,3,1,576]{5,4,3,2,1,0:T(1,128)}, u32[]{:S(2)}) copy-start(f32[1,1,16,3,1,576]{5,4,3,2,1,0:T(1,128)} %param.9) | copy-start | bytes 331780
  2.2 25.1 %collective-permute-start = (f32[4,3,1,128]{3,2,1,0:T(1,128)S(1)}, f32[4,3,1,128]{3,2,1,0:T(1,128)S(1)}, u32[]{:S(2)}, u32[]{:S(2)}) collective-permute-start(f32[4,3,1,128]{3,2,1,0:T(1,128)S(1)} %pad_maximum_fusion.52), channel_id=1, source_target_pairs={{0,256},{256,0},{1,257},{257,1},{2,258},{258,2},{3,259},{259,3},{4... | collective-permute-start | bytes 18440 | tf_op jit(solution)/shard_map/ppermute | solution.py:114
  8.0 0.7 copy-start.3
  8.9 0.7 copy-start.4
  10.7 21.7 %all-to-all-start = ((f32[16,1,770]{2,1,0:T(1,128)}), f32[16,1,770]{2,1,0:T(1,128)S(1)}, u32[]{:S(2)}, u32[]{:S(2)}) async-start(f32[16,1,770]{2,1,0:T(1,128)} %pad_maximum_fusion.49), calls=%async_computation | async-start | bytes 114688 | tf_op jit(solution)/shard_map/all_to_all | solution.py:185
  21.1 5.9 %copy-start.5 = (s32[1,4]{1,0:T(1,128)S(1)}, s32[1,4]{1,0:T(1,128)}, u32[]{:S(2)}) copy-start(s32[1,4]{1,0:T(1,128)} %param.8) | copy-start | bytes 52
  21.2 7.1 %collective-permute-start.1 = (f32[3,1,128]{2,1,0:T(1,128)S(1)}, f32[3,1,128]{2,1,0:T(1,128)S(1)}, u32[]{:S(2)}, u32[]{:S(2)}) collective-permute-start(f32[3,1,128]{2,1,0:T(1,128)S(1)} %pad_maximum_fusion.57), channel_id=1, source_target_pairs={{0,16},{16,32},{32,48},{48,64},{64,80},{80,96},{96,112},{112,128},... | collective-permute-start | bytes 4616 | tf_op jit(solution)/shard_map/ppermute | solution.py:115
  24.2 8.2 %collective-permute-start.2 = (f32[3,1,128]{2,1,0:T(1,128)S(1)}, f32[3,1,128]{2,1,0:T(1,128)S(1)}, u32[]{:S(2)}, u32[]{:S(2)}) collective-permute-start(f32[3,1,128]{2,1,0:T(1,128)S(1)} %pad_maximum_fusion.56), channel_id=1, source_target_pairs={{16,0},{32,16},{48,32},{64,48},{80,64},{96,80},{112,96},{128,112},... | collective-permute-start | bytes 4616 | tf_op jit(solution)/shard_map/ppermute | solution.py:116
  27.3 0.7 copy-start.6
  33.8 0.8 %copy-start.1 = (f32[1,128,128]{2,1,0:T(8,128)S(1)}, f32[1,128,128]{2,1,0:T(8,128)}, u32[]{:S(2)}) copy-start(f32[1,128,128]{2,1,0:T(8,128)} %param.7) | copy-start | bytes 196612
  34.9 0.9 %copy-start = (f32[1,3,1,128,128]{4,3,2,1,0:T(8,128)S(1)}, f32[1,3,1,128,128]{4,3,2,1,0:T(8,128)}, u32[]{:S(2)}) copy-start(f32[1,3,1,128,128]{4,3,2,1,0:T(8,128)} %param.6) | copy-start | bytes 589828
  38.9 25.1 %all-to-all-start.1 = ((f32[16,1,768]{2,1,0:T(1,128)}), f32[16,1,768]{2,1,0:T(1,128)S(1)}, u32[]{:S(2)}, u32[]{:S(2)}) async-start(f32[16,1,768]{2,1,0:T(1,128)} %copy.559), calls=%async_computation.1 | async-start | bytes 98304 | tf_op jit(solution)/shard_map/all_to_all | solution.py:225
  46.2 15.4 %collective-permute-start.4 = (f32[3,1,128]{2,1,0:T(1,128)S(1)}, f32[3,1,128]{2,1,0:T(1,128)S(1)}, u32[]{:S(2)}, u32[]{:S(2)}) collective-permute-start(f32[3,1,128]{2,1,0:T(1,128)S(1)} %pad_maximum_fusion.61), channel_id=1, source_target_pairs={{0,16},{16,32},{32,48},{48,64},{64,80},{80,96},{96,112},{112,128},... | collective-permute-start | bytes 4616 | tf_op jit(solution)/shard_map/ppermute | solution.py:115
  48.1 13.2 %collective-permute-start.3 = (f32[4,3,1,128]{3,2,1,0:T(1,128)S(1)}, f32[4,3,1,128]{3,2,1,0:T(1,128)S(1)}, u32[]{:S(2)}, u32[]{:S(2)}) collective-permute-start(f32[4,3,1,128]{3,2,1,0:T(1,128)S(1)} %pad_maximum_fusion.53), channel_id=1, source_target_pairs={{0,256},{256,0},{1,257},{257,1},{2,258},{258,2},{3,259},{259,3},{4... | collective-permute-start | bytes 18440 | tf_op jit(solution)/shard_map/ppermute | solution.py:114
  55.9 8.2 %collective-permute-start.5 = (f32[3,1,128]{2,1,0:T(1,128)S(1)}, f32[3,1,128]{2,1,0:T(1,128)S(1)}, u32[]{:S(2)}, u32[]{:S(2)}) collective-permute-start(f32[3,1,128]{2,1,0:T(1,128)S(1)} %pad_maximum_fusion.60), channel_id=1, source_target_pairs={{16,0},{32,16},{48,32},{64,48},{80,64},{96,80},{112,96},{128,112},... | collective-permute-start | bytes 4616 | tf_op jit(solution)/shard_map/ppermute | solution.py:116

commit v12 on v6

--- a/solution.py
+++ b/solution.py
@@ -176,12 +176,15 @@
     strips0 = edge_strips((tile[0], tile[1], tile[2]))
     columns0 = column_halos(strips0[2], strips0[3])
     ask_out = jnp.concatenate(
-        [outgoing.reshape(devices_y, capacity * (cells + 1)), columns0.reshape(devices_y, -1)],
-        axis=1,
+        [
+            outgoing.reshape(devices_y, 1, capacity * (cells + 1)),
+            columns0.reshape(devices_y, 1, -1),
+        ],
+        axis=2,
     )
     ask_in = lax.all_to_all(ask_out, "gy", split_axis=0, concat_axis=0, tiled=True)
-    asked_payload = ask_in[:, : capacity * (cells + 1)].reshape(width, cells + 1)
-    got0 = ask_in[:, capacity * (cells + 1) :].reshape(columns0.shape)
+    asked_payload = ask_in[:, 0, : capacity * (cells + 1)].reshape(width, cells + 1)
+    got0 = ask_in[:, 0, capacity * (cells + 1) :].reshape(columns0.shape)
     asked = asked_payload[:, 0].astype(jnp.int32) - 1
     asked_means = asked_payload[:, 1:].reshape(width, 3, level_stack, PATCH, PATCH)
 
@@ -216,15 +219,16 @@
     strips1 = edge_strips(fields)
     columns1 = column_halos(strips1[2], strips1[3])
     answer_out = jnp.concatenate(
-        [picked.reshape(devices_y, capacity * cells), columns1.reshape(devices_y, -1)], axis=1
+        [picked.reshape(devices_y, 1, capacity * cells), columns1.reshape(devices_y, 1, -1)],
+        axis=2,
     )
     answer_in = lax.all_to_all(answer_out, "gy", split_axis=0, concat_axis=0, tiled=True)
-    incoming = answer_in[:, : capacity * cells].reshape(width, cells)
-    got1 = answer_in[:, capacity * cells :].reshape(columns1.shape)
+    incoming = answer_in[:, 0, : capacity * cells].reshape(width, cells)
+    got1 = answer_in[:, 0, capacity * cells :].reshape(columns1.shape)
     south1, north1 = received_columns(got1)
     fields = substep(fields, strips1, south1, north1, cell_coriolis, turns, flags)
 
-    parent = jnp.take(incoming, slot_of, axis=0)
+    parent = jnp.dot(slot_hit.T, incoming, precision=HI)
     coarse = parent.reshape(slots * 3 * level_stack, coarse_cells)
     upsampled = jnp.dot(coarse, spread, precision=HI)
     blended = smoothed + ALPHA * (upsampled - smoothed)
@@ -235,6 +239,7 @@
     row_mask = jnp.sum(row_sel, axis=1)
     col_mask = jnp.sum(col_sel, axis=1)
     count = jnp.dot(row_mask.T, col_mask, precision=HI)
+    dense, count = lax.optimization_barrier((dense, count))
     after = jnp.stack(fields, axis=0)
     final_result = after + BETA * (dense - count[None, None] * after)
     return (final_result[None], blended.reshape(1, 1, slots, 3, level_stack, fine_cells))

time: 70.1 us -> 69.6 us (level)
  the two profiles are of different devices: /device:TPU:58 before, /device:TPU:56 now
where the time goes in v12:
time: 69.6 us; the launch traced here: 69.1 us
  starting transfers between devices  41.8 us (60%)
  local copies, waits for them, and re-layouts  9.3 us (13%)
  other arithmetic  6.68 us (10%)
  waiting for transfers between devices  6.64 us (10%)
  matrix products  3.3 us (5%)
  between operations  1.39 us (2%)
    ppermute x2, starting transfers between devices, substep(): partner = lax.ppermute(edges, 'panel', [(0, 1), (1, 0)])  12.4 us
    all_to_all x1, starting transfers between devices, step(): lax.all_to_all(ask_out, 'gy', split_axis=0, concat_axis=0, tiled=True)  10.4 us
    all_to_all x1, starting transfers between devices, step(): lax.all_to_all(answer_out, 'gy', split_axis=0, concat_axis=0, tiled=True)  7.21 us
    ppermute x2, starting transfers between devices, substep(): from_east = lax.ppermute(first_rows, 'gx', shift_pairs(nx, -1))  6.71 us
    ppermute x2, waiting for transfers between devices, substep(): from_east = lax.ppermute(first_rows, 'gx', shift_pairs(nx, -1))  6.62 us
    ppermute x2, starting transfers between devices, substep(): from_west = lax.ppermute(last_rows, 'gx', shift_pairs(nx, 1))  4.98 us
    unnamed x12, local copies, waits for them, and re-layouts  3.35 us
    unnamed x2, other arithmetic  1.95 us
  transfers between devices with their start and end apart: 8, of which 2 were waited for; matrix products, arithmetic and copies ran while one was open for 3% of the time, Pallas kernels for 0%

profile of v12, /device:TPU:56, one launch (start us, length us, event | category | flops | bytes accessed | tf_op | source)
XLA Modules:
  0.0 69.1 jit_solution(3811984479536561964)
XLA Ops:
  0.6 1.2 %reduce.6 = f32[16,3,576]{2,1,0:T(4,128)S(1)} reduce(f32[1,1,16,3,1,576]{5,4,3,2,1,0:T(1,128)} %param.9, f32[]{:T(128)} %constant.125), dimensions={0,1,4}, to_apply=%param.9.reduce_sub_computation | reduce | bytes 221188 | tf_op args[3]
  2.4 0.7 %copy-done = f32[1,3,1,128,128]{4,3,2,1,0:T(8,128)S(1)} copy-done((f32[1,3,1,128,128]{4,3,2,1,0:T(8,128)S(1)}, f32[1,3,1,128,128]{4,3,2,1,0:T(8,128)}, u32[]{:S(2)}) %copy-start) | copy-done | bytes 196632
  3.1 0.2 slice_reduce_fusion.8
  3.3 0.2 slice_reduce_fusion.7
  3.5 0.2 slice_reduce_fusion.6
  3.8 0.2 fusion.18
  4.0 0.2 convolution_multiply_fusion
  4.3 0.7 copy-done.2
  5.0 0.2 convert_reduce_fusion.2
  5.2 0.6 copy-done.3
  5.9 0.2 fusion.82
  6.2 0.8 %pad_maximum_fusion.49 = f32[16,1,770]{2,1,0:T(1,128)} fusion(f32[16,1,384]{2,1,0:T(1,128)S(1)} %copy.502, f32[16,1,386]{2,1,0:T(1,128)S(1)} %reshape.1013), kind=kLoop, calls=%fused_computation.165 | loop fusion | flops 12320 | bytes 98560 | tf_op jit(solution)/shard_map/concatenate | solution.py:178
  7.0 10.4 %all-to-all-start = ((f32[16,1,770]{2,1,0:T(1,128)}), f32[16,1,770]{2,1,0:T(1,128)S(1)}, u32[]{:S(2)}, u32[]{:S(2)}) async-start(f32[16,1,770]{2,1,0:T(1,128)} %pad_maximum_fusion.49), calls=%async_computation | async-start | bytes 114688 | tf_op jit(solution)/shard_map/all_to_all | solution.py:185
  17.5 4.7 %collective-permute-start = (f32[4,3,1,128]{3,2,1,0:T(1,128)S(1)}, f32[4,3,1,128]{3,2,1,0:T(1,128)S(1)}, u32[]{:S(2)}, u32[]{:S(2)}) collective-permute-start(f32[4,3,1,128]{3,2,1,0:T(1,128)S(1)} %pad_maximum_fusion.52), channel_id=1, source_target_pairs={{0,256},{256,0},{1,257},{257,1},{2,258},{258,2},{3,259},{259,3},{4... | collective-permute-start | bytes 18440 | tf_op jit(solution)/shard_map/ppermute | solution.py:114
  22.2 3.1 %collective-permute-start.1 = (f32[3,1,128]{2,1,0:T(1,128)S(1)}, f32[3,1,128]{2,1,0:T(1,128)S(1)}, u32[]{:S(2)}, u32[]{:S(2)}) collective-permute-start(f32[3,1,128]{2,1,0:T(1,128)S(1)} %pad_maximum_fusion.57), channel_id=1, source_target_pairs={{0,16},{16,32},{32,48},{48,64},{64,80},{80,96},{96,112},{112,128},... | collective-permute-start | bytes 4616 | tf_op jit(solution)/shard_map/ppermute | solution.py:115
  25.3 2.8 %collective-permute-start.2 = (f32[3,1,128]{2,1,0:T(1,128)S(1)}, f32[3,1,128]{2,1,0:T(1,128)S(1)}, u32[]{:S(2)}, u32[]{:S(2)}) collective-permute-start(f32[3,1,128]{2,1,0:T(1,128)S(1)} %pad_maximum_fusion.56), channel_id=1, source_target_pairs={{16,0},{32,16},{48,32},{64,48},{80,64},{96,80},{112,96},{128,112},... | collective-permute-start | bytes 4616 | tf_op jit(solution)/shard_map/ppermute | solution.py:116
  28.4 0.7 copy-done.5
  29.1 0.2 fusion.90
  29.3 4.2 %collective-permute-done.2 = f32[3,1,128]{2,1,0:T(1,128)S(1)} collective-permute-done((f32[3,1,128]{2,1,0:T(1,128)S(1)}, f32[3,1,128]{2,1,0:T(1,128)S(1)}, u32[]{:S(2)}, u32[]{:S(2)}) %collective-permute-start.2) | collective-permute-done | bytes 1568 | tf_op jit(solution)/shard_map/ppermute | solution.py:116
  33.5 0.1 slice_reduce_fusion.15
  34.1 0.1 copy.507
  34.3 0.1 copy.508
  34.5 0.1 copy.509
  34.7 0.1 copy.510
  34.9 0.2 maximum_multiply_fusion
  35.1 0.6 copy-done.1
  35.7 0.1 fusion.67
  35.8 0.2 maximum_multiply_fusion.1
  36.0 0.2 fusion.55
  36.4 0.1 fusion.81
  36.6 0.1 fusion.73
  36.7 0.2 slice_reduce_fusion.5
  36.9 0.2 slice_reduce_fusion.4
  37.1 0.2 slice_reduce_fusion.3
  37.4 0.4 convolution_bitcast_fusion
  37.8 0.1 convert_reduce_fusion.1
  38.0 0.1 convert_reduce_fusion
  38.1 0.5 fusion.10
  38.7 0.2 reshape.1005
  39.0 0.7 copy.519
  39.7 7.2 %all-to-all-start.1 = ((f32[16,1,768]{2,1,0:T(1,128)}), f32[16,1,768]{2,1,0:T(1,128)S(1)}, u32[]{:S(2)}, u32[]{:S(2)}) async-start(f32[16,1,768]{2,1,0:T(1,128)} %copy.519), calls=%async_computation.1 | async-start | bytes 98304 | tf_op jit(solution)/shard_map/all_to_all | solution.py:225
  46.9 1.9 %collective-permute-start.4 = (f32[3,1,128]{2,1,0:T(1,128)S(1)}, f32[3,1,128]{2,1,0:T(1,128)S(1)}, u32[]{:S(2)}, u32[]{:S(2)}) collective-permute-start(f32[3,1,128]{2,1,0:T(1,128)S(1)} %pad_maximum_fusion.61), channel_id=1, source_target_pairs={{0,16},{16,32},{32,48},{48,64},{64,80},{80,96},{96,112},{112,128},... | collective-permute-start | bytes 4616 | tf_op jit(solution)/shard_map/ppermute | solution.py:115
  48.8 7.7 %collective-permute-start.3 = (f32[4,3,1,128]{3,2,1,0:T(1,128)S(1)}, f32[4,3,1,128]{3,2,1,0:T(1,128)S(1)}, u32[]{:S(2)}, u32[]{:S(2)}) collective-permute-start(f32[4,3,1,128]{3,2,1,0:T(1,128)S(1)} %pad_maximum_fusion.53), channel_id=1, source_target_pairs={{0,256},{256,0},{1,257},{257,1},{2,258},{258,2},{3,259},{259,3},{4... | collective-permute-start | bytes 18440 | tf_op jit(solution)/shard_map/ppermute | solution.py:114
  56.6 3.9 %collective-permute-start.5 = (f32[3,1,128]{2,1,0:T(1,128)S(1)}, f32[3,1,128]{2,1,0:T(1,128)S(1)}, u32[]{:S(2)}, u32[]{:S(2)}) collective-permute-start(f32[3,1,128]{2,1,0:T(1,128)S(1)} %pad_maximum_fusion.60), channel_id=1, source_target_pairs={{16,0},{32,16},{48,32},{64,48},{80,64},{96,80},{112,96},{128,112},... | collective-permute-start | bytes 4616 | tf_op jit(solution)/shard_map/ppermute | solution.py:116
  60.6 0.2 copy.536
  60.8 0.5 fusion.2
  61.3 0.4 convolution_bitcast_fusion.1
  61.8 0.3 fusion.154
  62.1 0.2 fusion.87
  62.3 2.5 %collective-permute-done.5 = f32[3,1,128]{2,1,0:T(1,128)S(1)} collective-permute-done((f32[3,1,128]{2,1,0:T(1,128)S(1)}, f32[3,1,128]{2,1,0:T(1,128)S(1)}, u32[]{:S(2)}, u32[]{:S(2)}) %collective-permute-start.5) | collective-permute-done | bytes 1568 | tf_op jit(solution)/shard_map/ppermute | solution.py:116
  64.8 0.1 slice_reduce_fusion.13
  65.4 0.1 copy.524
  65.6 0.1 copy.525
  65.8 0.1 copy.526
  66.0 0.1 copy.527
  66.1 0.2 maximum_multiply_fusion.2
  66.3 0.1 fusion.42
  66.4 0.2 maximum_multiply_fusion.3
  66.6 0.2 fusion.29
  67.0 0.2 fusion.86
  67.2 0.2 fusion.1
  67.5 0.8 %reshape.1014 = f32[1,1,16,3,1,576]{5,4,3,2,1,0:T(1,128)} reshape(f32[48,576]{1,0:T(8,128)S(1)} %fusion.1) | data formatting | bytes 221184 | tf_op jit(solution)/shard_map/reshape | solution.py:245
  68.2 0.1 fusion.49
  68.4 0.7 %add_bitcast_fusion = f32[1,3,1,128,128]{4,3,2,1,0:T(8,128)} fusion(f32[3,1,128,128]{3,2,1,0:T(8,128)S(1)} %convolution_bitcast_fusion.1, f32[1,1,128,128]{3,2,1,0:T(8,128)S(1)} %fusion.29, f32[1,1,128,128]{3,2,1,0:T(8,128)S(1)} %fusion.42, f32[1,1,128,128]{3,2,1,0:T(8,128)S(1)} %fusion.49, f32[128,128]{1,0:T(8,128)S(1)} %fusion.154), kind=kLoop, calls=%fused_computation.12 | loop fusion | flops 294912 | bytes 655360
  (100 shorter events, 3.4 us)
Async XLA Ops:
  2.1 0.9 %copy-start = (f32[1,3,1,128,128]{4,3,2,1,0:T(8,128)S(1)}, f32[1,3,1,128,128]{4,3,2,1,0:T(8,128)}, u32[]{:S(2)}) copy-start(f32[1,3,1,128,128]{4,3,2,1,0:T(8,128)} %param.6) | copy-start | bytes 589828
  4.3 0.7 copy-start.2
  5.1 0.7 copy-start.3
  7.0 26.5 %all-to-all-start = ((f32[16,1,770]{2,1,0:T(1,128)}), f32[16,1,770]{2,1,0:T(1,128)S(1)}, u32[]{:S(2)}, u32[]{:S(2)}) async-start(f32[16,1,770]{2,1,0:T(1,128)} %pad_maximum_fusion.49), calls=%async_computation | async-start | bytes 114688 | tf_op jit(solution)/shard_map/all_to_all | solution.py:185
  17.5 10.9 %collective-permute-start = (f32[4,3,1,128]{3,2,1,0:T(1,128)S(1)}, f32[4,3,1,128]{3,2,1,0:T(1,128)S(1)}, u32[]{:S(2)}, u32[]{:S(2)}) collective-permute-start(f32[4,3,1,128]{3,2,1,0:T(1,128)S(1)} %pad_maximum_fusion.52), channel_id=1, source_target_pairs={{0,256},{256,0},{1,257},{257,1},{2,258},{258,2},{3,259},{259,3},{4... | collective-permute-start | bytes 18440 | tf_op jit(solution)/shard_map/ppermute | solution.py:114
  22.2 5.9 %copy-start.4 = (s32[1,4]{1,0:T(1,128)S(1)}, s32[1,4]{1,0:T(1,128)}, u32[]{:S(2)}) copy-start(s32[1,4]{1,0:T(1,128)} %param.8) | copy-start | bytes 52
  22.2 7.0 %collective-permute-start.1 = (f32[3,1,128]{2,1,0:T(1,128)S(1)}, f32[3,1,128]{2,1,0:T(1,128)S(1)}, u32[]{:S(2)}, u32[]{:S(2)}) collective-permute-start(f32[3,1,128]{2,1,0:T(1,128)S(1)} %pad_maximum_fusion.57), channel_id=1, source_target_pairs={{0,16},{16,32},{32,48},{48,64},{64,80},{80,96},{96,112},{112,128},... | collective-permute-start | bytes 4616 | tf_op jit(solution)/shard_map/ppermute | solution.py:115
  25.3 8.2 %collective-permute-start.2 = (f32[3,1,128]{2,1,0:T(1,128)S(1)}, f32[3,1,128]{2,1,0:T(1,128)S(1)}, u32[]{:S(2)}, u32[]{:S(2)}) collective-permute-start(f32[3,1,128]{2,1,0:T(1,128)S(1)} %pad_maximum_fusion.56), channel_id=1, source_target_pairs={{16,0},{32,16},{48,32},{64,48},{80,64},{96,80},{112,96},{128,112},... | collective-permute-start | bytes 4616 | tf_op jit(solution)/shard_map/ppermute | solution.py:116
  28.4 0.7 copy-start.5
  34.8 0.8 %copy-start.1 = (f32[1,128,128]{2,1,0:T(8,128)S(1)}, f32[1,128,128]{2,1,0:T(8,128)}, u32[]{:S(2)}) copy-start(f32[1,128,128]{2,1,0:T(8,128)} %param.7) | copy-start | bytes 196612
  39.7 25.1 %all-to-all-start.1 = ((f32[16,1,768]{2,1,0:T(1,128)}), f32[16,1,768]{2,1,0:T(1,128)S(1)}, u32[]{:S(2)}, u32[]{:S(2)}) async-start(f32[16,1,768]{2,1,0:T(1,128)} %copy.519), calls=%async_computation.1 | async-start | bytes 98304 | tf_op jit(solution)/shard_map/all_to_all | solution.py:225
  46.9 15.4 %collective-permute-start.4 = (f32[3,1,128]{2,1,0:T(1,128)S(1)}, f32[3,1,128]{2,1,0:T(1,128)S(1)}, u32[]{:S(2)}, u32[]{:S(2)}) collective-permute-start(f32[3,1,128]{2,1,0:T(1,128)S(1)} %pad_maximum_fusion.61), channel_id=1, source_target_pairs={{0,16},{16,32},{32,48},{48,64},{64,80},{80,96},{96,112},{112,128},... | collective-permute-start | bytes 4616 | tf_op jit(solution)/shard_map/ppermute | solution.py:115
  48.8 13.2 %collective-permute-start.3 = (f32[4,3,1,128]{3,2,1,0:T(1,128)S(1)}, f32[4,3,1,128]{3,2,1,0:T(1,128)S(1)}, u32[]{:S(2)}, u32[]{:S(2)}) collective-permute-start(f32[4,3,1,128]{3,2,1,0:T(1,128)S(1)} %pad_maximum_fusion.53), channel_id=1, source_target_pairs={{0,256},{256,0},{1,257},{257,1},{2,258},{258,2},{3,259},{259,3},{4... | collective-permute-start | bytes 18440 | tf_op jit(solution)/shard_map/ppermute | solution.py:114
  56.6 8.2 %collective-permute-start.5 = (f32[3,1,128]{2,1,0:T(1,128)S(1)}, f32[3,1,128]{2,1,0:T(1,128)S(1)}, u32[]{:S(2)}, u32[]{:S(2)}) collective-permute-start(f32[3,1,128]{2,1,0:T(1,128)S(1)} %pad_maximum_fusion.60), channel_id=1, source_target_pairs={{16,0},{32,16},{48,32},{64,48},{80,64},{96,80},{112,96},{128,112},... | collective-permute-start | bytes 4616 | tf_op jit(solution)/shard_map/ppermute | solution.py:116

commit v13 on v12

--- a/solution.py
+++ b/solution.py
@@ -182,9 +182,13 @@
         ],
         axis=2,
     )
+    lanes = -ask_out.shape[2] % 128
+    ask_out = jnp.pad(ask_out, ((0, 0), (0, 0), (0, lanes)))
     ask_in = lax.all_to_all(ask_out, "gy", split_axis=0, concat_axis=0, tiled=True)
     asked_payload = ask_in[:, 0, : capacity * (cells + 1)].reshape(width, cells + 1)
-    got0 = ask_in[:, 0, capacity * (cells + 1) :].reshape(columns0.shape)
+    got0 = ask_in[:, 0, capacity * (cells + 1) : capacity * (cells + 1) + columns0[0].size].reshape(
+        columns0.shape
+    )
     asked = asked_payload[:, 0].astype(jnp.int32) - 1
     asked_means = asked_payload[:, 1:].reshape(width, 3, level_stack, PATCH, PATCH)
 

time: 69.6 us -> 69.6 us (level)
  no operation moved by 1% of the time
where the time goes in v13:
time: 69.6 us; the launch traced here: 69.1 us
  starting transfers between devices  41.8 us (60%)
  local copies, waits for them, and re-layouts  9.3 us (13%)
  other arithmetic  6.68 us (10%)
  waiting for transfers between devices  6.64 us (10%)
  matrix products  3.3 us (5%)
  between operations  1.39 us (2%)
    ppermute x2, starting transfers between devices, substep(): partner = lax.ppermute(edges, 'panel', [(0, 1), (1, 0)])  12.5 us
    all_to_all x1, starting transfers between devices, step(): lax.all_to_all(ask_out, 'gy', split_axis=0, concat_axis=0, tiled=True)  10.4 us
    all_to_all x1, starting transfers between devices, step(): lax.all_to_all(answer_out, 'gy', split_axis=0, concat_axis=0, tiled=True)  7.21 us
    ppermute x2, starting transfers between devices, substep(): from_east = lax.ppermute(first_rows, 'gx', shift_pairs(nx, -1))  6.71 us
    ppermute x2, waiting for transfers between devices, substep(): from_east = lax.ppermute(first_rows, 'gx', shift_pairs(nx, -1))  6.62 us
    ppermute x2, starting transfers between devices, substep(): from_west = lax.ppermute(last_rows, 'gx', shift_pairs(nx, 1))  4.98 us
    unnamed x12, local copies, waits for them, and re-layouts  3.35 us
    unnamed x2, other arithmetic  1.95 us
  transfers between devices with their start and end apart: 8, of which 2 were waited for; matrix products, arithmetic and copies ran while one was open for 3% of the time, Pallas kernels for 0%

profile of v13, /device:TPU:56, one launch (start us, length us, event | category | flops | bytes accessed | tf_op | source)
XLA Modules:
  0.0 69.1 jit_solution(16371718341170287264)
XLA Ops:
  0.6 1.2 %reduce.6 = f32[16,3,576]{2,1,0:T(4,128)S(1)} reduce(f32[1,1,16,3,1,576]{5,4,3,2,1,0:T(1,128)} %param.9, f32[]{:T(128)} %constant.128), dimensions={0,1,4}, to_apply=%param.9.reduce_sub_computation | reduce | bytes 221188 | tf_op args[3]
  2.4 0.7 %copy-done = f32[1,3,1,128,128]{4,3,2,1,0:T(8,128)S(1)} copy-done((f32[1,3,1,128,128]{4,3,2,1,0:T(8,128)S(1)}, f32[1,3,1,128,128]{4,3,2,1,0:T(8,128)}, u32[]{:S(2)}) %copy-start) | copy-done | bytes 196632
  3.1 0.2 slice_reduce_fusion.8
  3.3 0.2 slice_reduce_fusion.7
  3.5 0.2 slice_reduce_fusion.6
  3.8 0.2 fusion.18
  4.0 0.2 convolution_multiply_fusion
  4.3 0.7 copy-done.2
  5.0 0.2 convert_reduce_fusion.2
  5.2 0.6 copy-done.3
  5.9 0.2 fusion.83
  6.2 0.8 %fusion.80 = f32[16,1,896]{2,1,0:T(1,128)} fusion(f32[16,1,384]{2,1,0:T(1,128)S(1)} %copy.502, f32[16,1,386]{2,1,0:T(1,128)S(1)} %reshape.1013), kind=kLoop, calls=%fused_computation.167 | loop fusion | flops 57344 | bytes 106624 | tf_op jit(solution)/shard_map/concatenate | solution.py:178
  7.0 10.4 %all-to-all-start = ((f32[16,1,896]{2,1,0:T(1,128)}), f32[16,1,896]{2,1,0:T(1,128)S(1)}, u32[]{:S(2)}, u32[]{:S(2)}) async-start(f32[16,1,896]{2,1,0:T(1,128)} %fusion.80), calls=%async_computation | async-start | bytes 114688 | tf_op jit(solution)/shard_map/all_to_all | solution.py:187
  17.5 4.7 %collective-permute-start = (f32[4,3,1,128]{3,2,1,0:T(1,128)S(1)}, f32[4,3,1,128]{3,2,1,0:T(1,128)S(1)}, u32[]{:S(2)}, u32[]{:S(2)}) collective-permute-start(f32[4,3,1,128]{3,2,1,0:T(1,128)S(1)} %pad_maximum_fusion.51), channel_id=1, source_target_pairs={{0,256},{256,0},{1,257},{257,1},{2,258},{258,2},{3,259},{259,3},{4... | collective-permute-start | bytes 18440 | tf_op jit(solution)/shard_map/ppermute | solution.py:114
  22.2 3.1 %collective-permute-start.1 = (f32[3,1,128]{2,1,0:T(1,128)S(1)}, f32[3,1,128]{2,1,0:T(1,128)S(1)}, u32[]{:S(2)}, u32[]{:S(2)}) collective-permute-start(f32[3,1,128]{2,1,0:T(1,128)S(1)} %pad_maximum_fusion.56), channel_id=1, source_target_pairs={{0,16},{16,32},{32,48},{48,64},{64,80},{80,96},{96,112},{112,128},... | collective-permute-start | bytes 4616 | tf_op jit(solution)/shard_map/ppermute | solution.py:115
  25.3 2.8 %collective-permute-start.2 = (f32[3,1,128]{2,1,0:T(1,128)S(1)}, f32[3,1,128]{2,1,0:T(1,128)S(1)}, u32[]{:S(2)}, u32[]{:S(2)}) collective-permute-start(f32[3,1,128]{2,1,0:T(1,128)S(1)} %pad_maximum_fusion.55), channel_id=1, source_target_pairs={{16,0},{32,16},{48,32},{64,48},{80,64},{96,80},{112,96},{128,112},... | collective-permute-start | bytes 4616 | tf_op jit(solution)/shard_map/ppermute | solution.py:116
  28.4 0.7 copy-done.5
  29.1 0.2 fusion.91
  29.3 4.2 %collective-permute-done.2 = f32[3,1,128]{2,1,0:T(1,128)S(1)} collective-permute-done((f32[3,1,128]{2,1,0:T(1,128)S(1)}, f32[3,1,128]{2,1,0:T(1,128)S(1)}, u32[]{:S(2)}, u32[]{:S(2)}) %collective-permute-start.2) | collective-permute-done | bytes 1568 | tf_op jit(solution)/shard_map/ppermute | solution.py:116
  33.5 0.1 slice_reduce_fusion.15
  34.1 0.1 copy.507
  34.3 0.1 copy.508
  34.5 0.1 copy.509
  34.7 0.1 copy.510
  34.9 0.2 maximum_multiply_fusion
  35.1 0.6 copy-done.1
  35.7 0.1 fusion.67
  35.8 0.2 maximum_multiply_fusion.1
  36.0 0.2 fusion.55
  36.4 0.1 fusion.82
  36.6 0.1 fusion.73
  36.7 0.2 slice_reduce_fusion.5
  36.9 0.2 slice_reduce_fusion.4
  37.1 0.2 slice_reduce_fusion.3
  37.4 0.4 convolution_bitcast_fusion
  37.8 0.1 convert_reduce_fusion.1
  38.0 0.1 convert_reduce_fusion
  38.1 0.5 fusion.10
  38.7 0.2 reshape.1005
  39.0 0.7 copy.519
  39.7 7.2 %all-to-all-start.1 = ((f32[16,1,768]{2,1,0:T(1,128)}), f32[16,1,768]{2,1,0:T(1,128)S(1)}, u32[]{:S(2)}, u32[]{:S(2)}) async-start(f32[16,1,768]{2,1,0:T(1,128)} %copy.519), calls=%async_computation.1 | async-start | bytes 98304 | tf_op jit(solution)/shard_map/all_to_all | solution.py:229
  46.9 1.9 %collective-permute-start.4 = (f32[3,1,128]{2,1,0:T(1,128)S(1)}, f32[3,1,128]{2,1,0:T(1,128)S(1)}, u32[]{:S(2)}, u32[]{:S(2)}) collective-permute-start(f32[3,1,128]{2,1,0:T(1,128)S(1)} %pad_maximum_fusion.60), channel_id=1, source_target_pairs={{0,16},{16,32},{32,48},{48,64},{64,80},{80,96},{96,112},{112,128},... | collective-permute-start | bytes 4616 | tf_op jit(solution)/shard_map/ppermute | solution.py:115
  48.8 7.7 %collective-permute-start.3 = (f32[4,3,1,128]{3,2,1,0:T(1,128)S(1)}, f32[4,3,1,128]{3,2,1,0:T(1,128)S(1)}, u32[]{:S(2)}, u32[]{:S(2)}) collective-permute-start(f32[4,3,1,128]{3,2,1,0:T(1,128)S(1)} %pad_maximum_fusion.52), channel_id=1, source_target_pairs={{0,256},{256,0},{1,257},{257,1},{2,258},{258,2},{3,259},{259,3},{4... | collective-permute-start | bytes 18440 | tf_op jit(solution)/shard_map/ppermute | solution.py:114
  56.6 3.9 %collective-permute-start.5 = (f32[3,1,128]{2,1,0:T(1,128)S(1)}, f32[3,1,128]{2,1,0:T(1,128)S(1)}, u32[]{:S(2)}, u32[]{:S(2)}) collective-permute-start(f32[3,1,128]{2,1,0:T(1,128)S(1)} %pad_maximum_fusion.59), channel_id=1, source_target_pairs={{16,0},{32,16},{48,32},{64,48},{80,64},{96,80},{112,96},{128,112},... | collective-permute-start | bytes 4616 | tf_op jit(solution)/shard_map/ppermute | solution.py:116
  60.6 0.2 copy.536
  60.8 0.5 fusion.2
  61.3 0.4 convolution_bitcast_fusion.1
  61.8 0.3 fusion.155
  62.1 0.2 fusion.88
  62.3 2.5 %collective-permute-done.5 = f32[3,1,128]{2,1,0:T(1,128)S(1)} collective-permute-done((f32[3,1,128]{2,1,0:T(1,128)S(1)}, f32[3,1,128]{2,1,0:T(1,128)S(1)}, u32[]{:S(2)}, u32[]{:S(2)}) %collective-permute-start.5) | collective-permute-done | bytes 1568 | tf_op jit(solution)/shard_map/ppermute | solution.py:116
  64.8 0.1 slice_reduce_fusion.13
  65.4 0.1 copy.524
  65.6 0.1 copy.525
  65.8 0.1 copy.526
  66.0 0.1 copy.527
  66.1 0.2 maximum_multiply_fusion.2
  66.3 0.1 fusion.42
  66.4 0.2 maximum_multiply_fusion.3
  66.6 0.2 fusion.29
  67.0 0.2 fusion.87
  67.2 0.2 fusion.1
  67.5 0.8 %reshape.1014 = f32[1,1,16,3,1,576]{5,4,3,2,1,0:T(1,128)} reshape(f32[48,576]{1,0:T(8,128)S(1)} %fusion.1) | data formatting | bytes 221184 | tf_op jit(solution)/shard_map/reshape | solution.py:249
  68.2 0.1 fusion.49
  68.4 0.7 %add_bitcast_fusion = f32[1,3,1,128,128]{4,3,2,1,0:T(8,128)} fusion(f32[3,1,128,128]{3,2,1,0:T(8,128)S(1)} %convolution_bitcast_fusion.1, f32[1,1,128,128]{3,2,1,0:T(8,128)S(1)} %fusion.29, f32[1,1,128,128]{3,2,1,0:T(8,128)S(1)} %fusion.42, f32[1,1,128,128]{3,2,1,0:T(8,128)S(1)} %fusion.49, f32[128,128]{1,0:T(8,128)S(1)} %fusion.155), kind=kLoop, calls=%fused_computation.12 | loop fusion | flops 294912 | bytes 655360
  (100 shorter events, 3.4 us)
Async XLA Ops:
  2.1 0.9 %copy-start = (f32[1,3,1,128,128]{4,3,2,1,0:T(8,128)S(1)}, f32[1,3,1,128,128]{4,3,2,1,0:T(8,128)}, u32[]{:S(2)}) copy-start(f32[1,3,1,128,128]{4,3,2,1,0:T(8,128)} %param.6) | copy-start | bytes 589828
  4.3 0.7 copy-start.2
  5.1 0.7 copy-start.3
  7.0 26.5 %all-to-all-start = ((f32[16,1,896]{2,1,0:T(1,128)}), f32[16,1,896]{2,1,0:T(1,128)S(1)}, u32[]{:S(2)}, u32[]{:S(2)}) async-start(f32[16,1,896]{2,1,0:T(1,128)} %fusion.80), calls=%async_computation | async-start | bytes 114688 | tf_op jit(solution)/shard_map/all_to_all | solution.py:187
  17.5 10.9 %collective-permute-start = (f32[4,3,1,128]{3,2,1,0:T(1,128)S(1)}, f32[4,3,1,128]{3,2,1,0:T(1,128)S(1)}, u32[]{:S(2)}, u32[]{:S(2)}) collective-permute-start(f32[4,3,1,128]{3,2,1,0:T(1,128)S(1)} %pad_maximum_fusion.51), channel_id=1, source_target_pairs={{0,256},{256,0},{1,257},{257,1},{2,258},{258,2},{3,259},{259,3},{4... | collective-permute-start | bytes 18440 | tf_op jit(solution)/shard_map/ppermute | solution.py:114
  22.2 5.9 %copy-start.4 = (s32[1,4]{1,0:T(1,128)S(1)}, s32[1,4]{1,0:T(1,128)}, u32[]{:S(2)}) copy-start(s32[1,4]{1,0:T(1,128)} %param.8) | copy-start | bytes 52
  22.2 7.0 %collective-permute-start.1 = (f32[3,1,128]{2,1,0:T(1,128)S(1)}, f32[3,1,128]{2,1,0:T(1,128)S(1)}, u32[]{:S(2)}, u32[]{:S(2)}) collective-permute-start(f32[3,1,128]{2,1,0:T(1,128)S(1)} %pad_maximum_fusion.56), channel_id=1, source_target_pairs={{0,16},{16,32},{32,48},{48,64},{64,80},{80,96},{96,112},{112,128},... | collective-permute-start | bytes 4616 | tf_op jit(solution)/shard_map/ppermute | solution.py:115
  25.3 8.2 %collective-permute-start.2 = (f32[3,1,128]{2,1,0:T(1,128)S(1)}, f32[3,1,128]{2,1,0:T(1,128)S(1)}, u32[]{:S(2)}, u32[]{:S(2)}) collective-permute-start(f32[3,1,128]{2,1,0:T(1,128)S(1)} %pad_maximum_fusion.55), channel_id=1, source_target_pairs={{16,0},{32,16},{48,32},{64,48},{80,64},{96,80},{112,96},{128,112},... | collective-permute-start | bytes 4616 | tf_op jit(solution)/shard_map/ppermute | solution.py:116
  28.4 0.7 copy-start.5
  34.8 0.8 %copy-start.1 = (f32[1,128,128]{2,1,0:T(8,128)S(1)}, f32[1,128,128]{2,1,0:T(8,128)}, u32[]{:S(2)}) copy-start(f32[1,128,128]{2,1,0:T(8,128)} %param.7) | copy-start | bytes 196612
  39.7 25.1 %all-to-all-start.1 = ((f32[16,1,768]{2,1,0:T(1,128)}), f32[16,1,768]{2,1,0:T(1,128)S(1)}, u32[]{:S(2)}, u32[]{:S(2)}) async-start(f32[16,1,768]{2,1,0:T(1,128)} %copy.519), calls=%async_computation.1 | async-start | bytes 98304 | tf_op jit(solution)/shard_map/all_to_all | solution.py:229
  46.9 15.4 %collective-permute-start.4 = (f32[3,1,128]{2,1,0:T(1,128)S(1)}, f32[3,1,128]{2,1,0:T(1,128)S(1)}, u32[]{:S(2)}, u32[]{:S(2)}) collective-permute-start(f32[3,1,128]{2,1,0:T(1,128)S(1)} %pad_maximum_fusion.60), channel_id=1, source_target_pairs={{0,16},{16,32},{32,48},{48,64},{64,80},{80,96},{96,112},{112,128},... | collective-permute-start | bytes 4616 | tf_op jit(solution)/shard_map/ppermute | solution.py:115
  48.8 13.2 %collective-permute-start.3 = (f32[4,3,1,128]{3,2,1,0:T(1,128)S(1)}, f32[4,3,1,128]{3,2,1,0:T(1,128)S(1)}, u32[]{:S(2)}, u32[]{:S(2)}) collective-permute-start(f32[4,3,1,128]{3,2,1,0:T(1,128)S(1)} %pad_maximum_fusion.52), channel_id=1, source_target_pairs={{0,256},{256,0},{1,257},{257,1},{2,258},{258,2},{3,259},{259,3},{4... | collective-permute-start | bytes 18440 | tf_op jit(solution)/shard_map/ppermute | solution.py:114
  56.6 8.2 %collective-permute-start.5 = (f32[3,1,128]{2,1,0:T(1,128)S(1)}, f32[3,1,128]{2,1,0:T(1,128)S(1)}, u32[]{:S(2)}, u32[]{:S(2)}) collective-permute-start(f32[3,1,128]{2,1,0:T(1,128)S(1)} %pad_maximum_fusion.59), channel_id=1, source_target_pairs={{16,0},{32,16},{48,32},{64,48},{80,64},{96,80},{112,96},{128,112},... | collective-permute-start | bytes 4616 | tf_op jit(solution)/shard_map/ppermute | solution.py:116
